TPU v7x, 128 devices: a whole 4x4x4 slice. The times are simulated.
128 devices in a mesh: seq: 8 (over z, core), exp: 16 (over y, x).
Axes of the slice: x: 4, y: 4, z: 4, core: 2. Of those that a mesh axis runs over, the one named last changes fastest.
Arguments:
- tokens: bfloat16 [16, 1024, 2048], P('exp', 'seq'), may hold values from -6 to 6
- in_gain: float32 [2048], replicated, may hold values from 0.1 to 1.9
- post_gain: float32 [2048], replicated, may hold values from 0.1 to 1.9
- w_query: bfloat16 [2048, 2048], P(None, 'seq'), may hold values from -0.125 to 0.125
- w_key: bfloat16 [2048, 2048], P(None, 'seq'), may hold values from -0.125 to 0.125
- w_value: bfloat16 [2048, 4096], P(None, 'seq'), may hold values from -0.125 to 0.125
- w_gate_out: bfloat16 [2048, 4096], P(None, 'seq'), may hold values from -0.125 to 0.125
- w_rates: bfloat16 [2048, 64], replicated, may hold values from -0.125 to 0.125
- conv_query: float32 [4, 2048], P(None, 'seq'), may hold values from -0.5 to 0.5
- conv_key: float32 [4, 2048], P(None, 'seq'), may hold values from -0.5 to 0.5
- conv_value: float32 [4, 4096], P(None, 'seq'), may hold values from -0.5 to 0.5
- decay_rate: float32 [32], P('seq'), may hold values from 1e-05 to 0.1
- time_bias: float32 [32], P('seq'), may hold values from -4 to 4
- head_gain: float32 [128], replicated, may hold values from 0.1 to 1.9
- w_out: bfloat16 [4096, 2048], P('seq'), may hold values from -0.25 to 0.25
- expert_ids: int32 [16, 1024, 10], P('exp', 'seq'), may hold values from 0 to 255, all different within a row; in each aligned block of 128 rows (0 to 127, 128 to 255, ..., all dimensions but the last counted through in order) at most 6 rows name the same one
- route_gates: float32 [16, 1024, 10], P('exp', 'seq'), may hold values from 0.05 to 0.6
- w_expert_gate: bfloat16 [256, 2048, 512], P(('seq', 'exp')), may hold values from -0.125 to 0.125
- w_expert_up: bfloat16 [256, 2048, 512], P(('seq', 'exp')), may hold values from -0.125 to 0.125
- w_expert_down: bfloat16 [256, 512, 2048], P(('seq', 'exp')), may hold values from -0.25 to 0.25
Outputs:
- mixed: bfloat16 [16, 1024, 2048], P('exp', 'seq')
Inputs may be any that keep to these rules, and one draw needn't show every extreme that they name: `expert_ids`: each token names 10 different experts. Within the tokens of one device (aligned blocks of 128 rows in sequence order) no expert is named by more than 6 rows, a bound that some block reaches.
All inputs are finite; a program needn't handle non-finite values.
Results may differ from a plain program's by a relative error of at most 0.02.
Values may be sent and summed in bfloat16 or wider, within the bound.
No kernel may reach another device: no remote copies, remote signals or barrier semaphores. Data moves between devices by JAX's collectives and lax.ppermute only.
A program may use at most 128 MiB of HBM per device.

v0:
```python
import jax
import jax.numpy as jnp
from jax import lax
from jax.sharding import PartitionSpec as P

DK = 128
DV = 128
CH = 64


EPSILON = 1e-06
HIGHEST = lax.Precision.HIGHEST


def carried_in(value, axis, join, neutral):
    count, mine = (lax.axis_size(axis), lax.axis_index(axis))
    pieces = jax.tree.map(lambda part: lax.all_gather(part, axis), value)
    running = jax.tree.map(
        lambda part, zero: jnp.full_like(part, 0) + jnp.asarray(zero, part.dtype), value, neutral
    )

    def turn(position, running):
        longer = join(running, jax.tree.map(lambda part: part[position], pieces))
        return jax.tree.map(lambda new, old: jnp.where(position < mine, new, old), longer, running)

    return lax.fori_loop(0, count - 1, turn, running)


def scale_rows(values, row_gain):
    factor = lax.rsqrt(jnp.mean(values * values, axis=-1, keepdims=True) + EPSILON)
    return values * factor * row_gain


def causal_conv(projected, before, weights):
    taps = weights.shape[0]
    length = projected.shape[0]
    padded = jnp.concatenate([before, projected], axis=0)
    summed = weights[0] * projected
    for lag_index in range(1, taps):
        begin = taps - 1 - lag_index
        summed = summed + weights[lag_index] * padded[begin : begin + length]
    return jax.nn.silu(summed)


def unit_heads(values, head_count):
    shaped = values.reshape(values.shape[0], head_count, values.shape[1] // head_count)
    return shaped * lax.rsqrt(jnp.sum(shaped * shaped, axis=-1, keepdims=True) + EPSILON)


def span_parts(queries, key_vecs, value_vecs, beta_rates, decays):
    span_len = queries.shape[1]
    key_width = key_vecs.shape[2]
    cumulative = jnp.cumsum(decays, axis=1)
    lower_mask = jnp.tril(jnp.ones((span_len, span_len), dtype=bool))
    strict = jnp.tril(jnp.ones((span_len, span_len), dtype=bool), -1)
    spread = cumulative[:, :, None] - cumulative[:, None, :]
    fading = jnp.where(lower_mask, jnp.exp(jnp.where(lower_mask, spread, 0.0)), 0.0)
    key_dots = jnp.einsum("nik,njk->nij", key_vecs, key_vecs, precision=HIGHEST)
    system = jnp.where(strict, beta_rates[:, :, None] * key_dots * fading, 0.0) + jnp.eye(
        span_len, dtype=jnp.float32
    )
    targets = jnp.concatenate(
        [
            (beta_rates * jnp.exp(cumulative))[:, :, None] * key_vecs,
            beta_rates[:, :, None] * value_vecs,
        ],
        axis=2,
    )
    solved = lax.linalg.triangular_solve(
        system, targets, left_side=True, lower=True, unit_diagonal=True
    )
    key_mix = solved[:, :, :key_width]
    value_mix = solved[:, :, key_width:]
    query_fade = jnp.exp(cumulative)[:, :, None] * queries
    scores = jnp.einsum("nik,njk->nij", queries, key_vecs, precision=HIGHEST) * fading
    ending = cumulative[:, -1]
    key_fade = jnp.exp(ending[:, None] - cumulative)[:, :, None] * key_vecs
    return (query_fade, scores, key_mix, value_mix, key_fade, jnp.exp(ending))


def output_step(carried, pieces):
    query_fade, scores, key_mix, value_mix, key_fade, end_fade = pieces
    new_values = value_mix - jnp.dot(key_mix, carried, precision=HIGHEST)
    output = jnp.dot(query_fade, carried, precision=HIGHEST) + jnp.dot(
        scores, new_values, precision=HIGHEST
    )
    carried = end_fade * carried + jnp.dot(key_fade.T, new_values, precision=HIGHEST)
    return (carried, output)


def map_step(carried, pieces):
    query_fade, scores, key_mix, value_mix, key_fade, end_fade = pieces
    widened = jnp.concatenate(
        [jnp.zeros((value_mix.shape[0], key_mix.shape[1]), jnp.float32), value_mix], axis=1
    )
    new_values = widened - jnp.dot(key_mix, carried, precision=HIGHEST)
    carried = end_fade * carried + jnp.dot(key_fade.T, new_values, precision=HIGHEST)
    return (carried, None)


def head_map(pieces):
    key_width = pieces[2].shape[-1]
    value_width = pieces[3].shape[-1]
    start_map = jnp.concatenate(
        [jnp.eye(key_width, dtype=jnp.float32), jnp.zeros((key_width, value_width), jnp.float32)],
        axis=1,
    )
    return lax.scan(map_step, start_map, pieces)[0]


def head_outputs(pieces, initial):
    return lax.scan(output_step, initial, pieces)[1]


def head_spans(values):
    moved = jnp.moveaxis(values, 1, 0)
    return moved.reshape((moved.shape[0], moved.shape[1] // CH, CH) + moved.shape[2:])


def keep_later(earlier, later):
    early_flag, early_tail = earlier
    late_flag, late_tail = later
    return (
        jnp.maximum(early_flag, late_flag),
        late_flag * late_tail + (1.0 - late_flag) * early_tail,
    )


def compose_maps(earlier, later):
    early_map, early_shift = earlier
    late_map, late_shift = later
    joined_map = jnp.einsum("hij,hjk->hik", late_map, early_map, precision=HIGHEST)
    joined_shift = jnp.einsum("hij,hjk->hik", late_map, early_shift, precision=HIGHEST) + late_shift
    return (joined_map, joined_shift)


def hand_on(payload, combine, identity):
    return carried_in(payload, "exp", combine, identity)


def run_experts(arrived, local_experts, capacity, gate_weight, up_weight, down_weight):
    peers = arrived.shape[0]
    model_width = arrived.shape[2]
    grouped = arrived.reshape(peers, local_experts, capacity, model_width)
    gate_part = jnp.einsum(
        "pecd,edf->pecf", grouped, gate_weight, preferred_element_type=jnp.float32
    )
    up_part = jnp.einsum("pecd,edf->pecf", grouped, up_weight, preferred_element_type=jnp.float32)
    hidden = (jax.nn.silu(gate_part) * up_part).astype(jnp.bfloat16)
    expert_out = jnp.einsum(
        "pecf,efd->pecd", hidden, down_weight, preferred_element_type=jnp.float32
    ).astype(jnp.bfloat16)
    return expert_out.reshape(peers, local_experts * capacity, model_width)


def local(
    tokens,
    in_gain,
    post_gain,
    w_query,
    w_key,
    w_value,
    w_gate_out,
    w_rates,
    conv_query,
    conv_key,
    conv_value,
    decay_rate,
    time_bias,
    head_gain,
    w_out,
    expert_ids,
    route_gates,
    w_expert_gate,
    w_expert_up,
    w_expert_down,
):
    seq_count = lax.axis_size("seq")
    exp_count = lax.axis_size("exp")
    token_rows = tokens.reshape(tokens.shape[1], tokens.shape[2])
    local_rows = token_rows.shape[0]
    model_width = token_rows.shape[1]
    normed = scale_rows(token_rows.astype(jnp.float32), in_gain).astype(jnp.bfloat16)
    rate_logits = jnp.dot(normed, w_rates, preferred_element_type=jnp.float32).astype(jnp.bfloat16)
    block_rows, block_rates = (
        lax.all_gather(normed, "seq", axis=0, tiled=True),
        lax.all_gather(rate_logits, "seq", axis=0, tiled=True),
    )
    seg_rows = block_rows.shape[0]
    query_proj = jnp.dot(block_rows, w_query, preferred_element_type=jnp.float32)
    key_proj = jnp.dot(block_rows, w_key, preferred_element_type=jnp.float32)
    value_proj = jnp.dot(block_rows, w_value, preferred_element_type=jnp.float32)
    gate_proj = jnp.dot(block_rows, w_gate_out, preferred_element_type=jnp.float32)
    lag_rows = conv_query.shape[0] - 1
    own_tail = jnp.concatenate(
        [
            query_proj[seg_rows - lag_rows :],
            key_proj[seg_rows - lag_rows :],
            value_proj[seg_rows - lag_rows :],
        ],
        axis=1,
    )
    present = jnp.ones((1, 1), jnp.float32)
    absent = jnp.zeros((1, 1), jnp.float32)
    prior = hand_on((present, own_tail), keep_later, (absent, jnp.zeros_like(own_tail)))[1]
    query_cols = query_proj.shape[1]
    key_cols = key_proj.shape[1]
    query_conv = causal_conv(query_proj, prior[:, :query_cols], conv_query)
    key_conv = causal_conv(key_proj, prior[:, query_cols : query_cols + key_cols], conv_key)
    value_conv = causal_conv(value_proj, prior[:, query_cols + key_cols :], conv_value)
    key_heads = query_cols // DK
    value_heads = decay_rate.shape[0]
    ratio = value_heads // key_heads
    total_heads = value_heads * seq_count
    queries = jnp.repeat(unit_heads(query_conv, key_heads) * DK ** (-0.5), ratio, axis=1)
    key_vecs = jnp.repeat(unit_heads(key_conv, key_heads), ratio, axis=1)
    value_vecs = value_conv.reshape(seg_rows, value_heads, DV)
    first_head = lax.axis_index("seq") * value_heads
    rate_values = block_rates.astype(jnp.float32)
    beta_rates = jax.nn.sigmoid(lax.dynamic_slice_in_dim(rate_values, first_head, value_heads, 1))
    decays = -decay_rate * jax.nn.softplus(
        lax.dynamic_slice_in_dim(rate_values, total_heads + first_head, value_heads, 1) + time_bias
    )
    pieces = jax.vmap(span_parts)(
        head_spans(queries),
        head_spans(key_vecs),
        head_spans(value_vecs),
        head_spans(beta_rates),
        head_spans(decays),
    )
    maps = jax.vmap(head_map)(pieces)
    key_width = key_vecs.shape[2]
    identity_map = jnp.broadcast_to(
        jnp.eye(key_width, dtype=jnp.float32), (value_heads, key_width, key_width)
    )
    identity_shift = jnp.zeros((value_heads, key_width, DV), jnp.float32)
    prefix = hand_on(
        (maps[:, :, :key_width], maps[:, :, key_width:]),
        compose_maps,
        (identity_map, identity_shift),
    )
    incoming = prefix[1]
    recurrent = jax.vmap(head_outputs)(pieces, incoming)
    recurrent = jnp.moveaxis(recurrent.reshape(value_heads, seg_rows, DV), 0, 1)
    gate_heads = gate_proj.reshape(seg_rows, value_heads, DV)
    gated = (
        (scale_rows(recurrent, head_gain) * jax.nn.silu(gate_heads))
        .reshape(seg_rows, value_heads * DV)
        .astype(jnp.bfloat16)
    )
    picked = gated
    attended = lax.psum_scatter(
        jnp.dot(picked, w_out, preferred_element_type=jnp.float32).astype(jnp.bfloat16),
        "seq",
        scatter_dimension=0,
        tiled=True,
    ).astype(jnp.float32)
    residual = (token_rows.astype(jnp.float32) + attended).astype(jnp.bfloat16)
    moe_in = scale_rows(residual.astype(jnp.float32), post_gain).astype(jnp.bfloat16)
    local_experts = w_expert_gate.shape[0]
    devices = seq_count * exp_count
    experts_all = local_experts * devices
    top_count = expert_ids.shape[2]
    capacity = max(2, local_rows * top_count * 6 // (5 * experts_all))
    pair_ids = expert_ids.reshape(-1)
    columns = jnp.arange(experts_all, dtype=jnp.int32)
    onehot = (pair_ids[:, None] == columns[None, :]).astype(jnp.int32)
    earlier = jnp.cumsum(onehot, axis=0) - onehot
    places = jnp.sum(earlier * onehot, axis=1)
    slots = pair_ids * capacity + places
    sources = jnp.arange(pair_ids.shape[0], dtype=jnp.int32) // top_count
    outgoing = (
        jnp.zeros((experts_all * capacity, model_width), jnp.bfloat16)
        .at[slots]
        .set(moe_in[sources])
    )
    slot_count = local_experts * capacity
    arrived = lax.all_to_all(
        outgoing.reshape(devices, slot_count, model_width),
        ("seq", "exp"),
        split_axis=0,
        concat_axis=0,
        tiled=True,
    )
    answers = run_experts(
        arrived, local_experts, capacity, w_expert_gate, w_expert_up, w_expert_down
    )
    returned = lax.all_to_all(answers, ("seq", "exp"), split_axis=0, concat_axis=0, tiled=True)
    picked = returned.reshape(experts_all * capacity, model_width)[slots].reshape(
        local_rows, top_count, model_width
    )
    gates = route_gates.reshape(local_rows, top_count)
    moe_sum = jnp.einsum("tk,tkd->td", gates, picked.astype(jnp.float32), precision=HIGHEST)
    mixed = (residual.astype(jnp.float32) + moe_sum).astype(jnp.bfloat16)
    return mixed.reshape(1, local_rows, model_width)


def solution(mesh):
    in_specs = (
        P("exp", "seq", None),
        P(),
        P(),
        P(None, "seq"),
        P(None, "seq"),
        P(None, "seq"),
        P(None, "seq"),
        P(),
        P(None, "seq"),
        P(None, "seq"),
        P(None, "seq"),
        P("seq"),
        P("seq"),
        P(),
        P("seq", None),
        P("exp", "seq", None),
        P("exp", "seq", None),
        P(("seq", "exp"), None, None),
        P(("seq", "exp"), None, None),
        P(("seq", "exp"), None, None),
    )
    out_specs = P("exp", "seq", None)
    return jax.shard_map(local, mesh=mesh, in_specs=in_specs, out_specs=out_specs, check_vma=False)
```

profile of v0, /device:TPU:5, one launch (start us, length us, event | category | flops | bytes accessed | tf_op | source)
XLA Modules:
  0.0 1207.2 jit_solution(13084941999026847295)
XLA Ops:
  11.6 29.9 %all-reduce.2 = f32[16]{0:T(128)S(1)} all-reduce(f32[16]{0:T(128)S(1)} %dynamic-update-slice), channel_id=1, replica_groups=mesh['seq'=8,'exp'=16] {'exp'}, use_global_device_ids=true, to_apply=%add.2 | all-reduce | flops 16 | bytes 128
  42.9 19.8 %all_gather.27 = bf16[1024,64]{0,1:T(8,128)(2,1)S(1)} all-gather(bf16[128,64]{0,1:T(8,128)(2,1)S(1)} %convolution_convert_fusion.2), channel_id=1, replica_groups=mesh['seq'=8,'exp'=16] {'seq'}, dimensions={0}, use_global_device_ids=true | all-gather | bytes 147456 | tf_op jit(solution)/shard_map/all_gather | solution.py:187
  67.4 3.9 fusion.112
  77.5 21.3 %all-gather.3 = f32[16,3,1024]{2,1,0:T(4,128)} all-gather(f32[1,3,1024]{2,1,0:T(4,128)S(1)} %maximum_bitcast_fusion), channel_id=2, replica_groups=mesh['seq'=8,'exp'=16] {'exp'}, dimensions={0}, use_global_device_ids=true | all-gather | bytes 208896 | tf_op jit(solution)/shard_map/all_gather | solution.py:17
  98.7 40.9 %while.52 = (s32[]{:T(128)}, f32[3,1024]{1,0:T(4,128)S(1)}, s32[]{:T(128)}, f32[16,1,1]{0,2,1:T(1,128)S(1)}, f32[16,3,1024]{2,1,0:T(4,128)}, /*index=5*/s32[]{:T(128)}, s32[]{:T(128)}) while((s32[]{:T(128)}, f32[3,1024]{1,0:T(4,128)S(1)}, s32[]{:T(128)}, f32[16,1,1]{0,2,1:T(1,128)S(1)}, f32[16,3,1024]{2,1,0:T(4,128)}, ...), condition=%wide.region_2.3_spmd.clone, body=%wide.region_1.2_spmd.clone.sunk | while | flops 15365 | bytes 36997 | solution.py:26
  139.6 5.8 divide_multiply_fusion
  161.5 4.9 add_bitcast_fusion
  166.4 316.0 %custom-call.3 = f32[4,16,1,64,64]{3,4,2,1,0:T(8,128)} custom-call(f32[4,16,1,64,64]{4,3,2,1,0:T(8,128)} %add_bitcast_fusion), custom_call_target="InvertDiagBlocksLowerTriangular" | custom-call | tf_op jit(solution)/shard_map/vmap()/triangular_solve | solution.py:69
  482.4 3.1 broadcast_multiply_fusion.1
  485.6 3.8 fusion.34
  494.7 73.8 %while.50 = (s32[]{:T(128)}, f32[4,128,256]{2,1,0:T(8,128)S(1)}, f32[16,4]{1,0:T(8,128)}, f32[16,4,64,128]{3,2,1,0:T(8,128)}, f32[16,4,64,128]{3,2,1,0:T(8,128)}, /*index=5*/f32[16,4,64,128]{3,2,1,0:T(8,128)}, s32[]{:T(128)}) while((s32[]{:T(128)}, f32[4,128,256]{2,1,0:T(8,128)S(1)}, f32[16,4]{1,0:T(8,128)}, f32[16,4,64,128]{3,2,1,0:T(8,128)}, ...), condition=%wide.region_6.7_spmd, body=%wide.region_5.6_spmd.sunk | while | flops 201654272 | bytes 2752661 | solution.py:108
  570.2 6.6 fusion.114
  587.5 4.8 bitcast_multiply_fusion.4
  592.3 33.1 %all-gather.12.cloned.1.call-done = f32[64,128,128]{2,1,0:T(8,128)} async-done(((f32[4,128,128]{2,1,0:T(8,128)}), f32[64,128,128]{2,1,0:T(8,128)}) %all-gather.12.cloned.1.call-update) | async-done | bytes 4194320 | tf_op jit(solution)/shard_map/all_gather | solution.py:17
  625.4 53.3 %all-gather.10.cloned.1.call-done = f32[64,128,128]{2,1,0:T(8,128)} async-done(((f32[4,128,128]{2,1,0:T(8,128)}), f32[64,128,128]{2,1,0:T(8,128)}) %all-gather.10.cloned.1.call-update) | async-done | bytes 4194320 | tf_op jit(solution)/shard_map/all_gather | solution.py:17
  678.6 22.3 %while.53 = (s32[]{:T(128)}, f32[4,128,128]{2,1,0:T(8,128)S(1)}, s32[]{:T(128)}, f32[16,4,128,128]{3,2,1,0:T(8,128)}, f32[16,4,128,128]{3,2,1,0:T(8,128)}, /*index=5*/s32[]{:T(128)}, s32[]{:T(128)}) while((s32[]{:T(128)}, f32[4,128,128]{2,1,0:T(8,128)S(1)}, s32[]{:T(128)}, f32[16,4,128,128]{3,2,1,0:T(8,128)}, ...), condition=%wide.region_8.9_spmd.clone, body=%wide.region_7.8_spmd.clone.sunk | while | flops 100925440 | bytes 1837671 | solution.py:26
  700.9 107.0 %while.51 = (s32[]{:T(128)}, f32[4,128,128]{2,1,0:T(8,128)S(1)}, f32[16,4,64,128]{3,2,0,1:T(8,128)}, f32[16,4]{1,0:T(8,128)}, f32[16,4,64,128]{3,2,1,0:T(8,128)}...) while((s32[]{:T(128)}, f32[4,128,128]{2,1,0:T(8,128)S(1)}, ...), condition=%wide.region_11.12_spmd, body=%wide.region_10.11_spmd.sunk | while | flops 176357376 | bytes 2492585 | solution.py:112
  814.1 5.5 convolution_convert_fusion.1
  823.1 31.7 %reduce-scatter.2.cloned.1.call-done = bf16[128,2048]{1,0:T(8,128)(2,1)} async-done(((bf16[1024,2048]{1,0:T(8,128)(2,1)}), bf16[128,2048]{1,0:T(8,128)(2,1)}) %reduce-scatter.2.cloned.1.call-update) | async-done | bytes 524304 | tf_op jit(solution)/shard_map/reduce_scatter | solution.py:252
  857.4 33.9 %scatter_custom_fusion = bf16[1536,2048]{1,0:T(8,128)(2,1)} fusion(s32[1280]{0:T(1024)S(1)} %fusion.100, bf16[128,2048]{1,0:T(8,128)(2,1)S(1)} %fusion.86, s32[2048]{0:T(1024)S(1)} %pad_clamp_fusion.1, bf16[]{:T(256)} %constant.164.clone.1), kind=kCustom, calls=%fused_computation.46 | custom fusion | bytes 6291458 | tf_op jit(solution)/shard_map/scatter | solution.py:275
  891.3 10.6 reshape.244
  901.9 106.5 %all_to_all.10 = bf16[128,12,2048]{2,1,0:T(8,128)(2,1)S(1)} all-to-all(bf16[128,12,2048]{2,1,0:T(8,128)(2,1)} %reshape.244), channel_id=1, replica_groups=mesh['seq'=8,'exp'=16] {'seq','exp'}, dimensions={0} | all-to-all | bytes 12582912 | tf_op jit(solution)/shard_map/all_to_all | solution.py:278
  1008.4 6.0 copy.108
  1014.5 9.0 fusion.39
  1023.5 12.7 %convolution_convert_fusion = bf16[2,128,6,2048]{3,1,2,0:T(8,128)(2,1)} fusion(bf16[2,512,2048]{2,1,0:T(8,128)(2,1)} %param.47, f32[2,128,6,512]{3,1,2,0:T(8,128)} %fusion.39, bf16[128,2,6,2048]{3,0,2,1:T(8,128)(2,1)} %bitcast.268, bf16[2,2048,512]{2,1,0:T(8,128)(2,1)} %param.45), kind=kOutput, calls=%fused_computation.48 | convolution fusion | flops 6450315264 | bytes 24117248 | tf_op jit(solution)/shard_map/pecf,efd->pecd/dot_general | solution.py:150
  1036.2 9.7 copy.109
  1045.9 5.8 all-to-all-start.1
  1051.8 106.6 %all-to-all-done.1 = bf16[128,12,2048]{2,1,0:T(8,128)(2,1)} async-done(((bf16[128,12,2048]{2,1,0:T(8,128)(2,1)}), bf16[128,12,2048]{2,1,0:T(8,128)(2,1)}, u32[]{:S(2)}, u32[]{:S(2)}) %all-to-all-start.1) | async-done | bytes 6291488 | tf_op jit(solution)/shard_map/all_to_all | solution.py:288
  1158.4 10.7 reshape.247
  1169.2 14.4 %gather_fusion = bf16[1280,2048]{1,0:T(8,128)(2,1)} fusion(bf16[1536,2048]{1,0:T(8,128)(2,1)} %reshape.247, s32[2048]{0:T(1024)S(1)} %pad_clamp_fusion), kind=kCustom, calls=%fused_computation.1 | custom fusion | bytes 10490880 | tf_op jit(solution)/shard_map/gather | solution.py:289
  1183.6 9.6 reshape.248
  1193.2 6.0 fusion.115
  (369 shorter events, 305.9 us)
Async XLA Ops:
  6.5 807.6 %copy-start = (bf16[512,2048]{1,0:T(8,128)(2,1)S(1)}, bf16[512,2048]{1,0:T(8,128)(2,1)}, u32[]{:S(2)}) copy-start(bf16[512,2048]{1,0:T(8,128)(2,1)} %param.42) | copy-start | bytes 6291460
  6.5 3.6 copy-start.34
  6.5 35.0 %copy-start.33 = (f32[4]{0:T(128)S(1)}, f32[4]{0:T(128)}, u32[]{:S(2)}) copy-start(f32[4]{0:T(128)} %param.39) | copy-start | bytes 52
  6.5 35.0 %copy-start.12 = (bf16[2048,64]{0,1:T(8,128)(2,1)S(1)}, bf16[2048,64]{0,1:T(8,128)(2,1)}, u32[]{:S(2)}) copy-start(bf16[2048,64]{0,1:T(8,128)(2,1)} %param.35) | copy-start | bytes 786436
  6.5 56.2 %copy-start.28 = (f32[4]{0:T(128)S(1)}, f32[4]{0:T(128)}, u32[]{:S(2)}) copy-start(f32[4]{0:T(128)} %param.40) | copy-start | bytes 52
  6.5 58.2 %copy-start.18 = (f32[4,256]{1,0:T(4,128)S(1)}, f32[4,256]{1,0:T(4,128)}, u32[]{:S(2)}) copy-start(f32[4,256]{1,0:T(4,128)} %param.36) | copy-start | bytes 12292
  6.6 58.8 %copy-start.19 = (f32[4,256]{1,0:T(4,128)S(1)}, f32[4,256]{1,0:T(4,128)}, u32[]{:S(2)}) copy-start(f32[4,256]{1,0:T(4,128)} %param.37) | copy-start | bytes 12292
  6.6 59.4 %copy-start.15 = (f32[4,512]{1,0:T(4,128)S(1)}, f32[4,512]{1,0:T(4,128)}, u32[]{:S(2)}) copy-start(f32[4,512]{1,0:T(4,128)} %param.38) | copy-start | bytes 24580
  6.6 60.8 %all-gather.8.cloned.1.call-start = ((), (), s32[]{:S(2)}) async-start(), calls=%async_computation.3 | async-start | bytes 4718592 | tf_op jit(solution)/shard_map/all_gather | solution.py:186
  10.1 615.3 %all-gather.12.cloned.1.call-start = ((), (), s32[]{:S(2)}) async-start(), calls=%async_computation.6 | async-start | bytes 4456448 | tf_op jit(solution)/shard_map/all_gather | solution.py:17
  67.4 3.9 copy-start.30
  67.4 4.0 copy-start.32
  71.5 2.3 copy-start.31
  150.1 2.1 copy-start.11
  150.1 2.1 copy-start.20
  150.1 2.0 copy-start.21
  150.1 2.0 copy-start.22
  150.1 2.0 copy-start.23
  150.1 2.0 copy-start.24
  150.2 2.0 copy-start.25
  482.4 3.2 copy-start.5
  482.4 3.2 copy-start.9
  569.4 109.2 %all-gather.10.cloned.1.call-start = ((), (), s32[]{:S(2)}) async-start(), calls=%async_computation.5 | async-start | bytes 4456448 | tf_op jit(solution)/shard_map/all_gather | solution.py:17
  570.2 284.6 %reduce-scatter.2.cloned.1.call-start = ((), (), s32[]{:S(2)}) async-start(), calls=%async_computation.4 | async-start | bytes 4718592 | tf_op jit(solution)/shard_map/reduce_scatter | solution.py:252
  807.9 2.4 copy-start.6
  807.9 2.4 copy-start.29
  821.7 33.0 %copy-start.4 = (bf16[1,128,2048]{2,1,0:T(8,128)(2,1)S(1)}, bf16[1,128,2048]{2,1,0:T(8,128)(2,1)}, u32[]{:S(2)}) copy-start(bf16[1,128,2048]{2,1,0:T(8,128)(2,1)} %param.28) | copy-start | bytes 1572868
  821.8 34.3 %copy-start.14 = (f32[2048]{0:T(1024)S(1)}, f32[2048]{0:T(1024)}, u32[]{:S(2)}) copy-start(f32[2048]{0:T(1024)} %param.30) | copy-start | bytes 24580
  1045.9 5.9 copy-start.17
  1045.9 112.6 %all-to-all-start.1 = ((bf16[128,12,2048]{2,1,0:T(8,128)(2,1)}), bf16[128,12,2048]{2,1,0:T(8,128)(2,1)}, u32[]{:S(2)}, u32[]{:S(2)}) async-start(bf16[128,12,2048]{2,1,0:T(8,128)(2,1)} %copy.109), calls=%async_computation.2 | async-start | bytes 16777216 | tf_op jit(solution)/shard_map/all_to_all | solution.py:288
  1193.2 6.1 copy-start.7
  1193.2 7.3 copy-start.1
  (8 other events, 11.9 us)
Sparse Core Ops, SparseCore 0:
  10.2 35.0 all-gather.7
  569.5 55.7 all-gather.11
  627.5 51.1 all-gather.9
  819.8 34.9 reduce-scatter.1
where the time goes:
time: 1220 us; the launch traced here: 1210 us
  other arithmetic  394 us (32%)
  matrix products  227 us (19%)
  waiting for transfers between devices  225 us (18%)
  blocking collectives  178 us (15%)
  local copies, waits for them, and re-layouts  162 us (13%)
  between operations  14.1 us (1%)
    another operation x2, other arithmetic, span_parts(): lax.linalg.triangular_solve(system, targets, left_side=True, lower=True,...  316 us
    all_to_all x1, waiting for transfers between devices, local(): lax.all_to_all(answers, ('seq', 'exp'), split_axis=0, concat_axis=0, tile...  107 us
    all_to_all x1, blocking collectives, local(): lax.all_to_all(outgoing.reshape(devices, slot_count, model_width), ('seq'...  107 us
    all_gather x2, waiting for transfers between devices, carried_in(): pieces = jax.tree.map(lambda part: lax.all_gather(part, axis), value)  86.4 us
    scatter x1, local copies, waits for them, and re-layouts, local(): outgoing = jnp.zeros((experts_all * capacity, model_width), jnp.bfloat16)...  33.9 us
    reduce_scatter x1, waiting for transfers between devices, local(): lax.psum_scatter(jnp.dot(picked, w_out, preferred_element_type=jnp.float3...  31.7 us
    dot_general x16, matrix products, output_step(): jnp.dot(query_fade, carried, precision=HIGHEST)  31.1 us
    select_n x15, other arithmetic, turn(): jnp.where(position < mine, new, old)  30.7 us
  transfers between devices with their start and end apart: 5, of which 4 were waited for; matrix products, arithmetic and copies ran while one was open for 3% of the time, Pallas kernels for 0%

commit v1 on v0

--- a/solution.py
+++ b/solution.py
@@ -10,20 +10,6 @@
 
 EPSILON = 1e-06
 HIGHEST = lax.Precision.HIGHEST
-
-
-def carried_in(value, axis, join, neutral):
-    count, mine = (lax.axis_size(axis), lax.axis_index(axis))
-    pieces = jax.tree.map(lambda part: lax.all_gather(part, axis), value)
-    running = jax.tree.map(
-        lambda part, zero: jnp.full_like(part, 0) + jnp.asarray(zero, part.dtype), value, neutral
-    )
-
-    def turn(position, running):
-        longer = join(running, jax.tree.map(lambda part: part[position], pieces))
-        return jax.tree.map(lambda new, old: jnp.where(position < mine, new, old), longer, running)
-
-    return lax.fori_loop(0, count - 1, turn, running)
 
 
 def scale_rows(values, row_gain):
@@ -47,95 +33,100 @@
     return shaped * lax.rsqrt(jnp.sum(shaped * shaped, axis=-1, keepdims=True) + EPSILON)
 
 
-def span_parts(queries, key_vecs, value_vecs, beta_rates, decays):
-    span_len = queries.shape[1]
-    key_width = key_vecs.shape[2]
-    cumulative = jnp.cumsum(decays, axis=1)
+def mm(a, b):
+    return jnp.matmul(a, b, precision=HIGHEST)
+
+
+def unit_lower_inverse(strict_part):
+    size = strict_part.shape[-1]
+    power = -strict_part
+    inverse = jnp.eye(size, dtype=jnp.float32) + power
+    reach = 2
+    while reach < size:
+        power = mm(power, power)
+        inverse = inverse + mm(inverse, power)
+        reach *= 2
+    return inverse
+
+
+def chunk_parts(queries, key_vecs, value_vecs, beta_rates, decays):
+    span_len = queries.shape[-2]
+    cumulative = jnp.cumsum(decays, axis=-1)
     lower_mask = jnp.tril(jnp.ones((span_len, span_len), dtype=bool))
     strict = jnp.tril(jnp.ones((span_len, span_len), dtype=bool), -1)
-    spread = cumulative[:, :, None] - cumulative[:, None, :]
+    spread = cumulative[..., :, None] - cumulative[..., None, :]
     fading = jnp.where(lower_mask, jnp.exp(jnp.where(lower_mask, spread, 0.0)), 0.0)
-    key_dots = jnp.einsum("nik,njk->nij", key_vecs, key_vecs, precision=HIGHEST)
-    system = jnp.where(strict, beta_rates[:, :, None] * key_dots * fading, 0.0) + jnp.eye(
-        span_len, dtype=jnp.float32
-    )
-    targets = jnp.concatenate(
-        [
-            (beta_rates * jnp.exp(cumulative))[:, :, None] * key_vecs,
-            beta_rates[:, :, None] * value_vecs,
-        ],
-        axis=2,
-    )
-    solved = lax.linalg.triangular_solve(
-        system, targets, left_side=True, lower=True, unit_diagonal=True
-    )
-    key_mix = solved[:, :, :key_width]
-    value_mix = solved[:, :, key_width:]
-    query_fade = jnp.exp(cumulative)[:, :, None] * queries
-    scores = jnp.einsum("nik,njk->nij", queries, key_vecs, precision=HIGHEST) * fading
-    ending = cumulative[:, -1]
-    key_fade = jnp.exp(ending[:, None] - cumulative)[:, :, None] * key_vecs
-    return (query_fade, scores, key_mix, value_mix, key_fade, jnp.exp(ending))
-
-
-def output_step(carried, pieces):
-    query_fade, scores, key_mix, value_mix, key_fade, end_fade = pieces
-    new_values = value_mix - jnp.dot(key_mix, carried, precision=HIGHEST)
-    output = jnp.dot(query_fade, carried, precision=HIGHEST) + jnp.dot(
-        scores, new_values, precision=HIGHEST
-    )
-    carried = end_fade * carried + jnp.dot(key_fade.T, new_values, precision=HIGHEST)
-    return (carried, output)
-
-
-def map_step(carried, pieces):
-    query_fade, scores, key_mix, value_mix, key_fade, end_fade = pieces
-    widened = jnp.concatenate(
-        [jnp.zeros((value_mix.shape[0], key_mix.shape[1]), jnp.float32), value_mix], axis=1
-    )
-    new_values = widened - jnp.dot(key_mix, carried, precision=HIGHEST)
-    carried = end_fade * carried + jnp.dot(key_fade.T, new_values, precision=HIGHEST)
-    return (carried, None)
-
-
-def head_map(pieces):
-    key_width = pieces[2].shape[-1]
-    value_width = pieces[3].shape[-1]
-    start_map = jnp.concatenate(
-        [jnp.eye(key_width, dtype=jnp.float32), jnp.zeros((key_width, value_width), jnp.float32)],
-        axis=1,
-    )
-    return lax.scan(map_step, start_map, pieces)[0]
-
-
-def head_outputs(pieces, initial):
-    return lax.scan(output_step, initial, pieces)[1]
+    key_dots = jnp.einsum("...ik,...jk->...ij", key_vecs, key_vecs, precision=HIGHEST)
+    system = jnp.where(strict, beta_rates[..., :, None] * key_dots * fading, 0.0)
+    inverse = unit_lower_inverse(system)
+    key_mix = mm(inverse, (beta_rates * jnp.exp(cumulative))[..., None] * key_vecs)
+    value_mix = mm(inverse, beta_rates[..., None] * value_vecs)
+    query_fade = jnp.exp(cumulative)[..., None] * queries
+    scores = jnp.einsum("...ik,...jk->...ij", queries, key_vecs, precision=HIGHEST) * fading
+    ending = cumulative[..., -1]
+    key_fade = jnp.exp(ending[..., None] - cumulative)[..., None] * key_vecs
+    key_width = key_vecs.shape[-1]
+    fade_t = jnp.swapaxes(key_fade, -1, -2)
+    step_map = ending_eye(jnp.exp(ending), key_width) - mm(fade_t, key_mix)
+    step_shift = mm(fade_t, value_mix)
+    return (query_fade, scores, key_mix, value_mix), (step_map, step_shift)
+
+
+def ending_eye(scale, width):
+    return scale[..., None, None] * jnp.eye(width, dtype=jnp.float32)
+
+
+def chunk_prefix(step_map, step_shift):
+    chunks = step_map.shape[1]
+    width = step_map.shape[-1]
+    reach = 1
+    while reach < chunks:
+        eye = jnp.broadcast_to(
+            jnp.eye(width, dtype=jnp.float32), step_map[:, :reach].shape
+        )
+        prev_map = jnp.concatenate([eye, step_map[:, : chunks - reach]], axis=1)
+        prev_shift = jnp.concatenate(
+            [jnp.zeros_like(step_shift[:, :reach]), step_shift[:, : chunks - reach]], axis=1
+        )
+        joined = mm(step_map, jnp.concatenate([prev_map, prev_shift], axis=-1))
+        step_map, step_shift = joined[..., :width], joined[..., width:] + step_shift
+        reach *= 2
+    return step_map, step_shift
+
+
+def segment_entry(seg_map, seg_shift, axis):
+    count, mine = lax.axis_size(axis), lax.axis_index(axis)
+    width = seg_map.shape[-1]
+    excl_map = jnp.broadcast_to(jnp.eye(width, dtype=jnp.float32), seg_map.shape)
+    excl_shift = jnp.zeros_like(seg_shift)
+    reach = 1
+    while reach < count:
+        pairs = [(i, i + reach) for i in range(count - reach)]
+        last = reach * 2 >= count
+        if last:
+            got_shift = lax.ppermute(seg_shift, axis, pairs)
+            excl_shift = mm(excl_map, got_shift) + excl_shift
+        else:
+            got = lax.ppermute(jnp.concatenate([seg_map, seg_shift], axis=-1), axis, pairs)
+            has = mine >= reach
+            both = mm(jnp.stack([seg_map, excl_map]), got[None])
+            seg_shift = both[0, ..., width:] + seg_shift
+            excl_shift = both[1, ..., width:] + excl_shift
+            excl_map = jnp.where(has, both[1, ..., :width], excl_map)
+            seg_map = jnp.where(has, both[0, ..., :width], seg_map)
+        reach *= 2
+    return excl_shift
+
+
+def chunk_outputs(parts, chunk_states):
+    query_fade, scores, key_mix, value_mix = parts
+    new_values = value_mix - mm(key_mix, chunk_states)
+    return mm(query_fade, chunk_states) + mm(scores, new_values)
 
 
 def head_spans(values):
     moved = jnp.moveaxis(values, 1, 0)
     return moved.reshape((moved.shape[0], moved.shape[1] // CH, CH) + moved.shape[2:])
-
-
-def keep_later(earlier, later):
-    early_flag, early_tail = earlier
-    late_flag, late_tail = later
-    return (
-        jnp.maximum(early_flag, late_flag),
-        late_flag * late_tail + (1.0 - late_flag) * early_tail,
-    )
-
-
-def compose_maps(earlier, later):
-    early_map, early_shift = earlier
-    late_map, late_shift = later
-    joined_map = jnp.einsum("hij,hjk->hik", late_map, early_map, precision=HIGHEST)
-    joined_shift = jnp.einsum("hij,hjk->hik", late_map, early_shift, precision=HIGHEST) + late_shift
-    return (joined_map, joined_shift)
-
-
-def hand_on(payload, combine, identity):
-    return carried_in(payload, "exp", combine, identity)
 
 
 def run_experts(arrived, local_experts, capacity, gate_weight, up_weight, down_weight):
@@ -200,9 +191,7 @@
         ],
         axis=1,
     )
-    present = jnp.ones((1, 1), jnp.float32)
-    absent = jnp.zeros((1, 1), jnp.float32)
-    prior = hand_on((present, own_tail), keep_later, (absent, jnp.zeros_like(own_tail)))[1]
+    prior = lax.ppermute(own_tail, "exp", [(i, i + 1) for i in range(exp_count - 1)])
     query_cols = query_proj.shape[1]
     key_cols = key_proj.shape[1]
     query_conv = causal_conv(query_proj, prior[:, :query_cols], conv_query)
@@ -221,26 +210,18 @@
     decays = -decay_rate * jax.nn.softplus(
         lax.dynamic_slice_in_dim(rate_values, total_heads + first_head, value_heads, 1) + time_bias
     )
-    pieces = jax.vmap(span_parts)(
+    parts, (step_map, step_shift) = chunk_parts(
         head_spans(queries),
         head_spans(key_vecs),
         head_spans(value_vecs),
         head_spans(beta_rates),
         head_spans(decays),
     )
-    maps = jax.vmap(head_map)(pieces)
-    key_width = key_vecs.shape[2]
-    identity_map = jnp.broadcast_to(
-        jnp.eye(key_width, dtype=jnp.float32), (value_heads, key_width, key_width)
-    )
-    identity_shift = jnp.zeros((value_heads, key_width, DV), jnp.float32)
-    prefix = hand_on(
-        (maps[:, :, :key_width], maps[:, :, key_width:]),
-        compose_maps,
-        (identity_map, identity_shift),
-    )
-    incoming = prefix[1]
-    recurrent = jax.vmap(head_outputs)(pieces, incoming)
+    incl_map, incl_shift = chunk_prefix(step_map, step_shift)
+    entering = segment_entry(incl_map[:, -1], incl_shift[:, -1], "exp")
+    after = mm(incl_map[:, :-1], entering[:, None]) + incl_shift[:, :-1]
+    chunk_states = jnp.concatenate([entering[:, None], after], axis=1)
+    recurrent = chunk_outputs(parts, chunk_states)
     recurrent = jnp.moveaxis(recurrent.reshape(value_heads, seg_rows, DV), 0, 1)
     gate_heads = gate_proj.reshape(seg_rows, value_heads, DV)
     gated = (

time: 1220 us -> 768 us (0.63)
  other arithmetic: 394 us -> 49.9 us
  blocking collectives: 178 us -> 120 us
  matrix products: 227 us -> 177 us
  waiting for transfers between devices: 225 us -> 175 us
  local copies, waits for them, and re-layouts: 162 us -> 195 us
  starting transfers between devices: 6 us -> 28.2 us
    another operation x6 -> x4, other arithmetic: 317 us -> 3.06 us  [the longest x2 316 us: span_parts(): lax.linalg.triangular_solve(system, targets, left_side=True, lower=True,...]
    all_gather x2 -> x0, waiting for transfers between devices: 86.4 us -> none  [carried_in(): pieces = jax.tree.map(lambda part: lax.all_gather(part, axis), value)]
    unnamed x74 -> x95, local copies, waits for them, and re-layouts: 6.19 us -> 58.8 us
    dot_general x113 -> x28, matrix products: 174 us -> 129 us  [the longest x26 122 us: mm(): return jnp.matmul(a, b, precision=HIGHEST)]
    unnamed x1 -> x0, blocking collectives: 29.9 us -> none
    select_n x15 -> x4, other arithmetic: 30.7 us -> 1.23 us  [segment_entry(): seg_map = jnp.where(has, both[0, ..., :width], seg_map)]
    slice x2 -> x15, local copies, waits for them, and re-layouts: 0.97 us -> 24.1 us  [the longest x4 10.6 us: chunk_prefix(): joined[..., width:] + step_shift]
    ppermute x0 -> x5, starting transfers between devices: none -> 22.3 us  [the longest x3 13.3 us: segment_entry(): lax.ppermute(jnp.concatenate([seg_map, seg_shift], axis=-1), axis, pairs)]
  transfers between devices with their start and end apart: 5 -> 8, of which waited for: 4 -> 7; matrix products, arithmetic and copies ran while one was open for 3% -> 3% of each run, Pallas kernels for 0% -> 0%
where the time goes in v1:
time: 768 us; the launch traced here: 760 us
  local copies, waits for them, and re-layouts  195 us (25%)
  matrix products  177 us (23%)
  waiting for transfers between devices  175 us (23%)
  blocking collectives  120 us (16%)
  other arithmetic  49.9 us (6%)
  starting transfers between devices  28.2 us (4%)
  between operations  14.9 us (2%)
    dot_general x26, matrix products, mm(): return jnp.matmul(a, b, precision=HIGHEST)  122 us
    all_to_all x1, blocking collectives, local(): lax.all_to_all(outgoing.reshape(devices, slot_count, model_width), ('seq'...  107 us
    all_to_all x1, waiting for transfers between devices, local(): lax.all_to_all(answers, ('seq', 'exp'), split_axis=0, concat_axis=0, tile...  107 us
    unnamed x95, local copies, waits for them, and re-layouts  58.8 us
    scatter x1, local copies, waits for them, and re-layouts, local(): outgoing = jnp.zeros((experts_all * capacity, model_width), jnp.bfloat16)...  34.1 us
    reduce_scatter x1, waiting for transfers between devices, local(): lax.psum_scatter(jnp.dot(picked, w_out, preferred_element_type=jnp.float3...  31.9 us
    reshape x2, local copies, waits for them, and re-layouts, local(): returned.reshape(experts_all * capacity, model_width)[slots]  20.3 us
    all_gather x1, waiting for transfers between devices, local(): lax.all_gather(normed, 'seq', axis=0, tiled=True)  18.9 us
  transfers between devices with their start and end apart: 8, of which 7 were waited for; matrix products, arithmetic and copies ran while one was open for 3% of the time, Pallas kernels for 0%

profile of v1, /device:TPU:5, one launch (start us, length us, event | category | flops | bytes accessed | tf_op | source)
XLA Modules:
  0.0 759.9 jit_solution(8766014096523694381)
XLA Ops:
  11.5 13.3 %all_gather.6 = bf16[1024,64]{0,1:T(8,128)(2,1)S(1)} all-gather(bf16[128,64]{0,1:T(8,128)(2,1)S(1)} %convolution_convert_fusion.2), channel_id=1, replica_groups=mesh['seq'=8,'exp'=16] {'seq'}, dimensions={0}, use_global_device_ids=true | all-gather | bytes 147456 | tf_op jit(solution)/shard_map/all_gather | solution.py:178
  26.4 18.9 %all-gather.2.cloned.1.call-done = bf16[1024,2048]{1,0:T(8,128)(2,1)} async-done(((bf16[128,2048]{1,0:T(8,128)(2,1)}), bf16[1024,2048]{1,0:T(8,128)(2,1)}) %all-gather.2.cloned.1.call-update) | async-done | bytes 4194320 | tf_op jit(solution)/shard_map/all_gather | solution.py:177
  111.1 7.8 %fusion.79 = f32[4,16,128,128]{2,3,1,0:T(8,128)S(1)} fusion(f32[4,16,64,128]{3,2,1,0:T(8,128)S(1)} %fusion.66, f32[4,16,64,128]{3,2,1,0:T(8,128)S(1)} %bitcast.228, f32[4,16,64]{2,1,0:T(8,128)S(1)} %get-tuple-element.17), kind=kOutput, calls=%fused_computation.97 | convolution fusion | flops 805830656 | bytes 8404992 | tf_op jit(solution)/shard_map/dot_general | solution.py:37
  123.1 8.0 %multiply_subtract_fusion = f32[4,16,128,128]{2,3,1,0:T(8,128)S(1)} fusion(f32[4,16,64,128]{3,2,1,0:T(8,128)S(1)} %fusion.68, f32[128,128]{0,1:T(8,128)S(1)} %fusion.155, f32[4,16]{1,0:T(4,128)S(1)} %exp.57, f32[4,16,64,128]{3,2,1,0:T(8,128)S(1)} %bitcast.230, f32[4,16,64]{2,1,0:T(8,128)S(1)} %get-tuple-element.17), kind=kOutput, calls=%fused_computation.48 | convolution fusion | flops 807927808 | bytes 8470784 | tf_op jit(solution)/shard_map/dot_general | solution.py:37
  136.0 10.0 %fusion.6 = f32[4,16,128,256]{3,2,1,0:T(8,128)S(1)} fusion(f32[4,16,128,128]{2,3,1,0:T(8,128)} %copy-done.7, f32[4,15,128,128]{2,3,1,0:T(8,128)S(1)} %slice-done, f32[4,15,128,128]{2,3,1,0:T(8,128)} %slice.264, f32[4,1,128,128]{2,3,1,0:T(8,128)} %broadcast_in_dim.78), kind=kOutput, calls=%fused_computation.13 | convolution fusion | flops 3229614080 | bytes 20709376 | tf_op jit(solution)/shard_map/dot_general | solution.py:37
  171.5 10.6 %fusion.4 = f32[4,16,128,256]{3,2,1,0:T(8,128)S(1)} fusion(f32[4,14,128,128]{2,3,1,0:T(8,128)} %slice.274, f32[4,14,128,128]{2,3,1,0:T(8,128)} %copy.127, f32[4,2,128,128]{2,3,1,0:T(8,128)S(1)} %broadcast_in_dim.79, f32[4,16,128,256]{3,2,1,0:T(8,128)} %copy-done.4), kind=kOutput, calls=%fused_computation.10 | convolution fusion | flops 3229614080 | bytes 20447232 | tf_op jit(solution)/shard_map/dot_general | solution.py:37
  188.6 5.6 copy.130
  205.8 10.7 %fusion.2 = f32[4,16,128,256]{3,2,1,0:T(8,128)S(1)} fusion(f32[4,12,128,128]{2,3,1,0:T(8,128)} %slice.278, f32[4,12,128,128]{2,3,1,0:T(8,128)} %copy.129, f32[4,4,128,128]{2,3,1,0:T(8,128)S(1)} %broadcast_in_dim.80, f32[4,16,128,256]{3,2,1,0:T(8,128)} %copy-done.5), kind=kOutput, calls=%fused_computation.7 | convolution fusion | flops 3229614080 | bytes 19922944 | tf_op jit(solution)/shard_map/dot_general | solution.py:37
  240.9 10.9 %fusion = f32[4,16,128,256]{3,2,1,0:T(8,128)S(1)} fusion(f32[4,8,128,128]{2,3,1,0:T(8,128)S(1)} %copy-done.24, f32[4,8,128,128]{2,3,1,0:T(8,128)} %copy.131, f32[4,8,128,128]{2,3,1,0:T(8,128)} %broadcast_in_dim.81, f32[4,16,128,256]{3,2,1,0:T(8,128)} %copy-done.6), kind=kOutput, calls=%fused_computation.4 | convolution fusion | flops 3229614080 | bytes 18874368 | tf_op jit(solution)/shard_map/dot_general | solution.py:37
  256.5 5.8 copy.134
  272.3 6.6 fusion.196
  286.8 7.3 collective-permute-start.2
  295.5 7.5 collective-permute-done.2
  310.0 5.4 collective-permute-done.3
  316.5 6.1 collective-permute-start.4
  326.8 6.4 slice_add_fusion
  333.2 8.7 %fusion.40 = f32[4,16,64,128]{3,2,1,0:T(8,128)S(1)} fusion(f32[4,16,64,128]{3,2,1,0:T(8,128)S(1)} %copy-done.16, f32[4,15,128,128]{2,3,1,0:T(8,128)S(1)} %slice_add_fusion, f32[4,1,128,128]{2,3,1,0:T(8,128)S(1)} %bitcast.242), kind=kOutput, calls=%fused_computation.53 | convolution fusion | flops 806354944 | bytes 8388608 | tf_op jit(solution)/shard_map/dot_general | solution.py:37
  344.6 9.5 %fusion.84 = f32[4,16,64,128]{3,2,1,0:T(8,128)} fusion(f32[4,16,64,128]{3,2,1,0:T(8,128)S(1)} %fusion.63, f32[4,15,128,128]{2,3,1,0:T(8,128)S(1)} %slice_add_fusion, f32[4,1,128,128]{2,3,1,0:T(8,128)S(1)} %bitcast.243, f32[4,16,64,128]{3,2,1,0:T(8,128)S(1)} %bitcast.233, f32[4,16,64]{2,1,0:T(8,128)S(1)} %get-tuple-element.15), kind=kOutput, calls=%fused_computation.104 | convolution fusion | flops 807403520 | bytes 10502144 | tf_op jit(solution)/shard_map/dot_general | solution.py:37
  374.7 31.9 %reduce-scatter.2.cloned.1.call-done = bf16[128,2048]{1,0:T(8,128)(2,1)} async-done(((bf16[1024,2048]{1,0:T(8,128)(2,1)}), bf16[128,2048]{1,0:T(8,128)(2,1)}) %reduce-scatter.2.cloned.1.call-update) | async-done | bytes 524304 | tf_op jit(solution)/shard_map/reduce_scatter | solution.py:233
  409.2 34.1 %scatter_custom_fusion = bf16[1536,2048]{1,0:T(8,128)(2,1)} fusion(s32[1280]{0:T(1024)S(1)} %fusion.159, bf16[128,2048]{1,0:T(8,128)(2,1)S(1)} %fusion.106, s32[2048]{0:T(1024)S(1)} %pad_clamp_fusion.1, bf16[]{:T(256)} %constant.82.clone.1), kind=kCustom, calls=%fused_computation.28 | custom fusion | bytes 6291458 | tf_op jit(solution)/shard_map/scatter | solution.py:256
  443.3 10.6 %reshape.246 = bf16[128,12,2048]{2,1,0:T(8,128)(2,1)} reshape(bf16[1536,2048]{1,0:T(8,128)(2,1)} %scatter_custom_fusion) | data formatting | bytes 12582912 | tf_op jit(solution)/shard_map/reshape | solution.py:260
  453.9 106.7 %all_to_all.10 = bf16[128,12,2048]{2,1,0:T(8,128)(2,1)S(1)} all-to-all(bf16[128,12,2048]{2,1,0:T(8,128)(2,1)} %reshape.246), channel_id=1, replica_groups=mesh['seq'=8,'exp'=16] {'seq','exp'}, dimensions={0} | all-to-all | bytes 12582912 | tf_op jit(solution)/shard_map/all_to_all | solution.py:259
  560.6 6.1 copy.94
  566.7 9.1 %fusion.34 = f32[2,128,6,512]{3,1,2,0:T(8,128)} fusion(bf16[128,2,6,2048]{3,0,2,1:T(8,128)(2,1)} %bitcast.239, bf16[2,2048,512]{2,1,0:T(8,128)(2,1)} %param.38), kind=kOutput, calls=%fused_computation.44 | convolution fusion | flops 3221225472 | bytes 13631488 | tf_op jit(solution)/shard_map/pecd,edf->pecf/dot_general | solution.py:139
  575.7 12.7 %convolution_convert_fusion = bf16[2,128,6,2048]{3,1,2,0:T(8,128)(2,1)} fusion(bf16[2,512,2048]{2,1,0:T(8,128)(2,1)} %param.39, f32[2,128,6,512]{3,1,2,0:T(8,128)} %fusion.34, bf16[128,2,6,2048]{3,0,2,1:T(8,128)(2,1)} %bitcast.240, bf16[2,2048,512]{2,1,0:T(8,128)(2,1)} %param.37), kind=kOutput, calls=%fused_computation.30 | convolution fusion | flops 6450315264 | bytes 24117248 | tf_op jit(solution)/shard_map/pecf,efd->pecd/dot_general | solution.py:141
  588.5 9.7 %copy.95 = bf16[128,12,2048]{2,1,0:T(8,128)(2,1)} copy(bf16[128,12,2048]{2,0,1:T(8,128)(2,1)} %bitcast.241) | data formatting | bytes 12582912 | tf_op jit(solution)/shard_map/reshape | solution.py:144
  598.1 5.9 all-to-all-start.1
  604.1 106.6 %all-to-all-done.1 = bf16[128,12,2048]{2,1,0:T(8,128)(2,1)} async-done(((bf16[128,12,2048]{2,1,0:T(8,128)(2,1)}), bf16[128,12,2048]{2,1,0:T(8,128)(2,1)}, u32[]{:S(2)}, u32[]{:S(2)}) %all-to-all-start.1) | async-done | bytes 6291488 | tf_op jit(solution)/shard_map/all_to_all | solution.py:269
  710.7 10.7 %reshape.249 = bf16[1536,2048]{1,0:T(8,128)(2,1)} reshape(bf16[128,12,2048]{2,1,0:T(8,128)(2,1)} %all-to-all-done.1) | data formatting | bytes 12582912 | tf_op jit(solution)/shard_map/reshape | solution.py:270
  721.4 14.4 %gather_fusion = bf16[1280,2048]{1,0:T(8,128)(2,1)} fusion(bf16[1536,2048]{1,0:T(8,128)(2,1)} %reshape.249, s32[2048]{0:T(1024)S(1)} %pad_clamp_fusion), kind=kCustom, calls=%fused_computation.1 | custom fusion | bytes 10490880 | tf_op jit(solution)/shard_map/gather | solution.py:270
  735.9 9.6 %reshape.250 = bf16[128,10,2048]{2,1,0:T(8,128)(2,1)} reshape(bf16[1280,2048]{1,0:T(8,128)(2,1)} %gather_fusion) | data formatting | bytes 10485760 | tf_op jit(solution)/shard_map/reshape | solution.py:270
  745.4 5.9 fusion.197
  (225 shorter events, 211.9 us)
Async XLA Ops:
  6.5 355.0 %copy-start = (bf16[512,2048]{1,0:T(8,128)(2,1)S(1)}, bf16[512,2048]{1,0:T(8,128)(2,1)}, u32[]{:S(2)}) copy-start(bf16[512,2048]{1,0:T(8,128)(2,1)} %param.34) | copy-start | bytes 6291460
  6.5 18.3 %copy-start.42 = (f32[4]{0:T(128)S(1)}, f32[4]{0:T(128)}, u32[]{:S(2)}) copy-start(f32[4]{0:T(128)} %param.31) | copy-start | bytes 52
  6.5 18.3 %copy-start.37 = (f32[4]{0:T(128)S(1)}, f32[4]{0:T(128)}, u32[]{:S(2)}) copy-start(f32[4]{0:T(128)} %param.32) | copy-start | bytes 52
  6.5 19.7 %copy-start.35 = (f32[4,256]{1,0:T(4,128)S(1)}, f32[4,256]{1,0:T(4,128)}, u32[]{:S(2)}) copy-start(f32[4,256]{1,0:T(4,128)} %param.29) | copy-start | bytes 12292
  6.5 19.7 %copy-start.36 = (f32[4,256]{1,0:T(4,128)S(1)}, f32[4,256]{1,0:T(4,128)}, u32[]{:S(2)}) copy-start(f32[4,256]{1,0:T(4,128)} %param.28) | copy-start | bytes 12292
  6.6 19.7 %copy-start.33 = (f32[4,512]{1,0:T(4,128)S(1)}, f32[4,512]{1,0:T(4,128)}, u32[]{:S(2)}) copy-start(f32[4,512]{1,0:T(4,128)} %param.30) | copy-start | bytes 24580
  6.6 38.7 %all-gather.2.cloned.1.call-start = ((), (), s32[]{:S(2)}) async-start(), calls=%async_computation.3 | async-start | bytes 4718592 | tf_op jit(solution)/shard_map/all_gather | solution.py:177
  10.1 396.5 %reduce-scatter.2.cloned.1.call-start = ((), (), s32[]{:S(2)}) async-start(), calls=%async_computation.4 | async-start | bytes 4718592 | tf_op jit(solution)/shard_map/reduce_scatter | solution.py:233
  45.3 5.4 copy-start.39
  45.3 5.4 copy-start.40
  54.9 4.5 collective-permute-start
  111.1 7.8 %copy-start.13 = (f32[4,16,64,128]{3,2,1,0:T(8,128)}, f32[4,16,64,128]{3,2,1,0:T(8,128)S(1)}, u32[]{:S(2)}) copy-start(f32[4,16,64,128]{3,2,1,0:T(8,128)S(1)} %fusion.66) | copy-start | bytes 6291460
  123.1 8.0 %copy-start.15 = (f32[4,16,64,128]{3,2,1,0:T(8,128)}, f32[4,16,64,128]{3,2,1,0:T(8,128)S(1)}, u32[]{:S(2)}) copy-start(f32[4,16,64,128]{3,2,1,0:T(8,128)S(1)} %fusion.68) | copy-start | bytes 6291460
  131.1 4.0 copy-start.7
  131.1 4.9 slice-start
  146.0 4.5 copy-start.4
  182.1 4.5 copy-start.5
  216.6 4.5 copy-start.6
  251.9 4.6 copy-start.10
  269.5 14.2 %collective-permute-start.1 = (f32[4,128,256]{1,2,0:T(8,128)}, f32[4,128,256]{1,2,0:T(8,128)}, u32[]{:S(2)}, u32[]{:S(2)}) collective-permute-start(f32[4,128,256]{1,2,0:T(8,128)} %pad_maximum_fusion.8), channel_id=1, source_target_pairs={{0,1},{1,2},{2,3},{3,4},{4,5},{5,6},{6,7},{7,8},{8,9},{9,10},{10,1... | collective-permute-start | bytes 1572872 | tf_op jit(solution)/shard_map/ppermute | solution.py:110
  286.8 16.2 %collective-permute-start.2 = (f32[4,128,256]{1,2,0:T(8,128)S(1)}, f32[4,128,256]{1,2,0:T(8,128)S(1)}, u32[]{:S(2)}, u32[]{:S(2)}) collective-permute-start(f32[4,128,256]{1,2,0:T(8,128)S(1)} %pad_maximum_fusion.9), channel_id=1, source_target_pairs={{0,2},{1,3},{2,4},{3,5},{4,6},{5,7},{6,8},{7,9},{8,10},{9,11},{10,... | collective-permute-start | bytes 1572872 | tf_op jit(solution)/shard_map/ppermute | solution.py:110
  304.2 11.3 %collective-permute-start.3 = (f32[4,128,256]{1,2,0:T(8,128)S(1)}, f32[4,128,256]{1,2,0:T(8,128)S(1)}, u32[]{:S(2)}, u32[]{:S(2)}) collective-permute-start(f32[4,128,256]{1,2,0:T(8,128)S(1)} %pad_maximum_fusion.10), channel_id=1, source_target_pairs={{0,4},{1,5},{2,6},{3,7},{4,8},{5,9},{6,10},{7,11},{8,12},{9,13},{1... | collective-permute-start | bytes 1572872 | tf_op jit(solution)/shard_map/ppermute | solution.py:110
  316.5 6.3 copy-start.3
  316.5 9.8 %collective-permute-start.4 = (f32[4,128,128]{1,2,0:T(8,128)S(1)}, f32[4,128,128]{1,2,0:T(8,128)S(1)}, u32[]{:S(2)}, u32[]{:S(2)}) collective-permute-start(f32[4,128,128]{1,2,0:T(8,128)S(1)} %fusion.140), channel_id=1, source_target_pairs={{0,8},{1,9},{2,10},{3,11},{4,12},{5,13},{6,14},{7,15},{16,24},{17,... | collective-permute-start | bytes 786440 | tf_op jit(solution)/shard_map/ppermute | solution.py:107
  322.8 3.9 copy-start.21
  326.7 6.4 copy-start.16
  333.2 8.7 %copy-start.14 = (f32[4,16,64,128]{3,2,1,0:T(8,128)S(1)}, f32[4,16,64,128]{3,2,1,0:T(8,128)}, u32[]{:S(2)}) copy-start(f32[4,16,64,128]{3,2,1,0:T(8,128)} %copy-done.13) | copy-start | bytes 6291460
  370.7 35.9 %copy-start.22 = (bf16[1,128,2048]{2,1,0:T(8,128)(2,1)S(1)}, bf16[1,128,2048]{2,1,0:T(8,128)(2,1)}, u32[]{:S(2)}) copy-start(bf16[1,128,2048]{2,1,0:T(8,128)(2,1)} %param.20) | copy-start | bytes 1572868
  372.6 35.3 %copy-start.32 = (f32[2048]{0:T(1024)S(1)}, f32[2048]{0:T(1024)}, u32[]{:S(2)}) copy-start(f32[2048]{0:T(1024)} %param.22) | copy-start | bytes 24580
  598.1 5.9 copy-start.34
  598.1 112.6 %all-to-all-start.1 = ((bf16[128,12,2048]{2,1,0:T(8,128)(2,1)}), bf16[128,12,2048]{2,1,0:T(8,128)(2,1)}, u32[]{:S(2)}, u32[]{:S(2)}) async-start(bf16[128,12,2048]{2,1,0:T(8,128)(2,1)} %copy.95), calls=%async_computation.2 | async-start | bytes 16777216 | tf_op jit(solution)/shard_map/all_to_all | solution.py:269
  745.4 6.0 copy-start.26
  (20 other events, 44.7 us)
Sparse Core Ops, SparseCore 0:
  10.2 35.0 all-gather.1
  366.1 40.4 reduce-scatter.1

commit v2 on v1

--- a/solution.py
+++ b/solution.py
@@ -74,24 +74,6 @@
 
 def ending_eye(scale, width):
     return scale[..., None, None] * jnp.eye(width, dtype=jnp.float32)
-
-
-def chunk_prefix(step_map, step_shift):
-    chunks = step_map.shape[1]
-    width = step_map.shape[-1]
-    reach = 1
-    while reach < chunks:
-        eye = jnp.broadcast_to(
-            jnp.eye(width, dtype=jnp.float32), step_map[:, :reach].shape
-        )
-        prev_map = jnp.concatenate([eye, step_map[:, : chunks - reach]], axis=1)
-        prev_shift = jnp.concatenate(
-            [jnp.zeros_like(step_shift[:, :reach]), step_shift[:, : chunks - reach]], axis=1
-        )
-        joined = mm(step_map, jnp.concatenate([prev_map, prev_shift], axis=-1))
-        step_map, step_shift = joined[..., :width], joined[..., width:] + step_shift
-        reach *= 2
-    return step_map, step_shift
 
 
 def segment_entry(seg_map, seg_shift, axis):
@@ -118,10 +100,39 @@
     return excl_shift
 
 
+def tree_compose(step_map, step_shift):
+    width = step_map.shape[-1]
+    maps = [step_map[:, c] for c in range(step_map.shape[1])]
+    shifts = [step_shift[:, c] for c in range(step_shift.shape[1])]
+    while len(maps) > 1:
+        pairs = len(maps) // 2
+        early = jnp.stack(
+            [jnp.concatenate([maps[2 * i], shifts[2 * i]], axis=-1) for i in range(pairs)], axis=1
+        )
+        late_map = jnp.stack([maps[2 * i + 1] for i in range(pairs)], axis=1)
+        late_shift = jnp.stack([shifts[2 * i + 1] for i in range(pairs)], axis=1)
+        joined = mm(late_map, early)
+        new_maps = [joined[:, i, :, :width] for i in range(pairs)]
+        new_shifts = [joined[:, i, :, width:] + late_shift[:, i] for i in range(pairs)]
+        if len(maps) % 2:
+            new_maps.append(maps[-1])
+            new_shifts.append(shifts[-1])
+        maps, shifts = new_maps, new_shifts
+    return maps[0], shifts[0]
+
+
+def chunk_states_from(entering, step_map, step_shift):
+    states = [entering]
+    for c in range(step_map.shape[1] - 1):
+        states.append(mm(step_map[:, c], states[-1]) + step_shift[:, c])
+    return jnp.stack(states, axis=1)
+
+
 def chunk_outputs(parts, chunk_states):
     query_fade, scores, key_mix, value_mix = parts
-    new_values = value_mix - mm(key_mix, chunk_states)
-    return mm(query_fade, chunk_states) + mm(scores, new_values)
+    fixed = mm(scores, value_mix)
+    reader = query_fade - mm(scores, key_mix)
+    return fixed + mm(reader, chunk_states)
 
 
 def head_spans(values):
@@ -217,10 +228,9 @@
         head_spans(beta_rates),
         head_spans(decays),
     )
-    incl_map, incl_shift = chunk_prefix(step_map, step_shift)
-    entering = segment_entry(incl_map[:, -1], incl_shift[:, -1], "exp")
-    after = mm(incl_map[:, :-1], entering[:, None]) + incl_shift[:, :-1]
-    chunk_states = jnp.concatenate([entering[:, None], after], axis=1)
+    seg_map, seg_shift = tree_compose(step_map, step_shift)
+    entering = segment_entry(seg_map, seg_shift, "exp")
+    chunk_states = chunk_states_from(entering, step_map, step_shift)
     recurrent = chunk_outputs(parts, chunk_states)
     recurrent = jnp.moveaxis(recurrent.reshape(value_heads, seg_rows, DV), 0, 1)
     gate_heads = gate_proj.reshape(seg_rows, value_heads, DV)
@@ -249,29 +259,26 @@
     earlier = jnp.cumsum(onehot, axis=0) - onehot
     places = jnp.sum(earlier * onehot, axis=1)
     slots = pair_ids * capacity + places
-    sources = jnp.arange(pair_ids.shape[0], dtype=jnp.int32) // top_count
-    outgoing = (
-        jnp.zeros((experts_all * capacity, model_width), jnp.bfloat16)
-        .at[slots]
-        .set(moe_in[sources])
-    )
     slot_count = local_experts * capacity
-    arrived = lax.all_to_all(
-        outgoing.reshape(devices, slot_count, model_width),
-        ("seq", "exp"),
-        split_axis=0,
-        concat_axis=0,
-        tiled=True,
-    )
+    slot_table = slots.reshape(local_rows, top_count)
+    slot_grid = jnp.arange(experts_all * capacity, dtype=jnp.int32).reshape(devices, slot_count)
+    hits = slot_table[None, None, :, :] == slot_grid[:, :, None, None]
+    pick = jnp.any(hits, axis=-1).astype(jnp.bfloat16)
+    outgoing = jnp.einsum(
+        "dst,tx->dsx", pick, moe_in, preferred_element_type=jnp.float32
+    ).astype(jnp.bfloat16)
+    arrived = lax.all_to_all(outgoing, ("seq", "exp"), split_axis=0, concat_axis=0, tiled=True)
     answers = run_experts(
         arrived, local_experts, capacity, w_expert_gate, w_expert_up, w_expert_down
     )
     returned = lax.all_to_all(answers, ("seq", "exp"), split_axis=0, concat_axis=0, tiled=True)
-    picked = returned.reshape(experts_all * capacity, model_width)[slots].reshape(
-        local_rows, top_count, model_width
-    )
     gates = route_gates.reshape(local_rows, top_count)
-    moe_sum = jnp.einsum("tk,tkd->td", gates, picked.astype(jnp.float32), precision=HIGHEST)
+    weight = jnp.sum(
+        jnp.where(hits, gates[None, None, :, :], 0.0), axis=-1
+    )
+    moe_sum = jnp.einsum(
+        "dst,dsx->tx", weight, returned.astype(jnp.float32), precision=HIGHEST
+    )
     mixed = (residual.astype(jnp.float32) + moe_sum).astype(jnp.bfloat16)
     return mixed.reshape(1, local_rows, model_width)
 

time: 768 us -> 615 us (0.80)
  local copies, waits for them, and re-layouts: 195 us -> 87.8 us
  matrix products: 177 us -> 138 us
  other arithmetic: 49.9 us -> 38.3 us
    dot_general x26 -> x40, matrix products: 122 us -> 75.8 us  [mm(): return jnp.matmul(a, b, precision=HIGHEST)]
    scatter x1 -> x0, local copies, waits for them, and re-layouts: 34.1 us -> none  [local(): outgoing = jnp.zeros((experts_all * capacity, model_width), jnp.bfloat16)...]
    reshape x4 -> x0, local copies, waits for them, and re-layouts: 31 us -> none  [the longest x2 20.3 us: local(): returned.reshape(experts_all * capacity, model_width)[slots]]
    slice x15 -> x4, local copies, waits for them, and re-layouts: 23.9 us -> 4.1 us  [the longest x2 3.19 us: tree_compose(): joined[:, i, :, width:] + late_shift[:, i]]
    gather x1 -> x0, local copies, waits for them, and re-layouts: 14.4 us -> none  [local(): returned.reshape(experts_all * capacity, model_width)[slots]]
    unnamed x95 -> x128, local copies, waits for them, and re-layouts: 58.8 us -> 44.5 us
    add x4, other arithmetic: 16.9 us -> 4.43 us  [the longest x3 4.42 us: tree_compose(): joined[:, i, :, width:] + late_shift[:, i]]
    dot_general x1 -> x2, matrix products: 5.95 us -> 16.6 us  [the longest x1 13.7 us: local(): jnp.einsum('dst,dsx->tx', weight, returned.astype(jnp.float32), precision...]
  transfers between devices with their start and end apart: 8 -> 8, of which waited for: 7 -> 7; matrix products, arithmetic and copies ran while one was open for 3% -> 4% of each run, Pallas kernels for 0% -> 0%
where the time goes in v2:
time: 615 us; the launch traced here: 605 us
  waiting for transfers between devices  179 us (29%)
  matrix products  138 us (22%)
  blocking collectives  120 us (20%)
  local copies, waits for them, and re-layouts  87.8 us (14%)
  other arithmetic  38.3 us (6%)
  starting transfers between devices  26.5 us (4%)
  between operations  15 us (2%)
    all_to_all x1, blocking collectives, local(): lax.all_to_all(outgoing, ('seq', 'exp'), split_axis=0, concat_axis=0, til...  107 us
    all_to_all x1, waiting for transfers between devices, local(): lax.all_to_all(answers, ('seq', 'exp'), split_axis=0, concat_axis=0, tile...  105 us
    dot_general x40, matrix products, mm(): return jnp.matmul(a, b, precision=HIGHEST)  75.8 us
    unnamed x128, local copies, waits for them, and re-layouts  44.5 us
    reduce_scatter x1, waiting for transfers between devices, local(): lax.psum_scatter(jnp.dot(picked, w_out, preferred_element_type=jnp.float3...  32.2 us
    ppermute x3, waiting for transfers between devices, segment_entry(): lax.ppermute(jnp.concatenate([seg_map, seg_shift], axis=-1), axis, pairs)  22.4 us
    all_gather x1, waiting for transfers between devices, local(): lax.all_gather(normed, 'seq', axis=0, tiled=True)  18.8 us
    dot_general x1, matrix products, local(): jnp.einsum('dst,dsx->tx', weight, returned.astype(jnp.float32), precision...  13.7 us
  transfers between devices with their start and end apart: 8, of which 7 were waited for; matrix products, arithmetic and copies ran while one was open for 4% of the time, Pallas kernels for 0%

profile of v2, /device:TPU:5, one launch (start us, length us, event | category | flops | bytes accessed | tf_op | source)
XLA Modules:
  0.0 604.5 jit_solution(6860642544151367352)
XLA Ops:
  11.5 13.3 %all_gather.7 = bf16[1024,64]{0,1:T(8,128)(2,1)S(1)} all-gather(bf16[128,64]{0,1:T(8,128)(2,1)S(1)} %convolution_convert_fusion.3), channel_id=1, replica_groups=mesh['seq'=8,'exp'=16] {'seq'}, dimensions={0}, use_global_device_ids=true | all-gather | bytes 147456 | tf_op jit(solution)/shard_map/all_gather | solution.py:189
  26.5 18.8 %all-gather.2.cloned.1.call-done = bf16[1024,2048]{1,0:T(8,128)(2,1)} async-done(((bf16[128,2048]{1,0:T(8,128)(2,1)}), bf16[1024,2048]{1,0:T(8,128)(2,1)}) %all-gather.2.cloned.1.call-update) | async-done | bytes 4194320 | tf_op jit(solution)/shard_map/all_gather | solution.py:188
  45.3 3.9 fusion.200
  57.4 3.8 fusion.211
  65.2 5.6 divide_multiply_fusion
  70.8 2.9 reshape.185
  73.7 3.1 copy.378
  85.6 3.6 select_negate_fusion
  116.9 7.6 %fusion.44 = f32[4,16,128,128]{2,3,0,1:T(8,128)S(1)} fusion(f32[4,16,64,128]{3,2,1,0:T(8,128)S(1)} %fusion.53, f32[4,16,64,128]{3,2,1,0:T(8,128)S(1)} %bitcast.540, f32[4,16,64]{2,1,0:T(8,128)S(1)} %get-tuple-element.70), kind=kOutput, calls=%fused_computation.49 | convolution fusion | flops 805830656 | bytes 8404992 | tf_op jit(solution)/shard_map/dot_general | solution.py:37
  124.6 8.4 %multiply_subtract_fusion = f32[4,16,128,128]{2,3,1,0:T(8,128)S(1)} fusion(f32[4,16,64,128]{3,2,1,0:T(8,128)S(1)} %fusion.50, f32[128,128]{0,1:T(8,128)S(1)} %fusion.179, f32[4,16]{1,0:T(4,128)S(1)} %exp.61, f32[4,16,64,128]{3,2,1,0:T(8,128)S(1)} %bitcast.541, f32[4,16,64]{2,1,0:T(8,128)S(1)} %get-tuple-element.70), kind=kOutput, calls=%fused_computation.16 | convolution fusion | flops 807927808 | bytes 8470784 | tf_op jit(solution)/shard_map/dot_general | solution.py:37
  135.5 3.8 fusion.10
  193.0 3.1 collective-permute-start.1
  198.7 9.2 %collective-permute-done.1 = f32[4,128,256]{1,2,0:T(8,128)S(1)} collective-permute-done((f32[4,128,256]{1,2,0:T(8,128)S(1)}, f32[4,128,256]{1,2,0:T(8,128)S(1)}, u32[]{:S(2)}, u32[]{:S(2)}) %collective-permute-start.1) | collective-permute-done | bytes 524320 | tf_op jit(solution)/shard_map/ppermute | solution.py:92
  209.1 5.0 collective-permute-start.2
  214.2 3.6 fusion.55
  217.8 6.8 %collective-permute-done.2 = f32[4,128,256]{1,2,0:T(8,128)S(1)} collective-permute-done((f32[4,128,256]{1,2,0:T(8,128)S(1)}, f32[4,128,256]{1,2,0:T(8,128)S(1)}, u32[]{:S(2)}, u32[]{:S(2)}) %collective-permute-start.2) | collective-permute-done | bytes 524320 | tf_op jit(solution)/shard_map/ppermute | solution.py:92
  225.8 3.0 collective-permute-start.3
  231.2 6.4 %collective-permute-done.3 = f32[4,128,256]{1,2,0:T(8,128)S(1)} collective-permute-done((f32[4,128,256]{1,2,0:T(8,128)S(1)}, f32[4,128,256]{1,2,0:T(8,128)S(1)}, u32[]{:S(2)}, u32[]{:S(2)}) %collective-permute-start.3) | collective-permute-done | bytes 524320 | tf_op jit(solution)/shard_map/ppermute | solution.py:92
  238.8 6.3 %collective-permute-start.4 = (f32[4,128,128]{1,2,0:T(8,128)S(1)}, f32[4,128,128]{1,2,0:T(8,128)S(1)}, u32[]{:S(2)}, u32[]{:S(2)}) collective-permute-start(f32[4,128,128]{1,2,0:T(8,128)S(1)} %fusion.143), channel_id=1, source_target_pairs={{0,8},{1,9},{2,10},{3,11},{4,12},{5,13},{6,14},{7,15},{16,24},{17,... | collective-permute-start | bytes 786440 | tf_op jit(solution)/shard_map/ppermute | solution.py:89
  254.2 9.7 %fusion.64 = f32[4,16,64,128]{3,2,1,0:T(8,128)} fusion(f32[4,16,64,128]{3,2,1,0:T(8,128)S(1)} %fusion.209, f32[4,16,128,128]{2,3,0,1:T(8,128)S(1)} %fusion.73, f32[4,16,64,128]{3,2,1,0:T(8,128)S(1)} %fusion.210, f32[4,16,64,128]{3,2,1,0:T(8,128)S(1)} %bitcast.544, f32[4,16,64]{2,1,0:T(8,128)S(1)} %get-tuple-element.68), kind=kOutput, calls=%fused_computation.72 | convolution fusion | flops 806879232 | bytes 12599296 | tf_op jit(solution)/shard_map/dot_general | solution.py:37
  263.9 2.9 copy.487
  271.4 4.4 convolution_convert_fusion.2
  283.0 32.2 %reduce-scatter.2.cloned.1.call-done = bf16[128,2048]{1,0:T(8,128)(2,1)} async-done(((bf16[1024,2048]{1,0:T(8,128)(2,1)}), bf16[128,2048]{1,0:T(8,128)(2,1)}) %reduce-scatter.2.cloned.1.call-update) | async-done | bytes 524304 | tf_op jit(solution)/shard_map/reduce_scatter | solution.py:243
  319.5 7.3 %copy.494 = bf16[128,12,2048]{2,1,0:T(8,128)(2,1)} copy(bf16[128,12,2048]{2,0,1:T(8,128)(2,1)S(1)} %convolution_convert_fusion) | data formatting | bytes 12582912 | tf_op jit(solution)/shard_map/convert_element_type | solution.py:269
  326.8 106.8 %all_to_all.10 = bf16[128,12,2048]{2,1,0:T(8,128)(2,1)S(1)} all-to-all(bf16[128,12,2048]{2,1,0:T(8,128)(2,1)} %copy.494), channel_id=1, replica_groups=mesh['seq'=8,'exp'=16] {'seq','exp'}, dimensions={0} | all-to-all | bytes 12582912 | tf_op jit(solution)/shard_map/all_to_all | solution.py:270
  433.6 6.1 %copy.495 = bf16[128,12,2048]{2,0,1:T(8,128)(2,1)} copy(bf16[128,12,2048]{2,1,0:T(8,128)(2,1)S(1)} %all_to_all.10) | data formatting | bytes 12582912 | tf_op jit(solution)/shard_map/all_to_all | solution.py:270
  439.8 9.1 %fusion.4 = f32[2,128,6,512]{3,1,2,0:T(8,128)} fusion(bf16[128,2,6,2048]{3,0,2,1:T(8,128)(2,1)} %bitcast.548, bf16[2,2048,512]{2,1,0:T(8,128)(2,1)} %param.38), kind=kOutput, calls=%fused_computation.8 | convolution fusion | flops 3221225472 | bytes 13631488 | tf_op jit(solution)/shard_map/pecd,edf->pecf/dot_general | solution.py:150
  448.8 12.5 %convolution_convert_fusion.1 = bf16[2,128,6,2048]{3,1,2,0:T(8,128)(2,1)} fusion(bf16[2,512,2048]{2,1,0:T(8,128)(2,1)} %param.39, f32[2,128,6,512]{3,1,2,0:T(8,128)} %fusion.4, bf16[128,2,6,2048]{3,0,2,1:T(8,128)(2,1)} %bitcast.549, bf16[2,2048,512]{2,1,0:T(8,128)(2,1)} %param.37), kind=kOutput, calls=%fused_computation.6 | convolution fusion | flops 6450315264 | bytes 24117248 | tf_op jit(solution)/shard_map/pecf,efd->pecd/dot_general | solution.py:152
  461.3 9.7 %copy.496 = bf16[128,12,2048]{2,1,0:T(8,128)(2,1)} copy(bf16[128,12,2048]{2,0,1:T(8,128)(2,1)} %bitcast.550) | data formatting | bytes 12582912 | tf_op jit(solution)/shard_map/reshape | solution.py:155
  471.0 6.2 %all-to-all-start.1 = ((bf16[128,12,2048]{2,1,0:T(8,128)(2,1)}), bf16[128,12,2048]{2,1,0:T(8,128)(2,1)}, u32[]{:S(2)}, u32[]{:S(2)}) async-start(bf16[128,12,2048]{2,1,0:T(8,128)(2,1)} %copy.496), calls=%async_computation.2 | async-start | bytes 16777216 | tf_op jit(solution)/shard_map/all_to_all | solution.py:274
  479.2 104.6 %all-to-all-done.1 = bf16[128,12,2048]{2,1,0:T(8,128)(2,1)} async-done(((bf16[128,12,2048]{2,1,0:T(8,128)(2,1)}), bf16[128,12,2048]{2,1,0:T(8,128)(2,1)}, u32[]{:S(2)}, u32[]{:S(2)}) %all-to-all-start.1) | async-done | bytes 6291488 | tf_op jit(solution)/shard_map/all_to_all | solution.py:274
  583.8 13.7 %fusion.27 = bf16[1,128,2048]{2,1,0:T(8,128)(2,1)} fusion(f32[128,12,128]{2,0,1:T(8,128)} %fusion, bf16[128,12,2048]{2,1,0:T(8,128)(2,1)} %all-to-all-done.1, bf16[128,2048]{1,0:T(8,128)(2,1)S(1)} %copy-done.19, bf16[1,128,2048]{2,1,0:T(8,128)(2,1)S(1)} %copy-done.14), kind=kOutput, calls=%fused_computation.30 | convolution fusion | flops 4833673216 | bytes 8650752 | tf_op jit(solution)/shard_map/dst,dsx->tx/dot_general | solution.py:279
  (265 shorter events, 146.2 us)
Async XLA Ops:
  6.5 264.9 %copy-start = (bf16[512,2048]{1,0:T(8,128)(2,1)S(1)}, bf16[512,2048]{1,0:T(8,128)(2,1)}, u32[]{:S(2)}) copy-start(bf16[512,2048]{1,0:T(8,128)(2,1)} %param.34) | copy-start | bytes 6291460
  6.5 3.6 copy-start.48
  6.5 3.6 copy-start.31
  6.5 18.3 %copy-start.42 = (f32[4]{0:T(128)S(1)}, f32[4]{0:T(128)}, u32[]{:S(2)}) copy-start(f32[4]{0:T(128)} %param.32) | copy-start | bytes 52
  6.5 19.7 %copy-start.40 = (f32[4,256]{1,0:T(4,128)S(1)}, f32[4,256]{1,0:T(4,128)}, u32[]{:S(2)}) copy-start(f32[4,256]{1,0:T(4,128)} %param.28) | copy-start | bytes 12292
  6.5 19.7 %copy-start.41 = (f32[4,256]{1,0:T(4,128)S(1)}, f32[4,256]{1,0:T(4,128)}, u32[]{:S(2)}) copy-start(f32[4,256]{1,0:T(4,128)} %param.29) | copy-start | bytes 12292
  6.6 19.7 %copy-start.37 = (f32[4,512]{1,0:T(4,128)S(1)}, f32[4,512]{1,0:T(4,128)}, u32[]{:S(2)}) copy-start(f32[4,512]{1,0:T(4,128)} %param.30) | copy-start | bytes 24580
  6.6 38.7 %all-gather.2.cloned.1.call-start = ((), (), s32[]{:S(2)}) async-start(), calls=%async_computation.3 | async-start | bytes 4718592 | tf_op jit(solution)/shard_map/all_gather | solution.py:188
  10.1 305.2 %reduce-scatter.2.cloned.1.call-start = ((), (), s32[]{:S(2)}) async-start(), calls=%async_computation.4 | async-start | bytes 4718592 | tf_op jit(solution)/shard_map/reduce_scatter | solution.py:243
  26.5 22.7 %copy-start.47 = (bf16[2048,256]{1,0:T(8,128)(2,1)S(1)}, bf16[2048,256]{1,0:T(8,128)(2,1)}, u32[]{:S(2)}) copy-start(bf16[2048,256]{1,0:T(8,128)(2,1)} %param.23) | copy-start | bytes 3145732
  45.3 3.9 copy-start.44
  50.8 6.5 %copy-start.46 = (bf16[2048,512]{1,0:T(8,128)(2,1)S(1)}, bf16[2048,512]{1,0:T(8,128)(2,1)}, u32[]{:S(2)}) copy-start(bf16[2048,512]{1,0:T(8,128)(2,1)} %param.26) | copy-start | bytes 6291460
  54.5 6.6 %collective-permute-start = (f32[3,1024]{1,0:T(4,128)S(1)}, f32[3,1024]{1,0:T(4,128)S(1)}, u32[]{:S(2)}, u32[]{:S(2)}) collective-permute-start(f32[3,1024]{1,0:T(4,128)S(1)} %pad_maximum_fusion.8), channel_id=1, source_target_pairs={{0,1},{1,2},{2,3},{3,4},{4,5},{5,6},{6,7},{7,8},{8,9},{9,10},{10,1... | collective-permute-start | bytes 36872 | tf_op jit(solution)/shard_map/ppermute | solution.py:205
  85.6 39.0 %copy-start.1 = (f32[1024,2,2,128]{3,0,2,1:T(8,128)}, f32[1024,2,2,128]{3,0,2,1:T(8,128)S(1)}, u32[]{:S(2)}) copy-start(f32[1024,2,2,128]{3,0,2,1:T(8,128)S(1)} %broadcast_in_dim.66) | copy-start | bytes 6291460
  116.9 7.6 %copy-start.7 = (f32[4,16,64,128]{3,2,1,0:T(8,128)}, f32[4,16,64,128]{3,2,1,0:T(8,128)S(1)}, u32[]{:S(2)}) copy-start(f32[4,16,64,128]{3,2,1,0:T(8,128)S(1)} %fusion.50) | copy-start | bytes 6291460
  124.6 8.6 %copy-start.5 = (f32[4,16,128,128]{2,3,0,1:T(8,128)}, f32[4,16,128,128]{2,3,0,1:T(8,128)S(1)}, u32[]{:S(2)}) copy-start(f32[4,16,128,128]{2,3,0,1:T(8,128)S(1)} %fusion.44) | copy-start | bytes 12582916
  182.6 6.3 %copy-start.21 = (f32[4,1,128,128]{2,3,0,1:T(8,128)S(1)}, f32[4,1,128,128]{2,3,0,1:T(8,128)}, u32[]{:S(2)}) copy-start(f32[4,1,128,128]{2,3,0,1:T(8,128)} %copy.602) | copy-start | bytes 786436
  190.2 5.9 copy-start.18
  193.0 14.9 %collective-permute-start.1 = (f32[4,128,256]{1,2,0:T(8,128)S(1)}, f32[4,128,256]{1,2,0:T(8,128)S(1)}, u32[]{:S(2)}, u32[]{:S(2)}) collective-permute-start(f32[4,128,256]{1,2,0:T(8,128)S(1)} %pad_maximum_fusion.5), channel_id=1, source_target_pairs={{0,1},{1,2},{2,3},{3,4},{4,5},{5,6},{6,7},{7,8},{8,9},{9,10},{10,1... | collective-permute-start | bytes 1572872 | tf_op jit(solution)/shard_map/ppermute | solution.py:92
  209.0 5.2 copy-start.2
  209.1 15.6 %collective-permute-start.2 = (f32[4,128,256]{1,2,0:T(8,128)S(1)}, f32[4,128,256]{1,2,0:T(8,128)S(1)}, u32[]{:S(2)}, u32[]{:S(2)}) collective-permute-start(f32[4,128,256]{1,2,0:T(8,128)S(1)} %pad_maximum_fusion.6), channel_id=1, source_target_pairs={{0,2},{1,3},{2,4},{3,5},{4,6},{5,7},{6,8},{7,9},{8,10},{9,11},{10,... | collective-permute-start | bytes 1572872 | tf_op jit(solution)/shard_map/ppermute | solution.py:92
  224.7 4.2 copy-start.8
  225.8 11.9 %collective-permute-start.3 = (f32[4,128,256]{1,2,0:T(8,128)S(1)}, f32[4,128,256]{1,2,0:T(8,128)S(1)}, u32[]{:S(2)}, u32[]{:S(2)}) collective-permute-start(f32[4,128,256]{1,2,0:T(8,128)S(1)} %pad_maximum_fusion.7), channel_id=1, source_target_pairs={{0,4},{1,5},{2,6},{3,7},{4,8},{5,9},{6,10},{7,11},{8,12},{9,13},{1... | collective-permute-start | bytes 1572872 | tf_op jit(solution)/shard_map/ppermute | solution.py:92
  231.2 13.9 %copy-start.10 = (f32[4,16,64,128]{3,2,1,0:T(8,128)S(1)}, f32[4,16,64,128]{3,2,1,0:T(8,128)}, u32[]{:S(2)}) copy-start(f32[4,16,64,128]{3,2,1,0:T(8,128)} %copy-done.9) | copy-start | bytes 6291460
  238.7 9.7 %copy-start.6 = (f32[4,16,128,128]{2,3,0,1:T(8,128)S(1)}, f32[4,16,128,128]{2,3,0,1:T(8,128)}, u32[]{:S(2)}) copy-start(f32[4,16,128,128]{2,3,0,1:T(8,128)} %copy-done.5) | copy-start | bytes 12582916
  238.8 9.6 %copy-start.4 = (f32[4,16,128,128]{2,3,1,0:T(8,128)S(1)}, f32[4,16,128,128]{2,3,1,0:T(8,128)}, u32[]{:S(2)}) copy-start(f32[4,16,128,128]{2,3,1,0:T(8,128)} %copy-done.3) | copy-start | bytes 12582916
  238.8 9.2 %collective-permute-start.4 = (f32[4,128,128]{1,2,0:T(8,128)S(1)}, f32[4,128,128]{1,2,0:T(8,128)S(1)}, u32[]{:S(2)}, u32[]{:S(2)}) collective-permute-start(f32[4,128,128]{1,2,0:T(8,128)S(1)} %fusion.143), channel_id=1, source_target_pairs={{0,8},{1,9},{2,10},{3,11},{4,12},{5,13},{6,14},{7,15},{16,24},{17,... | collective-permute-start | bytes 786440 | tf_op jit(solution)/shard_map/ppermute | solution.py:89
  280.5 34.7 %copy-start.14 = (bf16[1,128,2048]{2,1,0:T(8,128)(2,1)S(1)}, bf16[1,128,2048]{2,1,0:T(8,128)(2,1)}, u32[]{:S(2)}) copy-start(bf16[1,128,2048]{2,1,0:T(8,128)(2,1)} %param.20) | copy-start | bytes 1572868
  281.3 35.2 %copy-start.36 = (f32[2048]{0:T(1024)S(1)}, f32[2048]{0:T(1024)}, u32[]{:S(2)}) copy-start(f32[2048]{0:T(1024)} %param.22) | copy-start | bytes 24580
  471.0 6.3 %copy-start.39 = (f32[1,128,10]{1,0,2:T(1,128)S(1)}, f32[1,128,10]{1,0,2:T(1,128)}, u32[]{:S(2)}) copy-start(f32[1,128,10]{1,0,2:T(1,128)} %param.36) | copy-start | bytes 15364
  471.0 112.8 %copy-start.19 = (bf16[128,2048]{1,0:T(8,128)(2,1)S(1)}, bf16[128,2048]{1,0:T(8,128)(2,1)}, u32[]{:S(2)}) copy-start(bf16[128,2048]{1,0:T(8,128)(2,1)} %reduce-scatter.2.cloned.1.call-done) | copy-start | bytes 1572868
  471.0 112.8 %all-to-all-start.1 = ((bf16[128,12,2048]{2,1,0:T(8,128)(2,1)}), bf16[128,12,2048]{2,1,0:T(8,128)(2,1)}, u32[]{:S(2)}, u32[]{:S(2)}) async-start(bf16[128,12,2048]{2,1,0:T(8,128)(2,1)} %copy.496), calls=%async_computation.2 | async-start | bytes 16777216 | tf_op jit(solution)/shard_map/all_to_all | solution.py:274
  (25 other events, 43.4 us)
Sparse Core Ops, SparseCore 0:
  10.2 35.0 all-gather.1
  275.9 39.2 reduce-scatter.1

commit v3 on v2

--- a/solution.py
+++ b/solution.py
@@ -76,49 +76,54 @@
     return scale[..., None, None] * jnp.eye(width, dtype=jnp.float32)
 
 
+def tree_compose(step_map, step_shift):
+    maps, shifts = step_map, step_shift
+    while maps.shape[1] > 1:
+        even = maps.shape[1] // 2 * 2
+        late_map = maps[:, 1:even:2]
+        joined_map = mm(late_map, maps[:, 0:even:2])
+        joined_shift = mm(late_map, shifts[:, 0:even:2]) + shifts[:, 1:even:2]
+        if even < maps.shape[1]:
+            joined_map = jnp.concatenate([joined_map, maps[:, even:]], axis=1)
+            joined_shift = jnp.concatenate([joined_shift, shifts[:, even:]], axis=1)
+        maps, shifts = joined_map, joined_shift
+    return maps[:, 0], shifts[:, 0]
+
+
 def segment_entry(seg_map, seg_shift, axis):
-    count, mine = lax.axis_size(axis), lax.axis_index(axis)
+    count = lax.axis_size(axis)
     width = seg_map.shape[-1]
-    excl_map = jnp.broadcast_to(jnp.eye(width, dtype=jnp.float32), seg_map.shape)
-    excl_shift = jnp.zeros_like(seg_shift)
-    reach = 1
-    while reach < count:
-        pairs = [(i, i + reach) for i in range(count - reach)]
-        last = reach * 2 >= count
+    ex_map, ex_shift = None, jnp.zeros_like(seg_shift)
+    inc_map, inc_shift = seg_map, seg_shift
+    stride = 1
+    while stride < count:
+        last = stride * 4 >= count
+        gaps = [k * stride for k in (1, 2, 3) if k * stride < count]
+        got = []
+        for gap in gaps:
+            pairs = [(i, i + gap) for i in range(count - gap)]
+            if last and gap == gaps[-1]:
+                got.append((None, lax.ppermute(inc_shift, axis, pairs)))
+            else:
+                both = lax.ppermute(jnp.concatenate([inc_map, inc_shift], axis=-1), axis, pairs)
+                got.append((both[..., :width], both[..., width:]))
+        t_map, t_shift = got[-1]
+        for g_map, g_shift in reversed(got[:-1]):
+            t_shift = mm(g_map, t_shift) + g_shift
+            if not last:
+                t_map = mm(g_map, t_map)
+        if ex_map is None:
+            new_shift, new_map = t_shift, t_map
+        else:
+            new_shift = mm(ex_map, t_shift) + ex_shift
+            new_map = None if last else mm(ex_map, t_map)
         if last:
-            got_shift = lax.ppermute(seg_shift, axis, pairs)
-            excl_shift = mm(excl_map, got_shift) + excl_shift
-        else:
-            got = lax.ppermute(jnp.concatenate([seg_map, seg_shift], axis=-1), axis, pairs)
-            has = mine >= reach
-            both = mm(jnp.stack([seg_map, excl_map]), got[None])
-            seg_shift = both[0, ..., width:] + seg_shift
-            excl_shift = both[1, ..., width:] + excl_shift
-            excl_map = jnp.where(has, both[1, ..., :width], excl_map)
-            seg_map = jnp.where(has, both[0, ..., :width], seg_map)
-        reach *= 2
-    return excl_shift
-
-
-def tree_compose(step_map, step_shift):
-    width = step_map.shape[-1]
-    maps = [step_map[:, c] for c in range(step_map.shape[1])]
-    shifts = [step_shift[:, c] for c in range(step_shift.shape[1])]
-    while len(maps) > 1:
-        pairs = len(maps) // 2
-        early = jnp.stack(
-            [jnp.concatenate([maps[2 * i], shifts[2 * i]], axis=-1) for i in range(pairs)], axis=1
-        )
-        late_map = jnp.stack([maps[2 * i + 1] for i in range(pairs)], axis=1)
-        late_shift = jnp.stack([shifts[2 * i + 1] for i in range(pairs)], axis=1)
-        joined = mm(late_map, early)
-        new_maps = [joined[:, i, :, :width] for i in range(pairs)]
-        new_shifts = [joined[:, i, :, width:] + late_shift[:, i] for i in range(pairs)]
-        if len(maps) % 2:
-            new_maps.append(maps[-1])
-            new_shifts.append(shifts[-1])
-        maps, shifts = new_maps, new_shifts
-    return maps[0], shifts[0]
+            return new_shift
+        ex_map, ex_shift = new_map, new_shift
+        joined = mm(seg_map, jnp.concatenate([ex_map, ex_shift], axis=-1))
+        inc_map, inc_shift = joined[..., :width], joined[..., width:] + seg_shift
+        stride *= 4
+    return ex_shift
 
 
 def chunk_states_from(entering, step_map, step_shift):
@@ -138,6 +143,14 @@
 def head_spans(values):
     moved = jnp.moveaxis(values, 1, 0)
     return moved.reshape((moved.shape[0], moved.shape[1] // CH, CH) + moved.shape[2:])
+
+
+def exchange_rows(rows):
+    devices, slots, width = rows.shape
+    piece = 512 if width % 512 == 0 else width
+    packed = rows.reshape(devices, slots * width // piece, piece)
+    moved = lax.all_to_all(packed, ("seq", "exp"), split_axis=0, concat_axis=0, tiled=True)
+    return moved.reshape(devices, slots, width)
 
 
 def run_experts(arrived, local_experts, capacity, gate_weight, up_weight, down_weight):
@@ -267,11 +280,11 @@
     outgoing = jnp.einsum(
         "dst,tx->dsx", pick, moe_in, preferred_element_type=jnp.float32
     ).astype(jnp.bfloat16)
-    arrived = lax.all_to_all(outgoing, ("seq", "exp"), split_axis=0, concat_axis=0, tiled=True)
+    arrived = exchange_rows(outgoing)
     answers = run_experts(
         arrived, local_experts, capacity, w_expert_gate, w_expert_up, w_expert_down
     )
-    returned = lax.all_to_all(answers, ("seq", "exp"), split_axis=0, concat_axis=0, tiled=True)
+    returned = exchange_rows(answers)
     gates = route_gates.reshape(local_rows, top_count)
     weight = jnp.sum(
         jnp.where(hits, gates[None, None, :, :], 0.0), axis=-1

time: 615 us -> 556 us (0.904)
  waiting for transfers between devices: 179 us -> 155 us
  blocking collectives: 120 us -> 97.5 us
  local copies, waits for them, and re-layouts: 87.8 us -> 71.9 us
  matrix products: 138 us -> 150 us
  other arithmetic: 38.3 us -> 31 us
    unnamed x128 -> x66, local copies, waits for them, and re-layouts: 44.5 us -> 4.35 us
    all_to_all x1, waiting for transfers between devices: 105 us -> 73.5 us  [exchange_rows(): lax.all_to_all(packed, ('seq', 'exp'), split_axis=0, concat_axis=0, tiled...]
    all_to_all x1, blocking collectives: 107 us -> 84.2 us  [exchange_rows(): lax.all_to_all(packed, ('seq', 'exp'), split_axis=0, concat_axis=0, tiled...]
    all_to_all x1 -> x2, local copies, waits for them, and re-layouts: 6.13 us -> 18.5 us  [exchange_rows(): lax.all_to_all(packed, ('seq', 'exp'), split_axis=0, concat_axis=0, tiled...]
    dot_general x40 -> x48, matrix products: 75.8 us -> 88.2 us  [mm(): return jnp.matmul(a, b, precision=HIGHEST)]
    another operation x3, local copies, waits for them, and re-layouts: 0.78 us -> 9.84 us  [the longest x1 9.07 us: exchange_rows(): packed = rows.reshape(devices, slots * width // piece, piece)]
    convert_element_type x0 -> x1, local copies, waits for them, and re-layouts: none -> 8.64 us  [run_experts(): expert_out = jnp.einsum('pecf,efd->pecd', hidden, down_weight, preferred_...]
    reduce_scatter x1, waiting for transfers between devices: 32.2 us -> 39.5 us  [local(): lax.psum_scatter(jnp.dot(picked, w_out, preferred_element_type=jnp.float3...]
  transfers between devices with their start and end apart: 8 -> 10, of which waited for: 7 -> 7; matrix products, arithmetic and copies ran while one was open for 4% -> 5% of each run, Pallas kernels for 0% -> 0%
where the time goes in v3:
time: 556 us; the launch traced here: 546 us
  waiting for transfers between devices  155 us (28%)
  matrix products  150 us (27%)
  blocking collectives  97.5 us (18%)
  local copies, waits for them, and re-layouts  71.9 us (13%)
  other arithmetic  31 us (6%)
  starting transfers between devices  25.9 us (5%)
  between operations  14.9 us (3%)
    dot_general x48, matrix products, mm(): return jnp.matmul(a, b, precision=HIGHEST)  88.2 us
    all_to_all x1, blocking collectives, exchange_rows(): lax.all_to_all(packed, ('seq', 'exp'), split_axis=0, concat_axis=0, tiled...  84.2 us
    all_to_all x1, waiting for transfers between devices, exchange_rows(): lax.all_to_all(packed, ('seq', 'exp'), split_axis=0, concat_axis=0, tiled...  73.5 us
    reduce_scatter x1, waiting for transfers between devices, local(): lax.psum_scatter(jnp.dot(picked, w_out, preferred_element_type=jnp.float3...  39.5 us
    all_gather x1, waiting for transfers between devices, local(): lax.all_gather(normed, 'seq', axis=0, tiled=True)  18.8 us
    all_to_all x2, local copies, waits for them, and re-layouts, exchange_rows(): lax.all_to_all(packed, ('seq', 'exp'), split_axis=0, concat_axis=0, tiled...  18.5 us
    ppermute x5, starting transfers between devices, segment_entry(): lax.ppermute(jnp.concatenate([inc_map, inc_shift], axis=-1), axis, pairs)  14.4 us
    ppermute x5, waiting for transfers between devices, segment_entry(): lax.ppermute(jnp.concatenate([inc_map, inc_shift], axis=-1), axis, pairs)  13.7 us
  transfers between devices with their start and end apart: 10, of which 7 were waited for; matrix products, arithmetic and copies ran while one was open for 5% of the time, Pallas kernels for 0%

profile of v3, /device:TPU:5, one launch (start us, length us, event | category | flops | bytes accessed | tf_op | source)
XLA Modules:
  0.0 545.7 jit_solution(6371365933915278292)
XLA Ops:
  11.5 13.3 %all_gather.7 = bf16[1024,64]{0,1:T(8,128)(2,1)S(1)} all-gather(bf16[128,64]{0,1:T(8,128)(2,1)S(1)} %convolution_convert_fusion.2), channel_id=1, replica_groups=mesh['seq'=8,'exp'=16] {'seq'}, dimensions={0}, use_global_device_ids=true | all-gather | bytes 147456 | tf_op jit(solution)/shard_map/all_gather | solution.py:202
  26.5 18.8 %all-gather.2.cloned.1.call-done = bf16[1024,2048]{1,0:T(8,128)(2,1)} async-done(((bf16[128,2048]{1,0:T(8,128)(2,1)}), bf16[1024,2048]{1,0:T(8,128)(2,1)}) %all-gather.2.cloned.1.call-update) | async-done | bytes 4194320 | tf_op jit(solution)/shard_map/all_gather | solution.py:201
  45.3 3.9 fusion.145
  57.5 3.8 fusion.156
  65.4 5.6 %divide_multiply_fusion = f32[1024,512]{1,0:T(8,128)} fusion(f32[1024,512]{1,0:T(8,128)} %copy-done.17, f32[3,512]{1,0:T(4,128)S(1)} %slice.369, f32[512]{0:T(512)S(1)} %bitcast.433, f32[512]{0:T(512)S(1)} %bitcast.434, f32[512]{0:T(512)S(1)} %bitcast.432, f32[512]{0:T(512)S(1)} %bitcast.431), kind=kLoop, calls=%fused_computation.57 | loop fusion | flops 7340032 | bytes 4208640 | tf_op jit(solution)/shard_map/jit(silu)/mul | solution.py:28
  70.9 2.9 reshape.177
  79.9 3.6 select_negate_fusion
  111.0 7.8 %fusion.45 = f32[4,16,128,128]{2,3,1,0:T(8,128)S(1)} fusion(f32[4,16,64,128]{3,2,1,0:T(8,128)S(1)} %fusion.40, f32[4,16,64,128]{3,2,1,0:T(8,128)S(1)} %bitcast.414, f32[4,16,64]{2,1,0:T(8,128)S(1)} %get-tuple-element.13), kind=kOutput, calls=%fused_computation.61 | convolution fusion | flops 805830656 | bytes 8404992 | tf_op jit(solution)/shard_map/dot_general | solution.py:37
  118.9 7.8 %multiply_subtract_fusion = f32[4,16,128,128]{3,2,1,0:T(8,128)S(1)} fusion(f32[4,16,64,128]{3,2,1,0:T(8,128)S(1)} %fusion.37, f32[128,128]{1,0:T(8,128)S(1)} %fusion.127, f32[4,16]{1,0:T(4,128)S(1)} %exp.61, f32[4,16,64,128]{3,2,1,0:T(8,128)S(1)} %bitcast.415, f32[4,16,64]{2,1,0:T(8,128)S(1)} %get-tuple-element.13), kind=kOutput, calls=%fused_computation.12 | convolution fusion | flops 807927808 | bytes 8470784 | tf_op jit(solution)/shard_map/dot_general | solution.py:37
  132.0 4.5 copy_add_fusion
  141.6 4.2 collective-permute-start.3
  145.7 3.5 collective-permute-start.2
  159.1 3.6 fusion.42
  167.4 8.3 %collective-permute-done.1 = f32[4,128,256]{1,2,0:T(8,128)} collective-permute-done((f32[4,128,256]{1,2,0:T(8,128)}, f32[4,128,256]{1,2,0:T(8,128)}, u32[]{:S(2)}, u32[]{:S(2)}) %collective-permute-start.1) | collective-permute-done | bytes 524320 | tf_op jit(solution)/shard_map/ppermute | solution.py:108
  189.7 9.0 %collective-permute-done.6 = f32[4,128,128]{1,2,0:T(8,128)S(1)} collective-permute-done((f32[4,128,128]{1,2,0:T(8,128)S(1)}, f32[4,128,128]{1,2,0:T(8,128)S(1)}, u32[]{:S(2)}, u32[]{:S(2)}) %collective-permute-start.6) | collective-permute-done | bytes 262176 | tf_op jit(solution)/shard_map/ppermute | solution.py:106
  199.0 3.6 collective-permute-done.4
  213.4 9.7 %fusion.54 = f32[4,16,64,128]{3,2,1,0:T(8,128)} fusion(f32[4,16,64,128]{3,2,1,0:T(8,128)S(1)} %fusion.154, f32[4,16,128,128]{2,3,0,1:T(8,128)S(1)} %fusion.67, f32[4,16,64,128]{3,2,1,0:T(8,128)S(1)} %fusion.155, f32[4,16,64,128]{3,2,1,0:T(8,128)S(1)} %bitcast.421, f32[4,16,64]{2,1,0:T(8,128)S(1)} %get-tuple-element.11), kind=kOutput, calls=%fused_computation.71 | convolution fusion | flops 806879232 | bytes 12599296 | tf_op jit(solution)/shard_map/dot_general | solution.py:37
  230.6 4.3 convolution_convert_fusion.1
  239.2 39.5 %reduce-scatter.2.cloned.1.call-done = bf16[128,2048]{1,0:T(8,128)(2,1)} async-done(((bf16[1024,2048]{1,0:T(8,128)(2,1)}), bf16[128,2048]{1,0:T(8,128)(2,1)}) %reduce-scatter.2.cloned.1.call-update) | async-done | bytes 524304 | tf_op jit(solution)/shard_map/reduce_scatter | solution.py:256
  280.0 5.5 %convolution_convert_fusion = bf16[128,12,2048]{2,0,1:T(8,128)(2,1)} fusion(pred[128,12,128]{2,0,1:T(8,128)(4,1)S(1)} %compare_reduce_fusion, f32[2048]{0:T(1024)S(1)} %copy-done.19, f32[128]{0:T(128)S(1)} %add_rsqrt_fusion.3, bf16[128,2048]{1,0:T(8,128)(2,1)} %reduce-scatter.2.cloned.1.call-done, bf16[1,128,2048]{2,1,0:T(8,128)(2,1)S(1)} %copy-done.13), kind=kOutput, calls=%fused_computation.4 | convolution fusion | flops 810549248 | bytes 7545344 | tf_op jit(solution)/shard_map/dst,tx->dsx/dot_general | solution.py:280
  285.6 8.6 %copy.343 = bf16[128,12,2048]{0,2,1:T(8,128)(2,1)} copy(bf16[128,12,2048]{2,0,1:T(8,128)(2,1)} %convolution_convert_fusion) | data formatting | bytes 12582912 | tf_op jit(solution)/shard_map/convert_element_type | solution.py:282
  294.2 9.1 %copy.344 = bf16[128,48,512]{2,1,0:T(8,128)(2,1)} copy(bf16[128,48,512]{0,2,1:T(8,128)(2,1)} %bitcast.418) | data formatting | bytes 12582912 | tf_op jit(solution)/shard_map/reshape | solution.py:151
  303.3 84.2 %all_to_all.10 = bf16[128,48,512]{2,1,0:T(8,128)(2,1)} all-to-all(bf16[128,48,512]{2,1,0:T(8,128)(2,1)} %copy.344), channel_id=1, replica_groups=mesh['seq'=8,'exp'=16] {'seq','exp'}, dimensions={0} | all-to-all | bytes 12582912 | tf_op jit(solution)/shard_map/all_to_all | solution.py:152
  387.4 9.2 %copy.345 = bf16[128,48,512]{0,2,1:T(8,128)(2,1)} copy(bf16[128,48,512]{2,1,0:T(8,128)(2,1)} %all_to_all.10) | data formatting | bytes 12582912 | tf_op jit(solution)/shard_map/all_to_all | solution.py:152
  396.7 9.1 %fusion.2 = f32[2,128,6,512]{3,1,2,0:T(8,128)} fusion(bf16[128,2,6,2048]{0,3,2,1:T(8,128)(2,1)} %bitcast.425, bf16[2,2048,512]{2,1,0:T(8,128)(2,1)} %param.38), kind=kOutput, calls=%fused_computation.6 | convolution fusion | flops 3221225472 | bytes 13631488 | tf_op jit(solution)/shard_map/pecd,edf->pecf/dot_general | solution.py:163
  405.8 12.6 %convert_bitcast_fusion = bf16[128,2,6,2048]{3,0,2,1:T(8,128)(2,1)} fusion(bf16[2,512,2048]{2,1,0:T(8,128)(2,1)} %param.39, f32[2,128,6,512]{3,1,2,0:T(8,128)} %fusion.2, bf16[128,2,6,2048]{0,3,2,1:T(8,128)(2,1)} %bitcast.426, bf16[2,2048,512]{2,1,0:T(8,128)(2,1)} %param.37), kind=kOutput, calls=%fused_computation.3 | convolution fusion | flops 6450315264 | bytes 24117248 | tf_op jit(solution)/shard_map/pecf,efd->pecd/dot_general | solution.py:165
  418.4 8.6 %copy.348 = bf16[128,2,6,2048]{0,3,2,1:T(8,128)(2,1)} copy(bf16[128,2,6,2048]{3,0,2,1:T(8,128)(2,1)} %convert_bitcast_fusion) | data formatting | bytes 12582912 | tf_op jit(solution)/shard_map/convert_element_type | solution.py:167
  427.0 9.1 %copy.349 = bf16[128,48,512]{2,1,0:T(8,128)(2,1)} copy(bf16[128,48,512]{0,2,1:T(8,128)(2,1)} %bitcast.419) | data formatting | bytes 12582912 | tf_op jit(solution)/shard_map/reshape;reshape | solution.py:151
  436.1 7.2 %all-to-all-start.1 = ((bf16[128,48,512]{2,1,0:T(8,128)(2,1)}), bf16[128,48,512]{2,1,0:T(8,128)(2,1)}, u32[]{:S(2)}, u32[]{:S(2)}) async-start(bf16[128,48,512]{2,1,0:T(8,128)(2,1)} %copy.349), calls=%async_computation.2 | async-start | bytes 12582912 | tf_op jit(solution)/shard_map/all_to_all | solution.py:152
  445.2 73.5 %all-to-all-done.1 = bf16[128,48,512]{2,1,0:T(8,128)(2,1)} async-done(((bf16[128,48,512]{2,1,0:T(8,128)(2,1)}), bf16[128,48,512]{2,1,0:T(8,128)(2,1)}, u32[]{:S(2)}, u32[]{:S(2)}) %all-to-all-start.1) | async-done | bytes 6291488 | tf_op jit(solution)/shard_map/all_to_all | solution.py:152
  518.7 9.3 %copy.350 = bf16[128,48,512]{0,2,1:T(8,128)(2,1)} copy(bf16[128,48,512]{2,1,0:T(8,128)(2,1)} %all-to-all-done.1) | data formatting | bytes 12582912 | tf_op jit(solution)/shard_map/all_to_all | solution.py:152
  528.0 10.4 %fusion.16 = bf16[1,128,2048]{2,1,0:T(8,128)(2,1)} fusion(f32[128,12,128]{2,0,1:T(8,128)} %fusion, bf16[128,12,2048]{0,2,1:T(8,128)(2,1)} %bitcast.417, bf16[128,2048]{1,0:T(8,128)(2,1)S(1)} %copy-done.14, bf16[1,128,2048]{2,1,0:T(8,128)(2,1)S(1)} %copy-done.13), kind=kOutput, calls=%fused_computation.26 | convolution fusion | flops 4833673216 | bytes 8650752 | tf_op jit(solution)/shard_map/dst,dsx->tx/dot_general | solution.py:292
  (190 shorter events, 116.6 us)
Async XLA Ops:
  6.5 224.0 %copy-start = (bf16[512,2048]{1,0:T(8,128)(2,1)S(1)}, bf16[512,2048]{1,0:T(8,128)(2,1)}, u32[]{:S(2)}) copy-start(bf16[512,2048]{1,0:T(8,128)(2,1)} %param.34) | copy-start | bytes 6291460
  6.5 18.3 %copy-start.25 = (f32[4]{0:T(128)S(1)}, f32[4]{0:T(128)}, u32[]{:S(2)}) copy-start(f32[4]{0:T(128)} %param.32) | copy-start | bytes 52
  6.5 19.7 %copy-start.23 = (f32[4,256]{1,0:T(4,128)S(1)}, f32[4,256]{1,0:T(4,128)}, u32[]{:S(2)}) copy-start(f32[4,256]{1,0:T(4,128)} %param.28) | copy-start | bytes 12292
  6.5 19.7 %copy-start.24 = (f32[4,256]{1,0:T(4,128)S(1)}, f32[4,256]{1,0:T(4,128)}, u32[]{:S(2)}) copy-start(f32[4,256]{1,0:T(4,128)} %param.29) | copy-start | bytes 12292
  6.6 19.7 %copy-start.20 = (f32[4,512]{1,0:T(4,128)S(1)}, f32[4,512]{1,0:T(4,128)}, u32[]{:S(2)}) copy-start(f32[4,512]{1,0:T(4,128)} %param.30) | copy-start | bytes 24580
  6.6 38.7 %all-gather.2.cloned.1.call-start = ((), (), s32[]{:S(2)}) async-start(), calls=%async_computation.3 | async-start | bytes 4718592 | tf_op jit(solution)/shard_map/all_gather | solution.py:201
  10.1 268.6 %reduce-scatter.2.cloned.1.call-start = ((), (), s32[]{:S(2)}) async-start(), calls=%async_computation.4 | async-start | bytes 4718592 | tf_op jit(solution)/shard_map/reduce_scatter | solution.py:256
  45.3 4.1 copy-start.30
  50.9 6.5 %copy-start.29 = (bf16[2048,512]{1,0:T(8,128)(2,1)S(1)}, bf16[2048,512]{1,0:T(8,128)(2,1)}, u32[]{:S(2)}) copy-start(bf16[2048,512]{1,0:T(8,128)(2,1)} %param.26) | copy-start | bytes 6291460
  54.7 6.6 %collective-permute-start = (f32[3,1024]{1,0:T(4,128)S(1)}, f32[3,1024]{1,0:T(4,128)S(1)}, u32[]{:S(2)}, u32[]{:S(2)}) collective-permute-start(f32[3,1024]{1,0:T(4,128)S(1)} %pad_maximum_fusion.5), channel_id=1, source_target_pairs={{0,1},{1,2},{2,3},{3,4},{4,5},{5,6},{6,7},{7,8},{8,9},{9,10},{10,1... | collective-permute-start | bytes 36872 | tf_op jit(solution)/shard_map/ppermute | solution.py:218
  79.9 38.9 %copy-start.2 = (f32[1024,2,2,128]{3,0,2,1:T(8,128)}, f32[1024,2,2,128]{3,0,2,1:T(8,128)S(1)}, u32[]{:S(2)}) copy-start(f32[1024,2,2,128]{3,0,2,1:T(8,128)S(1)} %broadcast_in_dim.63) | copy-start | bytes 6291460
  111.0 7.8 %copy-start.8 = (f32[4,16,64,128]{3,2,1,0:T(8,128)}, f32[4,16,64,128]{3,2,1,0:T(8,128)S(1)}, u32[]{:S(2)}) copy-start(f32[4,16,64,128]{3,2,1,0:T(8,128)S(1)} %fusion.37) | copy-start | bytes 6291460
  118.9 12.6 %copy-start.6 = (f32[4,16,128,128]{2,3,1,0:T(8,128)}, f32[4,16,128,128]{2,3,1,0:T(8,128)S(1)}, u32[]{:S(2)}) copy-start(f32[4,16,128,128]{2,3,1,0:T(8,128)S(1)} %fusion.45) | copy-start | bytes 12582916
  126.7 5.3 copy-start.4
  140.7 11.1 %copy-start.15 = (f32[4,128,128]{1,2,0:T(8,128)}, f32[4,128,128]{1,2,0:T(8,128)S(1)}, u32[]{:S(2)}) copy-start(f32[4,128,128]{1,2,0:T(8,128)S(1)} %fusion.69) | copy-start | bytes 786436
  141.6 21.1 %collective-permute-start.3 = (f32[4,128,256]{1,2,0:T(8,128)}, f32[4,128,256]{1,2,0:T(8,128)}, u32[]{:S(2)}, u32[]{:S(2)}) collective-permute-start(f32[4,128,256]{1,2,0:T(8,128)} %pad_maximum_fusion.3), channel_id=1, source_target_pairs={{0,3},{1,4},{2,5},{3,6},{4,7},{5,8},{6,9},{7,10},{8,11},{9,12},{10... | collective-permute-start | bytes 1572872 | tf_op jit(solution)/shard_map/ppermute | solution.py:108
  145.7 18.8 %collective-permute-start.2 = (f32[4,128,256]{1,2,0:T(8,128)}, f32[4,128,256]{1,2,0:T(8,128)}, u32[]{:S(2)}, u32[]{:S(2)}) collective-permute-start(f32[4,128,256]{1,2,0:T(8,128)} %pad_maximum_fusion.3), channel_id=1, source_target_pairs={{0,2},{1,3},{2,4},{3,5},{4,6},{5,7},{6,8},{7,9},{8,10},{9,11},{10,... | collective-permute-start | bytes 1572872 | tf_op jit(solution)/shard_map/ppermute | solution.py:108
  149.3 26.5 %collective-permute-start.1 = (f32[4,128,256]{1,2,0:T(8,128)}, f32[4,128,256]{1,2,0:T(8,128)}, u32[]{:S(2)}, u32[]{:S(2)}) collective-permute-start(f32[4,128,256]{1,2,0:T(8,128)} %pad_maximum_fusion.3), channel_id=1, source_target_pairs={{0,1},{1,2},{2,3},{3,4},{4,5},{5,6},{6,7},{7,8},{8,9},{9,10},{10,1... | collective-permute-start | bytes 1572872 | tf_op jit(solution)/shard_map/ppermute | solution.py:108
  162.7 16.6 %copy-start.16 = (f32[4,128,128]{1,2,0:T(8,128)S(1)}, f32[4,128,128]{1,2,0:T(8,128)}, u32[]{:S(2)}) copy-start(f32[4,128,128]{1,2,0:T(8,128)} %copy-done.15) | copy-start | bytes 786436
  177.2 4.7 copy-start.9
  179.4 7.9 %copy-start.11 = (f32[4,16,64,128]{3,2,1,0:T(8,128)S(1)}, f32[4,16,64,128]{3,2,1,0:T(8,128)}, u32[]{:S(2)}) copy-start(f32[4,16,64,128]{3,2,1,0:T(8,128)} %copy-done.10) | copy-start | bytes 6291460
  179.4 19.3 %collective-permute-start.5 = (f32[4,128,256]{1,2,0:T(8,128)S(1)}, f32[4,128,256]{1,2,0:T(8,128)S(1)}, u32[]{:S(2)}, u32[]{:S(2)}) collective-permute-start(f32[4,128,256]{1,2,0:T(8,128)S(1)} %pad_maximum_fusion.4), channel_id=1, source_target_pairs={{0,8},{1,9},{2,10},{3,11},{4,12},{5,13},{6,14},{7,15},{16,24},{17,... | collective-permute-start | bytes 1572872 | tf_op jit(solution)/shard_map/ppermute | solution.py:108
  184.2 14.4 %collective-permute-start.6 = (f32[4,128,128]{1,2,0:T(8,128)S(1)}, f32[4,128,128]{1,2,0:T(8,128)S(1)}, u32[]{:S(2)}, u32[]{:S(2)}) collective-permute-start(f32[4,128,128]{1,2,0:T(8,128)S(1)} %get-tuple-element.8), channel_id=1, source_target_pairs={{0,12},{1,13},{2,14},{3,15},{16,28},{17,29},{18,30},{19,31},{32,44... | collective-permute-start | bytes 786440 | tf_op jit(solution)/shard_map/ppermute | solution.py:106
  185.6 17.0 %collective-permute-start.4 = (f32[4,128,256]{1,2,0:T(8,128)S(1)}, f32[4,128,256]{1,2,0:T(8,128)S(1)}, u32[]{:S(2)}, u32[]{:S(2)}) collective-permute-start(f32[4,128,256]{1,2,0:T(8,128)S(1)} %pad_maximum_fusion.4), channel_id=1, source_target_pairs={{0,4},{1,5},{2,6},{3,7},{4,8},{5,9},{6,10},{7,11},{8,12},{9,13},{1... | collective-permute-start | bytes 1572872 | tf_op jit(solution)/shard_map/ppermute | solution.py:108
  187.3 16.1 %copy-start.5 = (f32[4,16,128,128]{3,2,1,0:T(8,128)S(1)}, f32[4,16,128,128]{3,2,1,0:T(8,128)}, u32[]{:S(2)}) copy-start(f32[4,16,128,128]{3,2,1,0:T(8,128)} %copy-done.4) | copy-start | bytes 12582916
  187.3 16.1 %copy-start.7 = (f32[4,16,128,128]{2,3,1,0:T(8,128)S(1)}, f32[4,16,128,128]{2,3,1,0:T(8,128)}, u32[]{:S(2)}) copy-start(f32[4,16,128,128]{2,3,1,0:T(8,128)} %copy-done.6) | copy-start | bytes 12582916
  236.7 42.0 %copy-start.13 = (bf16[1,128,2048]{2,1,0:T(8,128)(2,1)S(1)}, bf16[1,128,2048]{2,1,0:T(8,128)(2,1)}, u32[]{:S(2)}) copy-start(bf16[1,128,2048]{2,1,0:T(8,128)(2,1)} %param.20) | copy-start | bytes 1572868
  237.5 42.5 %copy-start.19 = (f32[2048]{0:T(1024)S(1)}, f32[2048]{0:T(1024)}, u32[]{:S(2)}) copy-start(f32[2048]{0:T(1024)} %param.22) | copy-start | bytes 24580
  436.1 7.2 %copy-start.22 = (f32[1,128,10]{1,0,2:T(1,128)S(1)}, f32[1,128,10]{1,0,2:T(1,128)}, u32[]{:S(2)}) copy-start(f32[1,128,10]{1,0,2:T(1,128)} %param.36) | copy-start | bytes 15364
  436.1 82.6 %all-to-all-start.1 = ((bf16[128,48,512]{2,1,0:T(8,128)(2,1)}), bf16[128,48,512]{2,1,0:T(8,128)(2,1)}, u32[]{:S(2)}, u32[]{:S(2)}) async-start(bf16[128,48,512]{2,1,0:T(8,128)(2,1)} %copy.349), calls=%async_computation.2 | async-start | bytes 12582912 | tf_op jit(solution)/shard_map/all_to_all | solution.py:152
  445.2 82.8 %copy-start.14 = (bf16[128,2048]{1,0:T(8,128)(2,1)S(1)}, bf16[128,2048]{1,0:T(8,128)(2,1)}, u32[]{:S(2)}) copy-start(bf16[128,2048]{1,0:T(8,128)(2,1)} %reduce-scatter.2.cloned.1.call-done) | copy-start | bytes 1572868
  528.0 10.4 %copy-start.1 = (bf16[512,2048]{1,0:T(8,128)(2,1)S(1)}, bf16[512,2048]{1,0:T(8,128)(2,1)}, u32[]{:S(2)}) copy-start(bf16[512,2048]{1,0:T(8,128)(2,1)} %param.34) | copy-start | bytes 6291460
  (10 other events, 23.0 us)
Sparse Core Ops, SparseCore 0:
  10.2 35.0 all-gather.1
  235.1 43.5 reduce-scatter.1

commit v4 on v3

--- a/solution.py
+++ b/solution.py
@@ -145,9 +145,13 @@
     return moved.reshape((moved.shape[0], moved.shape[1] // CH, CH) + moved.shape[2:])
 
 
+def row_piece(width):
+    return 512 if width % 512 == 0 else width
+
+
 def exchange_rows(rows):
     devices, slots, width = rows.shape
-    piece = 512 if width % 512 == 0 else width
+    piece = row_piece(width)
     packed = rows.reshape(devices, slots * width // piece, piece)
     moved = lax.all_to_all(packed, ("seq", "exp"), split_axis=0, concat_axis=0, tiled=True)
     return moved.reshape(devices, slots, width)
@@ -276,11 +280,26 @@
     slot_table = slots.reshape(local_rows, top_count)
     slot_grid = jnp.arange(experts_all * capacity, dtype=jnp.int32).reshape(devices, slot_count)
     hits = slot_table[None, None, :, :] == slot_grid[:, :, None, None]
-    pick = jnp.any(hits, axis=-1).astype(jnp.bfloat16)
-    outgoing = jnp.einsum(
-        "dst,tx->dsx", pick, moe_in, preferred_element_type=jnp.float32
+    piece = row_piece(model_width)
+    split = model_width // piece
+    out_rows = lax.broadcasted_iota(jnp.int32, (devices * slot_count * split, 1), 0)
+    in_cols = lax.broadcasted_iota(jnp.int32, (1, local_rows * split), 1)
+    spread_slots = jnp.repeat(slot_table, split, axis=0)
+    spread_pick = jnp.any(
+        spread_slots[None, :, :] == (out_rows // split)[:, :, None], axis=-1
+    ) & (out_rows % split == in_cols % split)
+    outgoing = jnp.dot(
+        spread_pick.astype(jnp.bfloat16),
+        moe_in.reshape(local_rows * split, piece),
+        preferred_element_type=jnp.float32,
     ).astype(jnp.bfloat16)
-    arrived = exchange_rows(outgoing)
+    arrived = lax.all_to_all(
+        outgoing.reshape(devices, slot_count * split, piece),
+        ("seq", "exp"),
+        split_axis=0,
+        concat_axis=0,
+        tiled=True,
+    ).reshape(devices, slot_count, model_width)
     answers = run_experts(
         arrived, local_experts, capacity, w_expert_gate, w_expert_up, w_expert_down
     )

time: 556 us -> 545 us (0.980)
  local copies, waits for them, and re-layouts: 71.9 us -> 56.8 us
  waiting for transfers between devices: 155 us -> 142 us
  other arithmetic: 31 us -> 41.8 us
    reduce_or x1, other arithmetic: 1 us -> 13.9 us  [local(): jnp.any(spread_slots[None, :, :] == (out_rows // split)[:, :, None], axis...]
    all_to_all x0 -> x1, local copies, waits for them, and re-layouts: none -> 9.36 us  [local(): lax.all_to_all(outgoing.reshape(devices, slot_count * split, piece), ('se...]
    reduce_scatter x1, waiting for transfers between devices: 39.5 us -> 30.1 us  [local(): lax.psum_scatter(jnp.dot(picked, w_out, preferred_element_type=jnp.float3...]
    all_to_all x2 -> x1, local copies, waits for them, and re-layouts: 18.5 us -> 9.25 us  [exchange_rows(): lax.all_to_all(packed, ('seq', 'exp'), split_axis=0, concat_axis=0, tiled...]
    reshape x1, local copies, waits for them, and re-layouts: 9.07 us -> 0.32 us  [local(): moe_in.reshape(local_rows * split, piece)]
    convert_element_type x1 -> x0, local copies, waits for them, and re-layouts: 8.63 us -> none  [local(): outgoing = jnp.einsum('dst,tx->dsx', pick, moe_in, preferred_element_type...]
  transfers between devices with their start and end apart: 10 -> 10, of which waited for: 7 -> 6; matrix products, arithmetic and copies ran while one was open for 5% -> 8% of each run, Pallas kernels for 0% -> 0%
where the time goes in v4:
time: 545 us; the launch traced here: 536 us
  matrix products  155 us (28%)
  waiting for transfers between devices  142 us (26%)
  blocking collectives  97.3 us (18%)
  local copies, waits for them, and re-layouts  56.8 us (10%)
  other arithmetic  41.8 us (8%)
  starting transfers between devices  28.2 us (5%)
  between operations  15 us (3%)
    dot_general x48, matrix products, mm(): return jnp.matmul(a, b, precision=HIGHEST)  93.2 us
    all_to_all x1, blocking collectives, local(): lax.all_to_all(outgoing.reshape(devices, slot_count * split, piece), ('se...  83.9 us
    all_to_all x1, waiting for transfers between devices, exchange_rows(): lax.all_to_all(packed, ('seq', 'exp'), split_axis=0, concat_axis=0, tiled...  73.4 us
    reduce_scatter x1, waiting for transfers between devices, local(): lax.psum_scatter(jnp.dot(picked, w_out, preferred_element_type=jnp.float3...  30.1 us
    all_gather x1, waiting for transfers between devices, local(): lax.all_gather(normed, 'seq', axis=0, tiled=True)  18.8 us
    ppermute x5, starting transfers between devices, segment_entry(): lax.ppermute(jnp.concatenate([inc_map, inc_shift], axis=-1), axis, pairs)  16.8 us
    reduce_or x1, other arithmetic, local(): jnp.any(spread_slots[None, :, :] == (out_rows // split)[:, :, None], axis...  13.9 us
    all_gather x1, blocking collectives, local(): lax.all_gather(rate_logits, 'seq', axis=0, tiled=True)  13.3 us
  transfers between devices with their start and end apart: 10, of which 6 were waited for; matrix products, arithmetic and copies ran while one was open for 8% of the time, Pallas kernels for 0%

profile of v4, /device:TPU:5, one launch (start us, length us, event | category | flops | bytes accessed | tf_op | source)
XLA Modules:
  0.0 536.2 jit_solution(598071488676390369)
XLA Ops:
  11.5 13.3 %all_gather.7 = bf16[1024,64]{0,1:T(8,128)(2,1)S(1)} all-gather(bf16[128,64]{0,1:T(8,128)(2,1)S(1)} %convolution_convert_fusion.1), channel_id=1, replica_groups=mesh['seq'=8,'exp'=16] {'seq'}, dimensions={0}, use_global_device_ids=true | all-gather | bytes 147456 | tf_op jit(solution)/shard_map/all_gather | solution.py:206
  26.5 18.8 %all-gather.2.cloned.1.call-done = bf16[1024,2048]{1,0:T(8,128)(2,1)} async-done(((bf16[128,2048]{1,0:T(8,128)(2,1)}), bf16[1024,2048]{1,0:T(8,128)(2,1)}) %all-gather.2.cloned.1.call-update) | async-done | bytes 4194320 | tf_op jit(solution)/shard_map/all_gather | solution.py:205
  45.3 5.3 fusion.158
  56.7 3.8 fusion.168
  68.8 3.6 select_negate_fusion
  88.9 3.6 fusion.165
  92.5 3.7 fusion.164
  104.4 4.0 convolution_add_fusion
  112.9 7.8 %fusion.52 = f32[4,16,128,128]{2,3,1,0:T(8,128)S(1)} fusion(f32[4,16,64,128]{3,2,1,0:T(8,128)S(1)} %fusion.47, f32[4,16,64,128]{3,2,1,0:T(8,128)S(1)} %bitcast.411, f32[4,16,64]{2,1,0:T(8,128)S(1)} %get-tuple-element.13), kind=kOutput, calls=%fused_computation.65 | convolution fusion | flops 805830656 | bytes 8404992 | tf_op jit(solution)/shard_map/dot_general | solution.py:37
  123.2 7.9 %multiply_subtract_fusion = f32[4,16,128,128]{3,2,1,0:T(8,128)S(1)} fusion(f32[4,16,64,128]{3,2,1,0:T(8,128)S(1)} %fusion.44, f32[128,128]{1,0:T(8,128)S(1)} %fusion.130, f32[4,16]{1,0:T(4,128)S(1)} %exp.61, f32[4,16,64,128]{3,2,1,0:T(8,128)S(1)} %bitcast.412, f32[4,16,64]{2,1,0:T(8,128)S(1)} %get-tuple-element.13), kind=kOutput, calls=%fused_computation.16 | convolution fusion | flops 807927808 | bytes 8470784 | tf_op jit(solution)/shard_map/dot_general | solution.py:37
  134.7 4.5 copy_add_fusion
  145.5 3.4 collective-permute-start.2
  148.9 4.5 collective-permute-start.3
  162.6 3.6 fusion.49
  166.2 7.3 %collective-permute-done.3 = f32[4,128,256]{1,2,0:T(8,128)} collective-permute-done((f32[4,128,256]{1,2,0:T(8,128)}, f32[4,128,256]{1,2,0:T(8,128)}, u32[]{:S(2)}, u32[]{:S(2)}) %collective-permute-start.3) | collective-permute-done | bytes 524320 | tf_op jit(solution)/shard_map/ppermute | solution.py:108
  180.1 4.9 collective-permute-start.5
  193.1 9.2 %collective-permute-done.6 = f32[4,128,128]{1,2,0:T(8,128)S(1)} collective-permute-done((f32[4,128,128]{1,2,0:T(8,128)S(1)}, f32[4,128,128]{1,2,0:T(8,128)S(1)}, u32[]{:S(2)}, u32[]{:S(2)}) %collective-permute-start.6) | collective-permute-done | bytes 262176 | tf_op jit(solution)/shard_map/ppermute | solution.py:106
  216.8 9.8 %fusion.61 = f32[4,16,64,128]{3,2,1,0:T(8,128)} fusion(f32[4,16,64,128]{3,2,1,0:T(8,128)S(1)} %fusion.166, f32[4,16,128,128]{2,3,0,1:T(8,128)S(1)} %fusion.74, f32[4,16,64,128]{3,2,1,0:T(8,128)S(1)} %fusion.167, f32[4,16,64,128]{3,2,1,0:T(8,128)S(1)} %bitcast.417, f32[4,16,64]{2,1,0:T(8,128)S(1)} %get-tuple-element.11), kind=kOutput, calls=%fused_computation.75 | convolution fusion | flops 806879232 | bytes 12599296 | tf_op jit(solution)/shard_map/dot_general | solution.py:37
  234.1 4.4 convolution_convert_fusion
  241.8 13.9 %compare_reduce_fusion = pred[6144,512]{1,0:T(8,128)(4,1)} fusion(s32[512,10]{0,1:T(8,128)S(1)} %copy.435, s32[6144]{0:T(1024)S(1)} %add_select_fusion), kind=kLoop, calls=%fused_computation | loop fusion | flops 59768832 | bytes 3190784 | tf_op jit(solution)/shard_map/reduce_or | solution.py:288
  255.8 30.1 %reduce-scatter.2.cloned.1.call-done = bf16[128,2048]{1,0:T(8,128)(2,1)} async-done(((bf16[1024,2048]{1,0:T(8,128)(2,1)}), bf16[128,2048]{1,0:T(8,128)(2,1)}) %reduce-scatter.2.cloned.1.call-update) | async-done | bytes 524304 | tf_op jit(solution)/shard_map/reduce_scatter | solution.py:260
  288.8 5.2 fusion.3
  293.9 83.9 %all_to_all.10 = bf16[128,48,512]{2,1,0:T(8,128)(2,1)} all-to-all(bf16[128,48,512]{2,1,0:T(8,128)(2,1)S(1)} %bitcast.421), channel_id=1, replica_groups=mesh['seq'=8,'exp'=16] {'seq','exp'}, dimensions={0} | all-to-all | bytes 12582912 | tf_op jit(solution)/shard_map/all_to_all | solution.py:296
  377.9 9.4 %copy.436 = bf16[128,48,512]{0,2,1:T(8,128)(2,1)} copy(bf16[128,48,512]{2,1,0:T(8,128)(2,1)} %all_to_all.10) | data formatting | bytes 12582912 | tf_op jit(solution)/shard_map/all_to_all | solution.py:296
  387.2 9.1 %fusion.9 = f32[2,128,6,512]{3,1,2,0:T(8,128)} fusion(bf16[128,2,6,2048]{0,3,2,1:T(8,128)(2,1)} %bitcast.422, bf16[2,2048,512]{2,1,0:T(8,128)(2,1)} %param.38), kind=kOutput, calls=%fused_computation.10 | convolution fusion | flops 3221225472 | bytes 13631488 | tf_op jit(solution)/shard_map/pecd,edf->pecf/dot_general | solution.py:167
  396.3 12.6 %convert_bitcast_fusion = bf16[128,2,6,2048]{3,0,2,1:T(8,128)(2,1)} fusion(bf16[2,512,2048]{2,1,0:T(8,128)(2,1)} %param.39, f32[2,128,6,512]{3,1,2,0:T(8,128)} %fusion.9, bf16[128,2,6,2048]{0,3,2,1:T(8,128)(2,1)} %bitcast.423, bf16[2,2048,512]{2,1,0:T(8,128)(2,1)} %param.37), kind=kOutput, calls=%fused_computation.6 | convolution fusion | flops 6450315264 | bytes 24117248 | tf_op jit(solution)/shard_map/pecf,efd->pecd/dot_general | solution.py:169
  408.9 8.7 %copy.439 = bf16[128,2,6,2048]{0,3,2,1:T(8,128)(2,1)} copy(bf16[128,2,6,2048]{3,0,2,1:T(8,128)(2,1)} %convert_bitcast_fusion) | data formatting | bytes 12582912 | tf_op jit(solution)/shard_map/convert_element_type | solution.py:171
  417.6 9.1 %copy.440 = bf16[128,48,512]{2,1,0:T(8,128)(2,1)} copy(bf16[128,48,512]{0,2,1:T(8,128)(2,1)} %bitcast.415) | data formatting | bytes 12582912 | tf_op jit(solution)/shard_map/reshape;reshape | solution.py:155
  426.7 7.2 %all-to-all-start.1 = ((bf16[128,48,512]{2,1,0:T(8,128)(2,1)}), bf16[128,48,512]{2,1,0:T(8,128)(2,1)}, u32[]{:S(2)}, u32[]{:S(2)}) async-start(bf16[128,48,512]{2,1,0:T(8,128)(2,1)} %copy.440), calls=%async_computation.2 | async-start | bytes 12582912 | tf_op jit(solution)/shard_map/all_to_all | solution.py:156
  435.9 73.4 %all-to-all-done.1 = bf16[128,48,512]{2,1,0:T(8,128)(2,1)} async-done(((bf16[128,48,512]{2,1,0:T(8,128)(2,1)}), bf16[128,48,512]{2,1,0:T(8,128)(2,1)}, u32[]{:S(2)}, u32[]{:S(2)}) %all-to-all-start.1) | async-done | bytes 6291488 | tf_op jit(solution)/shard_map/all_to_all | solution.py:156
  509.3 9.2 %copy.441 = bf16[128,48,512]{0,2,1:T(8,128)(2,1)} copy(bf16[128,48,512]{2,1,0:T(8,128)(2,1)} %all-to-all-done.1) | data formatting | bytes 12582912 | tf_op jit(solution)/shard_map/all_to_all | solution.py:156
  518.6 10.4 %fusion.23 = bf16[1,128,2048]{2,1,0:T(8,128)(2,1)} fusion(f32[128,12,128]{2,0,1:T(8,128)} %select_reduce_fusion, bf16[128,12,2048]{0,2,1:T(8,128)(2,1)} %bitcast.414, bf16[128,2048]{1,0:T(8,128)(2,1)S(1)} %copy-done.18, bf16[1,128,2048]{2,1,0:T(8,128)(2,1)S(1)} %copy-done.16), kind=kOutput, calls=%fused_computation.30 | convolution fusion | flops 4833673216 | bytes 8650752 | tf_op jit(solution)/shard_map/dst,dsx->tx/dot_general | solution.py:311
  (205 shorter events, 115.6 us)
Async XLA Ops:
  6.5 227.5 %copy-start = (bf16[512,2048]{1,0:T(8,128)(2,1)S(1)}, bf16[512,2048]{1,0:T(8,128)(2,1)}, u32[]{:S(2)}) copy-start(bf16[512,2048]{1,0:T(8,128)(2,1)} %param.34) | copy-start | bytes 6291460
  6.5 18.3 %copy-start.36 = (f32[4]{0:T(128)S(1)}, f32[4]{0:T(128)}, u32[]{:S(2)}) copy-start(f32[4]{0:T(128)} %param.31) | copy-start | bytes 52
  6.5 18.3 %copy-start.30 = (f32[4]{0:T(128)S(1)}, f32[4]{0:T(128)}, u32[]{:S(2)}) copy-start(f32[4]{0:T(128)} %param.32) | copy-start | bytes 52
  6.5 19.7 %copy-start.28 = (f32[4,256]{1,0:T(4,128)S(1)}, f32[4,256]{1,0:T(4,128)}, u32[]{:S(2)}) copy-start(f32[4,256]{1,0:T(4,128)} %param.28) | copy-start | bytes 12292
  6.5 19.7 %copy-start.29 = (f32[4,256]{1,0:T(4,128)S(1)}, f32[4,256]{1,0:T(4,128)}, u32[]{:S(2)}) copy-start(f32[4,256]{1,0:T(4,128)} %param.29) | copy-start | bytes 12292
  6.6 19.7 %copy-start.25 = (f32[4,512]{1,0:T(4,128)S(1)}, f32[4,512]{1,0:T(4,128)}, u32[]{:S(2)}) copy-start(f32[4,512]{1,0:T(4,128)} %param.30) | copy-start | bytes 24580
  6.6 38.7 %all-gather.2.cloned.1.call-start = ((), (), s32[]{:S(2)}) async-start(), calls=%async_computation.3 | async-start | bytes 4718592 | tf_op jit(solution)/shard_map/all_gather | solution.py:205
  10.1 275.8 %reduce-scatter.2.cloned.1.call-start = ((), (), s32[]{:S(2)}) async-start(), calls=%async_computation.4 | async-start | bytes 4718592 | tf_op jit(solution)/shard_map/reduce_scatter | solution.py:260
  45.3 5.4 copy-start.32
  45.3 5.4 %copy-start.34 = (bf16[2048,256]{1,0:T(8,128)(2,1)S(1)}, bf16[2048,256]{1,0:T(8,128)(2,1)}, u32[]{:S(2)}) copy-start(bf16[2048,256]{1,0:T(8,128)(2,1)} %param.23) | copy-start | bytes 3145732
  52.6 4.1 copy-start.33
  53.9 6.6 %collective-permute-start = (f32[3,1024]{1,0:T(4,128)S(1)}, f32[3,1024]{1,0:T(4,128)S(1)}, u32[]{:S(2)}, u32[]{:S(2)}) collective-permute-start(f32[3,1024]{1,0:T(4,128)S(1)} %pad_maximum_fusion.5), channel_id=1, source_target_pairs={{0,1},{1,2},{2,3},{3,4},{4,5},{5,6},{6,7},{7,8},{8,9},{9,10},{10,1... | collective-permute-start | bytes 36872 | tf_op jit(solution)/shard_map/ppermute | solution.py:222
  110.7 12.5 %copy-start.9 = (f32[4,16,64,128]{3,2,1,0:T(8,128)}, f32[4,16,64,128]{3,2,1,0:T(8,128)S(1)}, u32[]{:S(2)}) copy-start(f32[4,16,64,128]{3,2,1,0:T(8,128)S(1)} %fusion.44) | copy-start | bytes 6291460
  112.9 7.8 %copy-start.11 = (f32[4,16,64,128]{3,2,1,0:T(8,128)}, f32[4,16,64,128]{3,2,1,0:T(8,128)S(1)}, u32[]{:S(2)}) copy-start(f32[4,16,64,128]{3,2,1,0:T(8,128)S(1)} %fusion.47) | copy-start | bytes 6291460
  144.0 11.3 %copy-start.19 = (f32[4,128,128]{1,2,0:T(8,128)}, f32[4,128,128]{1,2,0:T(8,128)S(1)}, u32[]{:S(2)}) copy-start(f32[4,128,128]{1,2,0:T(8,128)S(1)} %fusion.124) | copy-start | bytes 786436
  145.5 20.8 %collective-permute-start.2 = (f32[4,128,256]{1,2,0:T(8,128)}, f32[4,128,256]{1,2,0:T(8,128)}, u32[]{:S(2)}, u32[]{:S(2)}) collective-permute-start(f32[4,128,256]{1,2,0:T(8,128)} %pad_maximum_fusion.3), channel_id=1, source_target_pairs={{0,2},{1,3},{2,4},{3,5},{4,6},{5,7},{6,8},{7,9},{8,10},{9,11},{10,... | collective-permute-start | bytes 1572872 | tf_op jit(solution)/shard_map/ppermute | solution.py:108
  148.9 24.7 %collective-permute-start.3 = (f32[4,128,256]{1,2,0:T(8,128)}, f32[4,128,256]{1,2,0:T(8,128)}, u32[]{:S(2)}, u32[]{:S(2)}) collective-permute-start(f32[4,128,256]{1,2,0:T(8,128)} %pad_maximum_fusion.3), channel_id=1, source_target_pairs={{0,3},{1,4},{2,5},{3,6},{4,7},{5,8},{6,9},{7,10},{8,11},{9,12},{10... | collective-permute-start | bytes 1572872 | tf_op jit(solution)/shard_map/ppermute | solution.py:108
  153.4 23.1 %collective-permute-start.1 = (f32[4,128,256]{1,2,0:T(8,128)}, f32[4,128,256]{1,2,0:T(8,128)}, u32[]{:S(2)}, u32[]{:S(2)}) collective-permute-start(f32[4,128,256]{1,2,0:T(8,128)} %pad_maximum_fusion.3), channel_id=1, source_target_pairs={{0,1},{1,2},{2,3},{3,4},{4,5},{5,6},{6,7},{7,8},{8,9},{9,10},{10,1... | collective-permute-start | bytes 1572872 | tf_op jit(solution)/shard_map/ppermute | solution.py:108
  166.2 13.2 %copy-start.20 = (f32[4,128,128]{1,2,0:T(8,128)S(1)}, f32[4,128,128]{1,2,0:T(8,128)}, u32[]{:S(2)}) copy-start(f32[4,128,128]{1,2,0:T(8,128)} %copy-done.19) | copy-start | bytes 786436
  177.8 7.2 %copy-start.10 = (f32[4,16,64,128]{3,2,1,0:T(8,128)S(1)}, f32[4,16,64,128]{3,2,1,0:T(8,128)}, u32[]{:S(2)}) copy-start(f32[4,16,64,128]{3,2,1,0:T(8,128)} %copy-done.9) | copy-start | bytes 6291460
  180.1 10.7 %copy-start.12 = (f32[4,16,64,128]{3,2,1,0:T(8,128)S(1)}, f32[4,16,64,128]{3,2,1,0:T(8,128)}, u32[]{:S(2)}) copy-start(f32[4,16,64,128]{3,2,1,0:T(8,128)} %copy-done.11) | copy-start | bytes 6291460
  180.1 22.2 %collective-permute-start.5 = (f32[4,128,256]{1,2,0:T(8,128)S(1)}, f32[4,128,256]{1,2,0:T(8,128)S(1)}, u32[]{:S(2)}, u32[]{:S(2)}) collective-permute-start(f32[4,128,256]{1,2,0:T(8,128)S(1)} %pad_maximum_fusion.4), channel_id=1, source_target_pairs={{0,8},{1,9},{2,10},{3,11},{4,12},{5,13},{6,14},{7,15},{16,24},{17,... | collective-permute-start | bytes 1572872 | tf_op jit(solution)/shard_map/ppermute | solution.py:108
  187.4 14.9 %collective-permute-start.6 = (f32[4,128,128]{1,2,0:T(8,128)S(1)}, f32[4,128,128]{1,2,0:T(8,128)S(1)}, u32[]{:S(2)}, u32[]{:S(2)}) collective-permute-start(f32[4,128,128]{1,2,0:T(8,128)S(1)} %get-tuple-element.8), channel_id=1, source_target_pairs={{0,12},{1,13},{2,14},{3,15},{16,28},{17,29},{18,30},{19,31},{32,44... | collective-permute-start | bytes 786440 | tf_op jit(solution)/shard_map/ppermute | solution.py:106
  188.7 17.4 %collective-permute-start.4 = (f32[4,128,256]{1,2,0:T(8,128)S(1)}, f32[4,128,256]{1,2,0:T(8,128)S(1)}, u32[]{:S(2)}, u32[]{:S(2)}) collective-permute-start(f32[4,128,256]{1,2,0:T(8,128)S(1)} %pad_maximum_fusion.4), channel_id=1, source_target_pairs={{0,4},{1,5},{2,6},{3,7},{4,8},{5,9},{6,10},{7,11},{8,12},{9,13},{1... | collective-permute-start | bytes 1572872 | tf_op jit(solution)/shard_map/ppermute | solution.py:108
  190.8 16.1 %copy-start.6 = (f32[4,16,128,128]{3,2,1,0:T(8,128)S(1)}, f32[4,16,128,128]{3,2,1,0:T(8,128)}, u32[]{:S(2)}) copy-start(f32[4,16,128,128]{3,2,1,0:T(8,128)} %copy-done.5) | copy-start | bytes 12582916
  190.8 16.1 %copy-start.8 = (f32[4,16,128,128]{2,3,1,0:T(8,128)S(1)}, f32[4,16,128,128]{2,3,1,0:T(8,128)}, u32[]{:S(2)}) copy-start(f32[4,16,128,128]{2,3,1,0:T(8,128)} %copy-done.7) | copy-start | bytes 12582916
  241.5 44.4 %copy-start.16 = (bf16[1,128,2048]{2,1,0:T(8,128)(2,1)S(1)}, bf16[1,128,2048]{2,1,0:T(8,128)(2,1)}, u32[]{:S(2)}) copy-start(bf16[1,128,2048]{2,1,0:T(8,128)(2,1)} %param.20) | copy-start | bytes 1572868
  241.8 45.3 %copy-start.24 = (f32[2048]{0:T(1024)S(1)}, f32[2048]{0:T(1024)}, u32[]{:S(2)}) copy-start(f32[2048]{0:T(1024)} %param.22) | copy-start | bytes 24580
  426.7 7.3 %copy-start.27 = (f32[1,128,10]{1,0,2:T(1,128)S(1)}, f32[1,128,10]{1,0,2:T(1,128)}, u32[]{:S(2)}) copy-start(f32[1,128,10]{1,0,2:T(1,128)} %param.36) | copy-start | bytes 15364
  426.7 82.6 %all-to-all-start.1 = ((bf16[128,48,512]{2,1,0:T(8,128)(2,1)}), bf16[128,48,512]{2,1,0:T(8,128)(2,1)}, u32[]{:S(2)}, u32[]{:S(2)}) async-start(bf16[128,48,512]{2,1,0:T(8,128)(2,1)} %copy.440), calls=%async_computation.2 | async-start | bytes 12582912 | tf_op jit(solution)/shard_map/all_to_all | solution.py:156
  435.9 82.7 %copy-start.18 = (bf16[128,2048]{1,0:T(8,128)(2,1)S(1)}, bf16[128,2048]{1,0:T(8,128)(2,1)}, u32[]{:S(2)}) copy-start(bf16[128,2048]{1,0:T(8,128)(2,1)} %reduce-scatter.2.cloned.1.call-done) | copy-start | bytes 1572868
  518.6 10.4 %copy-start.1 = (bf16[512,2048]{1,0:T(8,128)(2,1)S(1)}, bf16[512,2048]{1,0:T(8,128)(2,1)}, u32[]{:S(2)}) copy-start(bf16[512,2048]{1,0:T(8,128)(2,1)} %param.34) | copy-start | bytes 6291460
  (15 other events, 39.3 us)
Sparse Core Ops, SparseCore 0:
  10.2 35.0 all-gather.1
  238.6 47.2 reduce-scatter.1

commit v5 on v4

--- a/solution.py
+++ b/solution.py
@@ -149,27 +149,31 @@
     return 512 if width % 512 == 0 else width
 
 
-def exchange_rows(rows):
-    devices, slots, width = rows.shape
-    piece = row_piece(width)
-    packed = rows.reshape(devices, slots * width // piece, piece)
-    moved = lax.all_to_all(packed, ("seq", "exp"), split_axis=0, concat_axis=0, tiled=True)
-    return moved.reshape(devices, slots, width)
-
-
-def run_experts(arrived, local_experts, capacity, gate_weight, up_weight, down_weight):
-    peers = arrived.shape[0]
-    model_width = arrived.shape[2]
-    grouped = arrived.reshape(peers, local_experts, capacity, model_width)
+def run_experts(packed, local_experts, capacity, gate_weight, up_weight, down_weight):
+    peers, rows, piece = packed.shape
+    split = rows // (local_experts * capacity)
+    grouped = packed.reshape(peers, local_experts, capacity, split, piece)
+    hidden_width = gate_weight.shape[2]
     gate_part = jnp.einsum(
-        "pecd,edf->pecf", grouped, gate_weight, preferred_element_type=jnp.float32
-    )
-    up_part = jnp.einsum("pecd,edf->pecf", grouped, up_weight, preferred_element_type=jnp.float32)
+        "pecjx,ejxf->pecf",
+        grouped,
+        gate_weight.reshape(local_experts, split, piece, hidden_width),
+        preferred_element_type=jnp.float32,
+    )
+    up_part = jnp.einsum(
+        "pecjx,ejxf->pecf",
+        grouped,
+        up_weight.reshape(local_experts, split, piece, hidden_width),
+        preferred_element_type=jnp.float32,
+    )
     hidden = (jax.nn.silu(gate_part) * up_part).astype(jnp.bfloat16)
     expert_out = jnp.einsum(
-        "pecf,efd->pecd", hidden, down_weight, preferred_element_type=jnp.float32
+        "pecf,efjx->pecjx",
+        hidden,
+        down_weight.reshape(local_experts, hidden_width, split, piece),
+        preferred_element_type=jnp.float32,
     ).astype(jnp.bfloat16)
-    return expert_out.reshape(peers, local_experts * capacity, model_width)
+    return expert_out.reshape(peers, rows, piece)
 
 
 def local(
@@ -299,11 +303,13 @@
         split_axis=0,
         concat_axis=0,
         tiled=True,
-    ).reshape(devices, slot_count, model_width)
+    )
     answers = run_experts(
         arrived, local_experts, capacity, w_expert_gate, w_expert_up, w_expert_down
     )
-    returned = exchange_rows(answers)
+    returned = lax.all_to_all(
+        answers, ("seq", "exp"), split_axis=0, concat_axis=0, tiled=True
+    ).reshape(devices, slot_count, model_width)
     gates = route_gates.reshape(local_rows, top_count)
     weight = jnp.sum(
         jnp.where(hits, gates[None, None, :, :], 0.0), axis=-1

time: 545 us -> 522 us (0.958)
  blocking collectives: 97.3 us -> 13.3 us
  waiting for transfers between devices: 142 us -> 210 us
  starting transfers between devices: 28.2 us -> 37.2 us
  matrix products: 155 us -> 146 us
  local copies, waits for them, and re-layouts: 56.8 us -> 50.3 us
    all_to_all x1 -> x0, blocking collectives: 83.9 us -> none  [local(): lax.all_to_all(outgoing.reshape(devices, slot_count * split, piece), ('se...]
    all_to_all x1 -> x2, waiting for transfers between devices: 73.4 us -> 141 us  [the longest x1 73.6 us: local(): lax.all_to_all(answers, ('seq', 'exp'), split_axis=0, concat_axis=0, tile...]
    reshape x0 -> x2, local copies, waits for them, and re-layouts: none -> 14.1 us  [the longest x1 7.84 us: run_experts(): down_weight.reshape(local_experts, hidden_width, split, piece)]
    dot_general x2 -> x3, matrix products: 21.7 us -> 11.2 us  [the longest x1 3.98 us: run_experts(): jnp.einsum('pecf,efjx->pecjx', hidden, down_weight.reshape(local_experts,...]
    another operation x3 -> x2, local copies, waits for them, and re-layouts: 9.88 us -> 0.77 us  [the longest x1 9.12 us: exchange_rows(): packed = rows.reshape(devices, slots * width // piece, piece)]
    all_to_all x1 -> x2, starting transfers between devices: 7.2 us -> 16.3 us  [the longest x1 11 us: local(): lax.all_to_all(outgoing.reshape(devices, slot_count * split, piece), ('se...]
    convert_element_type x1 -> x0, local copies, waits for them, and re-layouts: 8.66 us -> none  [run_experts(): expert_out = jnp.einsum('pecf,efd->pecd', hidden, down_weight, preferred_...]
  transfers between devices with their start and end apart: 10 -> 11, of which waited for: 6 -> 7; matrix products, arithmetic and copies ran while one was open for 8% -> 10% of each run, Pallas kernels for 0% -> 0%
where the time goes in v5:
time: 522 us; the launch traced here: 514 us
  waiting for transfers between devices  210 us (40%)
  matrix products  146 us (28%)
  local copies, waits for them, and re-layouts  50.3 us (10%)
  other arithmetic  41.8 us (8%)
  starting transfers between devices  37.2 us (7%)
  between operations  15 us (3%)
  blocking collectives  13.3 us (3%)
    dot_general x48, matrix products, mm(): return jnp.matmul(a, b, precision=HIGHEST)  93.1 us
    all_to_all x1, waiting for transfers between devices, local(): lax.all_to_all(answers, ('seq', 'exp'), split_axis=0, concat_axis=0, tile...  73.6 us
    all_to_all x1, waiting for transfers between devices, local(): lax.all_to_all(outgoing.reshape(devices, slot_count * split, piece), ('se...  67.5 us
    reduce_scatter x1, waiting for transfers between devices, local(): lax.psum_scatter(jnp.dot(picked, w_out, preferred_element_type=jnp.float3...  30 us
    all_gather x1, waiting for transfers between devices, local(): lax.all_gather(normed, 'seq', axis=0, tiled=True)  18.8 us
    ppermute x5, starting transfers between devices, segment_entry(): lax.ppermute(jnp.concatenate([inc_map, inc_shift], axis=-1), axis, pairs)  16.8 us
    reduce_or x1, other arithmetic, local(): jnp.any(spread_slots[None, :, :] == (out_rows // split)[:, :, None], axis...  13.9 us
    all_gather x1, blocking collectives, local(): lax.all_gather(rate_logits, 'seq', axis=0, tiled=True)  13.3 us
  transfers between devices with their start and end apart: 11, of which 7 were waited for; matrix products, arithmetic and copies ran while one was open for 10% of the time, Pallas kernels for 0%

profile of v5, /device:TPU:5, one launch (start us, length us, event | category | flops | bytes accessed | tf_op | source)
XLA Modules:
  0.0 513.6 jit_solution(14330253991072809722)
XLA Ops:
  11.5 13.3 %all_gather.7 = bf16[1024,64]{0,1:T(8,128)(2,1)S(1)} all-gather(bf16[128,64]{0,1:T(8,128)(2,1)S(1)} %convolution_convert_fusion.1), channel_id=1, replica_groups=mesh['seq'=8,'exp'=16] {'seq'}, dimensions={0}, use_global_device_ids=true | all-gather | bytes 147456 | tf_op jit(solution)/shard_map/all_gather | solution.py:210
  26.5 18.8 %all-gather.2.cloned.1.call-done = bf16[1024,2048]{1,0:T(8,128)(2,1)} async-done(((bf16[128,2048]{1,0:T(8,128)(2,1)}), bf16[1024,2048]{1,0:T(8,128)(2,1)}) %all-gather.2.cloned.1.call-update) | async-done | bytes 4194320 | tf_op jit(solution)/shard_map/all_gather | solution.py:209
  45.3 5.3 %fusion.153 = f32[1024,512]{1,0:T(8,128)S(1)} fusion(bf16[1024,2048]{1,0:T(8,128)(2,1)} %all-gather.2.cloned.1.call-done, bf16[2048,512]{1,0:T(8,128)(2,1)} %param.25), kind=kOutput, calls=%fused_computation.281 | convolution fusion | flops 2147483648 | bytes 8388608 | tf_op jit(solution)/shard_map/dot_general | solution.py:215
  56.7 3.8 fusion.163
  68.7 3.6 select_negate_fusion
  88.6 3.6 fusion.160
  92.3 3.7 fusion.159
  104.1 4.0 convolution_add_fusion
  112.6 7.8 %fusion.48 = f32[4,16,128,128]{2,3,1,0:T(8,128)S(1)} fusion(f32[4,16,64,128]{3,2,1,0:T(8,128)S(1)} %fusion.45, f32[4,16,64,128]{3,2,1,0:T(8,128)S(1)} %bitcast.412, f32[4,16,64]{2,1,0:T(8,128)S(1)} %get-tuple-element.13), kind=kOutput, calls=%fused_computation.62 | convolution fusion | flops 805830656 | bytes 8404992 | tf_op jit(solution)/shard_map/dot_general | solution.py:37
  123.0 7.8 %multiply_subtract_fusion = f32[4,16,128,128]{3,2,1,0:T(8,128)S(1)} fusion(f32[4,16,64,128]{3,2,1,0:T(8,128)S(1)} %fusion.42, f32[128,128]{1,0:T(8,128)S(1)} %fusion.126, f32[4,16]{1,0:T(4,128)S(1)} %exp.61, f32[4,16,64,128]{3,2,1,0:T(8,128)S(1)} %bitcast.413, f32[4,16,64]{2,1,0:T(8,128)S(1)} %get-tuple-element.13), kind=kOutput, calls=%fused_computation.12 | convolution fusion | flops 807927808 | bytes 8470784 | tf_op jit(solution)/shard_map/dot_general | solution.py:37
  134.4 4.5 copy_add_fusion
  148.6 4.5 collective-permute-start.3
  162.4 3.5 fusion.47
  165.9 7.4 %collective-permute-done.3 = f32[4,128,256]{1,2,0:T(8,128)} collective-permute-done((f32[4,128,256]{1,2,0:T(8,128)}, f32[4,128,256]{1,2,0:T(8,128)}, u32[]{:S(2)}, u32[]{:S(2)}) %collective-permute-start.3) | collective-permute-done | bytes 524320 | tf_op jit(solution)/shard_map/ppermute | solution.py:108
  179.9 4.9 collective-permute-start.5
  192.8 9.2 %collective-permute-done.6 = f32[4,128,128]{1,2,0:T(8,128)S(1)} collective-permute-done((f32[4,128,128]{1,2,0:T(8,128)S(1)}, f32[4,128,128]{1,2,0:T(8,128)S(1)}, u32[]{:S(2)}, u32[]{:S(2)}) %collective-permute-start.6) | collective-permute-done | bytes 262176 | tf_op jit(solution)/shard_map/ppermute | solution.py:106
  216.6 9.8 %fusion.57 = f32[4,16,64,128]{3,2,1,0:T(8,128)} fusion(f32[4,16,64,128]{3,2,1,0:T(8,128)S(1)} %fusion.161, f32[4,16,128,128]{2,3,0,1:T(8,128)S(1)} %fusion.70, f32[4,16,64,128]{3,2,1,0:T(8,128)S(1)} %fusion.162, f32[4,16,64,128]{3,2,1,0:T(8,128)S(1)} %bitcast.417, f32[4,16,64]{2,1,0:T(8,128)S(1)} %get-tuple-element.11), kind=kOutput, calls=%fused_computation.72 | convolution fusion | flops 806879232 | bytes 12599296 | tf_op jit(solution)/shard_map/dot_general | solution.py:37
  233.9 4.4 convolution_convert_fusion
  241.7 13.9 %compare_reduce_fusion = pred[6144,512]{1,0:T(8,128)(4,1)} fusion(s32[512,10]{0,1:T(8,128)S(1)} %copy.433, s32[6144]{0:T(1024)S(1)} %add_select_fusion), kind=kLoop, calls=%fused_computation | loop fusion | flops 59768832 | bytes 3190784 | tf_op jit(solution)/shard_map/reduce_or | solution.py:292
  255.6 30.0 %reduce-scatter.2.cloned.1.call-done = bf16[128,2048]{1,0:T(8,128)(2,1)} async-done(((bf16[1024,2048]{1,0:T(8,128)(2,1)}), bf16[128,2048]{1,0:T(8,128)(2,1)}) %reduce-scatter.2.cloned.1.call-update) | async-done | bytes 524304 | tf_op jit(solution)/shard_map/reduce_scatter | solution.py:264
  288.5 6.8 %fusion.3 = bf16[6144,512]{1,0:T(8,128)(2,1)} fusion(bf16[512,512]{1,0:T(8,128)(2,1)S(1)} %reshape.272, pred[6144,512]{1,0:T(8,128)(4,1)} %compare_reduce_fusion, s32[512]{0:T(512)S(1)} %add_select_fusion.1, s32[6144]{0:T(1024)S(1)} %fusion.127), kind=kOutput, calls=%fused_computation.4 | convolution fusion | flops 3230662656 | bytes 9988096 | tf_op jit(solution)/shard_map/dot_general | solution.py:295
  295.4 11.0 %all-to-all-start = ((bf16[128,48,512]{2,1,0:T(8,128)(2,1)}), bf16[128,48,512]{2,1,0:T(8,128)(2,1)}, u32[]{:S(2)}, u32[]{:S(2)}) async-start(bf16[128,48,512]{2,1,0:T(8,128)(2,1)} %bitcast.421), calls=%async_computation.1 | async-start | bytes 12582912 | tf_op jit(solution)/shard_map/all_to_all | solution.py:300
  306.4 7.8 %reshape.277 = bf16[2,512,4,512]{3,2,1,0:T(4,128)(2,1)} reshape(bf16[2,512,2048]{2,1,0:T(8,128)(2,1)} %param.39) | data formatting | bytes 8388608 | tf_op jit(solution)/shard_map/reshape | solution.py:173
  314.2 67.5 %all-to-all-done = bf16[128,48,512]{2,1,0:T(8,128)(2,1)} async-done(((bf16[128,48,512]{2,1,0:T(8,128)(2,1)}), bf16[128,48,512]{2,1,0:T(8,128)(2,1)}, u32[]{:S(2)}, u32[]{:S(2)}) %all-to-all-start) | async-done | bytes 6291488 | tf_op jit(solution)/shard_map/all_to_all | solution.py:300
  381.7 6.5 %copy.434 = bf16[128,48,512]{2,0,1:T(8,128)(2,1)S(1)} copy(bf16[128,48,512]{2,1,0:T(8,128)(2,1)} %all-to-all-done) | data formatting | bytes 12582912 | tf_op jit(solution)/shard_map/all_to_all | solution.py:300
  391.6 3.8 fusion.15
  395.4 4.0 fusion.12
  399.4 6.3 %copy.436 = bf16[128,48,512]{2,1,0:T(8,128)(2,1)} copy(bf16[128,48,512]{2,0,1:T(8,128)(2,1)S(1)} %bitcast.424) | data formatting | bytes 12582912 | tf_op jit(solution)/shard_map/reshape | solution.py:176
  405.7 5.3 %all-to-all-start.1 = ((bf16[128,48,512]{2,1,0:T(8,128)(2,1)}), bf16[128,48,512]{2,1,0:T(8,128)(2,1)}, u32[]{:S(2)}, u32[]{:S(2)}) async-start(bf16[128,48,512]{2,1,0:T(8,128)(2,1)} %copy.436), calls=%async_computation.2 | async-start | bytes 12582912 | tf_op jit(solution)/shard_map/all_to_all | solution.py:310
  413.0 73.6 %all-to-all-done.1 = bf16[128,48,512]{2,1,0:T(8,128)(2,1)} async-done(((bf16[128,48,512]{2,1,0:T(8,128)(2,1)}), bf16[128,48,512]{2,1,0:T(8,128)(2,1)}, u32[]{:S(2)}, u32[]{:S(2)}) %all-to-all-start.1) | async-done | bytes 6291488 | tf_op jit(solution)/shard_map/all_to_all | solution.py:310
  486.6 9.3 %copy.437 = bf16[128,48,512]{0,2,1:T(8,128)(2,1)} copy(bf16[128,48,512]{2,1,0:T(8,128)(2,1)} %all-to-all-done.1) | data formatting | bytes 12582912 | tf_op jit(solution)/shard_map/all_to_all | solution.py:310
  495.9 10.4 %fusion.21 = bf16[1,128,2048]{2,1,0:T(8,128)(2,1)} fusion(f32[128,12,128]{2,0,1:T(8,128)} %select_reduce_fusion, bf16[128,12,2048]{0,2,1:T(8,128)(2,1)} %bitcast.415, bf16[128,2048]{1,0:T(8,128)(2,1)S(1)} %copy-done.18, bf16[1,128,2048]{2,1,0:T(8,128)(2,1)S(1)} %copy-done.16), kind=kOutput, calls=%fused_computation.27 | convolution fusion | flops 4833673216 | bytes 8650752 | tf_op jit(solution)/shard_map/dst,dsx->tx/dot_general | solution.py:317
  (213 shorter events, 122.2 us)
Async XLA Ops:
  6.5 227.3 %copy-start = (bf16[512,2048]{1,0:T(8,128)(2,1)S(1)}, bf16[512,2048]{1,0:T(8,128)(2,1)}, u32[]{:S(2)}) copy-start(bf16[512,2048]{1,0:T(8,128)(2,1)} %param.34) | copy-start | bytes 6291460
  6.5 18.3 %copy-start.39 = (f32[4]{0:T(128)S(1)}, f32[4]{0:T(128)}, u32[]{:S(2)}) copy-start(f32[4]{0:T(128)} %param.31) | copy-start | bytes 52
  6.5 18.3 %copy-start.31 = (f32[4]{0:T(128)S(1)}, f32[4]{0:T(128)}, u32[]{:S(2)}) copy-start(f32[4]{0:T(128)} %param.32) | copy-start | bytes 52
  6.5 19.7 %copy-start.29 = (f32[4,256]{1,0:T(4,128)S(1)}, f32[4,256]{1,0:T(4,128)}, u32[]{:S(2)}) copy-start(f32[4,256]{1,0:T(4,128)} %param.28) | copy-start | bytes 12292
  6.5 19.7 %copy-start.30 = (f32[4,256]{1,0:T(4,128)S(1)}, f32[4,256]{1,0:T(4,128)}, u32[]{:S(2)}) copy-start(f32[4,256]{1,0:T(4,128)} %param.29) | copy-start | bytes 12292
  6.6 19.7 %copy-start.26 = (f32[4,512]{1,0:T(4,128)S(1)}, f32[4,512]{1,0:T(4,128)}, u32[]{:S(2)}) copy-start(f32[4,512]{1,0:T(4,128)} %param.30) | copy-start | bytes 24580
  6.6 38.7 %all-gather.2.cloned.1.call-start = ((), (), s32[]{:S(2)}) async-start(), calls=%async_computation.3 | async-start | bytes 4718592 | tf_op jit(solution)/shard_map/all_gather | solution.py:209
  10.1 275.6 %reduce-scatter.2.cloned.1.call-start = ((), (), s32[]{:S(2)}) async-start(), calls=%async_computation.4 | async-start | bytes 4718592 | tf_op jit(solution)/shard_map/reduce_scatter | solution.py:264
  45.3 5.4 %copy-start.37 = (bf16[2048,256]{1,0:T(8,128)(2,1)S(1)}, bf16[2048,256]{1,0:T(8,128)(2,1)}, u32[]{:S(2)}) copy-start(bf16[2048,256]{1,0:T(8,128)(2,1)} %param.23) | copy-start | bytes 3145732
  53.9 6.6 %collective-permute-start = (f32[3,1024]{1,0:T(4,128)S(1)}, f32[3,1024]{1,0:T(4,128)S(1)}, u32[]{:S(2)}, u32[]{:S(2)}) collective-permute-start(f32[3,1024]{1,0:T(4,128)S(1)} %pad_maximum_fusion.5), channel_id=1, source_target_pairs={{0,1},{1,2},{2,3},{3,4},{4,5},{5,6},{6,7},{7,8},{8,9},{9,10},{10,1... | collective-permute-start | bytes 36872 | tf_op jit(solution)/shard_map/ppermute | solution.py:226
  110.4 12.6 %copy-start.9 = (f32[4,16,64,128]{3,2,1,0:T(8,128)}, f32[4,16,64,128]{3,2,1,0:T(8,128)S(1)}, u32[]{:S(2)}) copy-start(f32[4,16,64,128]{3,2,1,0:T(8,128)S(1)} %fusion.42) | copy-start | bytes 6291460
  112.6 7.8 %copy-start.11 = (f32[4,16,64,128]{3,2,1,0:T(8,128)}, f32[4,16,64,128]{3,2,1,0:T(8,128)S(1)}, u32[]{:S(2)}) copy-start(f32[4,16,64,128]{3,2,1,0:T(8,128)S(1)} %fusion.45) | copy-start | bytes 6291460
  143.7 11.3 %copy-start.20 = (f32[4,128,128]{1,2,0:T(8,128)}, f32[4,128,128]{1,2,0:T(8,128)S(1)}, u32[]{:S(2)}) copy-start(f32[4,128,128]{1,2,0:T(8,128)S(1)} %fusion.120) | copy-start | bytes 786436
  145.2 20.7 %collective-permute-start.2 = (f32[4,128,256]{1,2,0:T(8,128)}, f32[4,128,256]{1,2,0:T(8,128)}, u32[]{:S(2)}, u32[]{:S(2)}) collective-permute-start(f32[4,128,256]{1,2,0:T(8,128)} %pad_maximum_fusion.3), channel_id=1, source_target_pairs={{0,2},{1,3},{2,4},{3,5},{4,6},{5,7},{6,8},{7,9},{8,10},{9,11},{10,... | collective-permute-start | bytes 1572872 | tf_op jit(solution)/shard_map/ppermute | solution.py:108
  148.6 24.7 %collective-permute-start.3 = (f32[4,128,256]{1,2,0:T(8,128)}, f32[4,128,256]{1,2,0:T(8,128)}, u32[]{:S(2)}, u32[]{:S(2)}) collective-permute-start(f32[4,128,256]{1,2,0:T(8,128)} %pad_maximum_fusion.3), channel_id=1, source_target_pairs={{0,3},{1,4},{2,5},{3,6},{4,7},{5,8},{6,9},{7,10},{8,11},{9,12},{10... | collective-permute-start | bytes 1572872 | tf_op jit(solution)/shard_map/ppermute | solution.py:108
  153.1 23.1 %collective-permute-start.1 = (f32[4,128,256]{1,2,0:T(8,128)}, f32[4,128,256]{1,2,0:T(8,128)}, u32[]{:S(2)}, u32[]{:S(2)}) collective-permute-start(f32[4,128,256]{1,2,0:T(8,128)} %pad_maximum_fusion.3), channel_id=1, source_target_pairs={{0,1},{1,2},{2,3},{3,4},{4,5},{5,6},{6,7},{7,8},{8,9},{9,10},{10,1... | collective-permute-start | bytes 1572872 | tf_op jit(solution)/shard_map/ppermute | solution.py:108
  165.9 13.2 %copy-start.21 = (f32[4,128,128]{1,2,0:T(8,128)S(1)}, f32[4,128,128]{1,2,0:T(8,128)}, u32[]{:S(2)}) copy-start(f32[4,128,128]{1,2,0:T(8,128)} %copy-done.20) | copy-start | bytes 786436
  177.6 7.2 %copy-start.10 = (f32[4,16,64,128]{3,2,1,0:T(8,128)S(1)}, f32[4,16,64,128]{3,2,1,0:T(8,128)}, u32[]{:S(2)}) copy-start(f32[4,16,64,128]{3,2,1,0:T(8,128)} %copy-done.9) | copy-start | bytes 6291460
  179.9 10.6 %copy-start.12 = (f32[4,16,64,128]{3,2,1,0:T(8,128)S(1)}, f32[4,16,64,128]{3,2,1,0:T(8,128)}, u32[]{:S(2)}) copy-start(f32[4,16,64,128]{3,2,1,0:T(8,128)} %copy-done.11) | copy-start | bytes 6291460
  179.9 22.2 %collective-permute-start.5 = (f32[4,128,256]{1,2,0:T(8,128)S(1)}, f32[4,128,256]{1,2,0:T(8,128)S(1)}, u32[]{:S(2)}, u32[]{:S(2)}) collective-permute-start(f32[4,128,256]{1,2,0:T(8,128)S(1)} %pad_maximum_fusion.4), channel_id=1, source_target_pairs={{0,8},{1,9},{2,10},{3,11},{4,12},{5,13},{6,14},{7,15},{16,24},{17,... | collective-permute-start | bytes 1572872 | tf_op jit(solution)/shard_map/ppermute | solution.py:108
  187.2 14.9 %collective-permute-start.6 = (f32[4,128,128]{1,2,0:T(8,128)S(1)}, f32[4,128,128]{1,2,0:T(8,128)S(1)}, u32[]{:S(2)}, u32[]{:S(2)}) collective-permute-start(f32[4,128,128]{1,2,0:T(8,128)S(1)} %get-tuple-element.8), channel_id=1, source_target_pairs={{0,12},{1,13},{2,14},{3,15},{16,28},{17,29},{18,30},{19,31},{32,44... | collective-permute-start | bytes 786440 | tf_op jit(solution)/shard_map/ppermute | solution.py:106
  188.5 17.4 %collective-permute-start.4 = (f32[4,128,256]{1,2,0:T(8,128)S(1)}, f32[4,128,256]{1,2,0:T(8,128)S(1)}, u32[]{:S(2)}, u32[]{:S(2)}) collective-permute-start(f32[4,128,256]{1,2,0:T(8,128)S(1)} %pad_maximum_fusion.4), channel_id=1, source_target_pairs={{0,4},{1,5},{2,6},{3,7},{4,8},{5,9},{6,10},{7,11},{8,12},{9,13},{1... | collective-permute-start | bytes 1572872 | tf_op jit(solution)/shard_map/ppermute | solution.py:108
  190.5 16.1 %copy-start.6 = (f32[4,16,128,128]{3,2,1,0:T(8,128)S(1)}, f32[4,16,128,128]{3,2,1,0:T(8,128)}, u32[]{:S(2)}) copy-start(f32[4,16,128,128]{3,2,1,0:T(8,128)} %copy-done.5) | copy-start | bytes 12582916
  190.5 16.1 %copy-start.8 = (f32[4,16,128,128]{2,3,1,0:T(8,128)S(1)}, f32[4,16,128,128]{2,3,1,0:T(8,128)}, u32[]{:S(2)}) copy-start(f32[4,16,128,128]{2,3,1,0:T(8,128)} %copy-done.7) | copy-start | bytes 12582916
  241.3 44.3 %copy-start.16 = (bf16[1,128,2048]{2,1,0:T(8,128)(2,1)S(1)}, bf16[1,128,2048]{2,1,0:T(8,128)(2,1)}, u32[]{:S(2)}) copy-start(bf16[1,128,2048]{2,1,0:T(8,128)(2,1)} %param.20) | copy-start | bytes 1572868
  241.6 45.3 %copy-start.25 = (f32[2048]{0:T(1024)S(1)}, f32[2048]{0:T(1024)}, u32[]{:S(2)}) copy-start(f32[2048]{0:T(1024)} %param.22) | copy-start | bytes 24580
  295.4 86.3 %all-to-all-start = ((bf16[128,48,512]{2,1,0:T(8,128)(2,1)}), bf16[128,48,512]{2,1,0:T(8,128)(2,1)}, u32[]{:S(2)}, u32[]{:S(2)}) async-start(bf16[128,48,512]{2,1,0:T(8,128)(2,1)} %bitcast.421), calls=%async_computation.1 | async-start | bytes 12582912 | tf_op jit(solution)/shard_map/all_to_all | solution.py:300
  381.7 6.5 %copy-start.33 = (bf16[2,2048,512]{2,1,0:T(8,128)(2,1)S(1)}, bf16[2,2048,512]{2,1,0:T(8,128)(2,1)}, u32[]{:S(2)}) copy-start(bf16[2,2048,512]{2,1,0:T(8,128)(2,1)} %param.38) | copy-start | bytes 12582916
  405.7 5.4 %copy-start.28 = (f32[1,128,10]{1,0,2:T(1,128)S(1)}, f32[1,128,10]{1,0,2:T(1,128)}, u32[]{:S(2)}) copy-start(f32[1,128,10]{1,0,2:T(1,128)} %param.36) | copy-start | bytes 15364
  405.7 80.9 %all-to-all-start.1 = ((bf16[128,48,512]{2,1,0:T(8,128)(2,1)}), bf16[128,48,512]{2,1,0:T(8,128)(2,1)}, u32[]{:S(2)}, u32[]{:S(2)}) async-start(bf16[128,48,512]{2,1,0:T(8,128)(2,1)} %copy.436), calls=%async_computation.2 | async-start | bytes 12582912 | tf_op jit(solution)/shard_map/all_to_all | solution.py:310
  413.0 82.9 %copy-start.18 = (bf16[128,2048]{1,0:T(8,128)(2,1)S(1)}, bf16[128,2048]{1,0:T(8,128)(2,1)}, u32[]{:S(2)}) copy-start(bf16[128,2048]{1,0:T(8,128)(2,1)} %reduce-scatter.2.cloned.1.call-done) | copy-start | bytes 1572868
  495.9 10.4 %copy-start.1 = (bf16[512,2048]{1,0:T(8,128)(2,1)S(1)}, bf16[512,2048]{1,0:T(8,128)(2,1)}, u32[]{:S(2)}) copy-start(bf16[512,2048]{1,0:T(8,128)(2,1)} %param.34) | copy-start | bytes 6291460
  (19 other events, 56.0 us)
Sparse Core Ops, SparseCore 0:
  10.2 35.0 all-gather.1
  238.4 47.1 reduce-scatter.1

commit v6 on v5

--- a/solution.py
+++ b/solution.py
@@ -204,10 +204,9 @@
     local_rows = token_rows.shape[0]
     model_width = token_rows.shape[1]
     normed = scale_rows(token_rows.astype(jnp.float32), in_gain).astype(jnp.bfloat16)
-    rate_logits = jnp.dot(normed, w_rates, preferred_element_type=jnp.float32).astype(jnp.bfloat16)
-    block_rows, block_rates = (
-        lax.all_gather(normed, "seq", axis=0, tiled=True),
-        lax.all_gather(rate_logits, "seq", axis=0, tiled=True),
+    block_rows = lax.all_gather(normed, "seq", axis=0, tiled=True)
+    block_rates = jnp.dot(block_rows, w_rates, preferred_element_type=jnp.float32).astype(
+        jnp.bfloat16
     )
     seg_rows = block_rows.shape[0]
     query_proj = jnp.dot(block_rows, w_query, preferred_element_type=jnp.float32)

time: 522 us -> 529 us (1.013)
  blocking collectives: 13.3 us -> 0 us
  waiting for transfers between devices: 210 us -> 223 us
    all_gather x1, waiting for transfers between devices: 18.8 us -> 35 us  [local(): block_rows = lax.all_gather(normed, 'seq', axis=0, tiled=True)]
    all_gather x1 -> x0, blocking collectives: 13.3 us -> none  [local(): lax.all_gather(rate_logits, 'seq', axis=0, tiled=True)]
  transfers between devices with their start and end apart: 11 -> 11, of which waited for: 7 -> 7; matrix products, arithmetic and copies ran while one was open for 10% -> 11% of each run, Pallas kernels for 0% -> 0%
where the time goes in v6:
time: 529 us; the launch traced here: 520 us
  waiting for transfers between devices  223 us (42%)
  matrix products  149 us (28%)
  local copies, waits for them, and re-layouts  52.4 us (10%)
  other arithmetic  43.3 us (8%)
  starting transfers between devices  37.5 us (7%)
  between operations  15 us (3%)
    dot_general x48, matrix products, mm(): return jnp.matmul(a, b, precision=HIGHEST)  93.1 us
    all_to_all x1, waiting for transfers between devices, local(): lax.all_to_all(answers, ('seq', 'exp'), split_axis=0, concat_axis=0, tile...  73.6 us
    all_to_all x1, waiting for transfers between devices, local(): lax.all_to_all(outgoing.reshape(devices, slot_count * split, piece), ('se...  67.4 us
    all_gather x1, waiting for transfers between devices, local(): block_rows = lax.all_gather(normed, 'seq', axis=0, tiled=True)  35 us
    reduce_scatter x1, waiting for transfers between devices, local(): lax.psum_scatter(jnp.dot(picked, w_out, preferred_element_type=jnp.float3...  27 us
    ppermute x5, starting transfers between devices, segment_entry(): lax.ppermute(jnp.concatenate([inc_map, inc_shift], axis=-1), axis, pairs)  16.8 us
    reduce_or x1, other arithmetic, local(): jnp.any(spread_slots[None, :, :] == (out_rows // split)[:, :, None], axis...  13.9 us
    all_to_all x1, starting transfers between devices, local(): lax.all_to_all(outgoing.reshape(devices, slot_count * split, piece), ('se...  11 us
  transfers between devices with their start and end apart: 11, of which 7 were waited for; matrix products, arithmetic and copies ran while one was open for 11% of the time, Pallas kernels for 0%

profile of v6, /device:TPU:5, one launch (start us, length us, event | category | flops | bytes accessed | tf_op | source)
XLA Modules:
  0.0 520.1 jit_solution(6138019726027626861)
XLA Ops:
  10.3 35.0 %all-gather.2.cloned.1.call-done = bf16[1024,2048]{1,0:T(8,128)(2,1)} async-done(((bf16[128,2048]{1,0:T(8,128)(2,1)}), bf16[1024,2048]{1,0:T(8,128)(2,1)}) %all-gather.2.cloned.1.call-update) | async-done | bytes 4194320 | tf_op jit(solution)/shard_map/all_gather | solution.py:207
  45.3 5.3 %fusion.154 = f32[1024,512]{1,0:T(8,128)S(1)} fusion(bf16[1024,2048]{1,0:T(8,128)(2,1)} %all-gather.2.cloned.1.call-done, bf16[2048,512]{1,0:T(8,128)(2,1)} %param.25), kind=kOutput, calls=%fused_computation.282 | convolution fusion | flops 2147483648 | bytes 8388608 | tf_op jit(solution)/shard_map/dot_general | solution.py:214
  59.6 6.7 %fusion.164 = f32[1024,512]{0,1:T(8,128)} fusion(bf16[1024,2048]{1,0:T(8,128)(2,1)} %all-gather.2.cloned.1.call-done, bf16[2048,512]{1,0:T(8,128)(2,1)} %param.26), kind=kOutput, calls=%fused_computation.292 | convolution fusion | flops 2147483648 | bytes 8388608 | tf_op jit(solution)/shard_map/dot_general | solution.py:215
  74.6 3.6 select_negate_fusion
  94.5 3.6 fusion.161
  98.2 3.7 fusion.160
  110.0 4.0 convolution_add_fusion
  118.5 7.8 %fusion.48 = f32[4,16,128,128]{2,3,1,0:T(8,128)S(1)} fusion(f32[4,16,64,128]{3,2,1,0:T(8,128)S(1)} %fusion.45, f32[4,16,64,128]{3,2,1,0:T(8,128)S(1)} %bitcast.412, f32[4,16,64]{2,1,0:T(8,128)S(1)} %get-tuple-element.13), kind=kOutput, calls=%fused_computation.62 | convolution fusion | flops 805830656 | bytes 8404992 | tf_op jit(solution)/shard_map/dot_general | solution.py:37
  128.8 7.8 %multiply_subtract_fusion = f32[4,16,128,128]{3,2,1,0:T(8,128)S(1)} fusion(f32[4,16,64,128]{3,2,1,0:T(8,128)S(1)} %fusion.42, f32[128,128]{1,0:T(8,128)S(1)} %fusion.127, f32[4,16]{1,0:T(4,128)S(1)} %exp.61, f32[4,16,64,128]{3,2,1,0:T(8,128)S(1)} %bitcast.413, f32[4,16,64]{2,1,0:T(8,128)S(1)} %get-tuple-element.13), kind=kOutput, calls=%fused_computation.12 | convolution fusion | flops 807927808 | bytes 8470784 | tf_op jit(solution)/shard_map/dot_general | solution.py:37
  140.3 4.5 copy_add_fusion
  154.5 4.5 collective-permute-start.3
  168.3 3.5 fusion.47
  171.8 7.4 %collective-permute-done.3 = f32[4,128,256]{1,2,0:T(8,128)} collective-permute-done((f32[4,128,256]{1,2,0:T(8,128)}, f32[4,128,256]{1,2,0:T(8,128)}, u32[]{:S(2)}, u32[]{:S(2)}) %collective-permute-start.3) | collective-permute-done | bytes 524320 | tf_op jit(solution)/shard_map/ppermute | solution.py:108
  185.7 4.9 collective-permute-start.5
  198.7 9.2 %collective-permute-done.6 = f32[4,128,128]{1,2,0:T(8,128)S(1)} collective-permute-done((f32[4,128,128]{1,2,0:T(8,128)S(1)}, f32[4,128,128]{1,2,0:T(8,128)S(1)}, u32[]{:S(2)}, u32[]{:S(2)}) %collective-permute-start.6) | collective-permute-done | bytes 262176 | tf_op jit(solution)/shard_map/ppermute | solution.py:106
  222.5 9.7 %fusion.57 = f32[4,16,64,128]{3,2,1,0:T(8,128)} fusion(f32[4,16,64,128]{3,2,1,0:T(8,128)S(1)} %fusion.162, f32[4,16,128,128]{2,3,0,1:T(8,128)S(1)} %fusion.70, f32[4,16,64,128]{3,2,1,0:T(8,128)S(1)} %fusion.163, f32[4,16,64,128]{3,2,1,0:T(8,128)S(1)} %bitcast.417, f32[4,16,64]{2,1,0:T(8,128)S(1)} %get-tuple-element.11), kind=kOutput, calls=%fused_computation.72 | convolution fusion | flops 806879232 | bytes 12599296 | tf_op jit(solution)/shard_map/dot_general | solution.py:37
  239.7 4.4 convolution_convert_fusion
  250.5 13.9 %compare_reduce_fusion = pred[6144,512]{1,0:T(8,128)(4,1)} fusion(s32[512,10]{0,1:T(8,128)S(1)} %copy.433, s32[6144]{0:T(1024)S(1)} %add_select_fusion), kind=kLoop, calls=%fused_computation | loop fusion | flops 59768832 | bytes 3190784 | tf_op jit(solution)/shard_map/reduce_or | solution.py:291
  264.4 27.0 %reduce-scatter.2.cloned.1.call-done = bf16[128,2048]{1,0:T(8,128)(2,1)} async-done(((bf16[1024,2048]{1,0:T(8,128)(2,1)}), bf16[128,2048]{1,0:T(8,128)(2,1)}) %reduce-scatter.2.cloned.1.call-update) | async-done | bytes 524304 | tf_op jit(solution)/shard_map/reduce_scatter | solution.py:263
  295.1 6.9 %fusion.3 = bf16[6144,512]{1,0:T(8,128)(2,1)} fusion(bf16[512,512]{1,0:T(8,128)(2,1)} %reshape.272, pred[6144,512]{1,0:T(8,128)(4,1)} %compare_reduce_fusion, s32[512]{0:T(512)S(1)} %add_select_fusion.1, s32[6144]{0:T(1024)S(1)} %fusion.128), kind=kOutput, calls=%fused_computation.4 | convolution fusion | flops 3230662656 | bytes 9988096 | tf_op jit(solution)/shard_map/dot_general | solution.py:294
  302.1 11.0 %all-to-all-start = ((bf16[128,48,512]{2,1,0:T(8,128)(2,1)}), bf16[128,48,512]{2,1,0:T(8,128)(2,1)}, u32[]{:S(2)}, u32[]{:S(2)}) async-start(bf16[128,48,512]{2,1,0:T(8,128)(2,1)} %bitcast.421), calls=%async_computation.1 | async-start | bytes 12582912 | tf_op jit(solution)/shard_map/all_to_all | solution.py:299
  313.1 7.9 %reshape.277 = bf16[2,512,4,512]{3,2,1,0:T(4,128)(2,1)} reshape(bf16[2,512,2048]{2,1,0:T(8,128)(2,1)} %param.39) | data formatting | bytes 8388608 | tf_op jit(solution)/shard_map/reshape | solution.py:173
  321.0 67.4 %all-to-all-done = bf16[128,48,512]{2,1,0:T(8,128)(2,1)} async-done(((bf16[128,48,512]{2,1,0:T(8,128)(2,1)}), bf16[128,48,512]{2,1,0:T(8,128)(2,1)}, u32[]{:S(2)}, u32[]{:S(2)}) %all-to-all-start) | async-done | bytes 6291488 | tf_op jit(solution)/shard_map/all_to_all | solution.py:299
  388.4 6.5 %copy.434 = bf16[128,48,512]{2,0,1:T(8,128)(2,1)S(1)} copy(bf16[128,48,512]{2,1,0:T(8,128)(2,1)} %all-to-all-done) | data formatting | bytes 12582912 | tf_op jit(solution)/shard_map/all_to_all | solution.py:299
  394.9 3.4 fusion.165
  398.3 3.8 fusion.15
  402.1 4.0 fusion.12
  406.1 6.3 %copy.436 = bf16[128,48,512]{2,1,0:T(8,128)(2,1)} copy(bf16[128,48,512]{2,0,1:T(8,128)(2,1)S(1)} %bitcast.424) | data formatting | bytes 12582912 | tf_op jit(solution)/shard_map/reshape | solution.py:176
  412.4 5.3 %all-to-all-start.1 = ((bf16[128,48,512]{2,1,0:T(8,128)(2,1)}), bf16[128,48,512]{2,1,0:T(8,128)(2,1)}, u32[]{:S(2)}, u32[]{:S(2)}) async-start(bf16[128,48,512]{2,1,0:T(8,128)(2,1)} %copy.436), calls=%async_computation.2 | async-start | bytes 12582912 | tf_op jit(solution)/shard_map/all_to_all | solution.py:309
  419.8 73.6 %all-to-all-done.1 = bf16[128,48,512]{2,1,0:T(8,128)(2,1)} async-done(((bf16[128,48,512]{2,1,0:T(8,128)(2,1)}), bf16[128,48,512]{2,1,0:T(8,128)(2,1)}, u32[]{:S(2)}, u32[]{:S(2)}) %all-to-all-start.1) | async-done | bytes 6291488 | tf_op jit(solution)/shard_map/all_to_all | solution.py:309
  493.3 9.2 %copy.437 = bf16[128,48,512]{0,2,1:T(8,128)(2,1)} copy(bf16[128,48,512]{2,1,0:T(8,128)(2,1)} %all-to-all-done.1) | data formatting | bytes 12582912 | tf_op jit(solution)/shard_map/all_to_all | solution.py:309
  502.6 10.3 %fusion.21 = bf16[1,128,2048]{2,1,0:T(8,128)(2,1)} fusion(f32[128,12,128]{2,0,1:T(8,128)} %select_reduce_fusion, bf16[128,12,2048]{0,2,1:T(8,128)(2,1)} %bitcast.415, bf16[128,2048]{1,0:T(8,128)(2,1)S(1)} %copy-done.19, bf16[1,128,2048]{2,1,0:T(8,128)(2,1)S(1)} %copy-done.15), kind=kOutput, calls=%fused_computation.27 | convolution fusion | flops 4833673216 | bytes 8650752 | tf_op jit(solution)/shard_map/dst,dsx->tx/dot_general | solution.py:316
  (213 shorter events, 122.7 us)
Async XLA Ops:
  6.5 233.2 %copy-start = (bf16[512,2048]{1,0:T(8,128)(2,1)S(1)}, bf16[512,2048]{1,0:T(8,128)(2,1)}, u32[]{:S(2)}) copy-start(bf16[512,2048]{1,0:T(8,128)(2,1)} %param.34) | copy-start | bytes 6291460
  6.5 38.7 %all-gather.2.cloned.1.call-start = ((), (), s32[]{:S(2)}) async-start(), calls=%async_computation.3 | async-start | bytes 4718592 | tf_op jit(solution)/shard_map/all_gather | solution.py:207
  10.0 281.4 %reduce-scatter.2.cloned.1.call-start = ((), (), s32[]{:S(2)}) async-start(), calls=%async_computation.4 | async-start | bytes 4718592 | tf_op jit(solution)/shard_map/reduce_scatter | solution.py:263
  45.3 5.4 %copy-start.18 = (bf16[1024,2048]{1,0:T(8,128)(2,1)S(1)}, bf16[1024,2048]{1,0:T(8,128)(2,1)}, u32[]{:S(2)}) copy-start(bf16[1024,2048]{1,0:T(8,128)(2,1)} %all-gather.2.cloned.1.call-done) | copy-start | bytes 12582916
  45.3 5.4 %copy-start.38 = (bf16[2048,256]{1,0:T(8,128)(2,1)S(1)}, bf16[2048,256]{1,0:T(8,128)(2,1)}, u32[]{:S(2)}) copy-start(bf16[2048,256]{1,0:T(8,128)(2,1)} %param.23) | copy-start | bytes 3145732
  52.6 4.3 copy-start.27
  53.9 4.4 copy-start.25
  53.9 4.4 copy-start.34
  53.9 12.5 %collective-permute-start = (f32[3,1024]{1,0:T(4,128)S(1)}, f32[3,1024]{1,0:T(4,128)S(1)}, u32[]{:S(2)}, u32[]{:S(2)}) collective-permute-start(f32[3,1024]{1,0:T(4,128)S(1)} %pad_maximum_fusion.5), channel_id=1, source_target_pairs={{0,1},{1,2},{2,3},{3,4},{4,5},{5,6},{6,7},{7,8},{8,9},{9,10},{10,1... | collective-permute-start | bytes 36872 | tf_op jit(solution)/shard_map/ppermute | solution.py:225
  59.6 6.8 %copy-start.26 = (f32[1024,256]{1,0:T(8,128)S(1)}, f32[1024,256]{1,0:T(8,128)}, u32[]{:S(2)}) copy-start(f32[1024,256]{1,0:T(8,128)} %copy-done.25) | copy-start | bytes 3145732
  110.0 4.1 copy-start.2
  116.3 12.5 %copy-start.8 = (f32[4,16,64,128]{3,2,1,0:T(8,128)}, f32[4,16,64,128]{3,2,1,0:T(8,128)S(1)}, u32[]{:S(2)}) copy-start(f32[4,16,64,128]{3,2,1,0:T(8,128)S(1)} %fusion.42) | copy-start | bytes 6291460
  118.5 7.8 %copy-start.10 = (f32[4,16,64,128]{3,2,1,0:T(8,128)}, f32[4,16,64,128]{3,2,1,0:T(8,128)S(1)}, u32[]{:S(2)}) copy-start(f32[4,16,64,128]{3,2,1,0:T(8,128)S(1)} %fusion.45) | copy-start | bytes 6291460
  149.6 11.3 %copy-start.21 = (f32[4,128,128]{1,2,0:T(8,128)}, f32[4,128,128]{1,2,0:T(8,128)S(1)}, u32[]{:S(2)}) copy-start(f32[4,128,128]{1,2,0:T(8,128)S(1)} %fusion.121) | copy-start | bytes 786436
  151.1 20.7 %collective-permute-start.2 = (f32[4,128,256]{1,2,0:T(8,128)}, f32[4,128,256]{1,2,0:T(8,128)}, u32[]{:S(2)}, u32[]{:S(2)}) collective-permute-start(f32[4,128,256]{1,2,0:T(8,128)} %pad_maximum_fusion.3), channel_id=1, source_target_pairs={{0,2},{1,3},{2,4},{3,5},{4,6},{5,7},{6,8},{7,9},{8,10},{9,11},{10,... | collective-permute-start | bytes 1572872 | tf_op jit(solution)/shard_map/ppermute | solution.py:108
  154.5 24.7 %collective-permute-start.3 = (f32[4,128,256]{1,2,0:T(8,128)}, f32[4,128,256]{1,2,0:T(8,128)}, u32[]{:S(2)}, u32[]{:S(2)}) collective-permute-start(f32[4,128,256]{1,2,0:T(8,128)} %pad_maximum_fusion.3), channel_id=1, source_target_pairs={{0,3},{1,4},{2,5},{3,6},{4,7},{5,8},{6,9},{7,10},{8,11},{9,12},{10... | collective-permute-start | bytes 1572872 | tf_op jit(solution)/shard_map/ppermute | solution.py:108
  159.0 23.1 %collective-permute-start.1 = (f32[4,128,256]{1,2,0:T(8,128)}, f32[4,128,256]{1,2,0:T(8,128)}, u32[]{:S(2)}, u32[]{:S(2)}) collective-permute-start(f32[4,128,256]{1,2,0:T(8,128)} %pad_maximum_fusion.3), channel_id=1, source_target_pairs={{0,1},{1,2},{2,3},{3,4},{4,5},{5,6},{6,7},{7,8},{8,9},{9,10},{10,1... | collective-permute-start | bytes 1572872 | tf_op jit(solution)/shard_map/ppermute | solution.py:108
  171.8 13.2 %copy-start.22 = (f32[4,128,128]{1,2,0:T(8,128)S(1)}, f32[4,128,128]{1,2,0:T(8,128)}, u32[]{:S(2)}) copy-start(f32[4,128,128]{1,2,0:T(8,128)} %copy-done.21) | copy-start | bytes 786436
  183.4 7.2 %copy-start.9 = (f32[4,16,64,128]{3,2,1,0:T(8,128)S(1)}, f32[4,16,64,128]{3,2,1,0:T(8,128)}, u32[]{:S(2)}) copy-start(f32[4,16,64,128]{3,2,1,0:T(8,128)} %copy-done.8) | copy-start | bytes 6291460
  185.7 10.7 %copy-start.11 = (f32[4,16,64,128]{3,2,1,0:T(8,128)S(1)}, f32[4,16,64,128]{3,2,1,0:T(8,128)}, u32[]{:S(2)}) copy-start(f32[4,16,64,128]{3,2,1,0:T(8,128)} %copy-done.10) | copy-start | bytes 6291460
  185.7 22.2 %collective-permute-start.5 = (f32[4,128,256]{1,2,0:T(8,128)S(1)}, f32[4,128,256]{1,2,0:T(8,128)S(1)}, u32[]{:S(2)}, u32[]{:S(2)}) collective-permute-start(f32[4,128,256]{1,2,0:T(8,128)S(1)} %pad_maximum_fusion.4), channel_id=1, source_target_pairs={{0,8},{1,9},{2,10},{3,11},{4,12},{5,13},{6,14},{7,15},{16,24},{17,... | collective-permute-start | bytes 1572872 | tf_op jit(solution)/shard_map/ppermute | solution.py:108
  193.0 14.9 %collective-permute-start.6 = (f32[4,128,128]{1,2,0:T(8,128)S(1)}, f32[4,128,128]{1,2,0:T(8,128)S(1)}, u32[]{:S(2)}, u32[]{:S(2)}) collective-permute-start(f32[4,128,128]{1,2,0:T(8,128)S(1)} %get-tuple-element.8), channel_id=1, source_target_pairs={{0,12},{1,13},{2,14},{3,15},{16,28},{17,29},{18,30},{19,31},{32,44... | collective-permute-start | bytes 786440 | tf_op jit(solution)/shard_map/ppermute | solution.py:106
  194.3 17.4 %collective-permute-start.4 = (f32[4,128,256]{1,2,0:T(8,128)S(1)}, f32[4,128,256]{1,2,0:T(8,128)S(1)}, u32[]{:S(2)}, u32[]{:S(2)}) collective-permute-start(f32[4,128,256]{1,2,0:T(8,128)S(1)} %pad_maximum_fusion.4), channel_id=1, source_target_pairs={{0,4},{1,5},{2,6},{3,7},{4,8},{5,9},{6,10},{7,11},{8,12},{9,13},{1... | collective-permute-start | bytes 1572872 | tf_op jit(solution)/shard_map/ppermute | solution.py:108
  196.4 16.1 %copy-start.5 = (f32[4,16,128,128]{3,2,1,0:T(8,128)S(1)}, f32[4,16,128,128]{3,2,1,0:T(8,128)}, u32[]{:S(2)}) copy-start(f32[4,16,128,128]{3,2,1,0:T(8,128)} %copy-done.4) | copy-start | bytes 12582916
  196.4 16.1 %copy-start.7 = (f32[4,16,128,128]{2,3,1,0:T(8,128)S(1)}, f32[4,16,128,128]{2,3,1,0:T(8,128)}, u32[]{:S(2)}) copy-start(f32[4,16,128,128]{2,3,1,0:T(8,128)} %copy-done.6) | copy-start | bytes 12582916
  250.1 41.4 %copy-start.15 = (bf16[1,128,2048]{2,1,0:T(8,128)(2,1)S(1)}, bf16[1,128,2048]{2,1,0:T(8,128)(2,1)}, u32[]{:S(2)}) copy-start(bf16[1,128,2048]{2,1,0:T(8,128)(2,1)} %param.20) | copy-start | bytes 1572868
  250.4 42.3 %copy-start.28 = (f32[2048]{0:T(1024)S(1)}, f32[2048]{0:T(1024)}, u32[]{:S(2)}) copy-start(f32[2048]{0:T(1024)} %param.22) | copy-start | bytes 24580
  302.1 86.3 %all-to-all-start = ((bf16[128,48,512]{2,1,0:T(8,128)(2,1)}), bf16[128,48,512]{2,1,0:T(8,128)(2,1)}, u32[]{:S(2)}, u32[]{:S(2)}) async-start(bf16[128,48,512]{2,1,0:T(8,128)(2,1)} %bitcast.421), calls=%async_computation.1 | async-start | bytes 12582912 | tf_op jit(solution)/shard_map/all_to_all | solution.py:299
  388.4 6.5 %copy-start.36 = (bf16[2,2048,512]{2,1,0:T(8,128)(2,1)S(1)}, bf16[2,2048,512]{2,1,0:T(8,128)(2,1)}, u32[]{:S(2)}) copy-start(bf16[2,2048,512]{2,1,0:T(8,128)(2,1)} %param.38) | copy-start | bytes 12582916
  412.4 5.4 %copy-start.31 = (f32[1,128,10]{1,0,2:T(1,128)S(1)}, f32[1,128,10]{1,0,2:T(1,128)}, u32[]{:S(2)}) copy-start(f32[1,128,10]{1,0,2:T(1,128)} %param.36) | copy-start | bytes 15364
  412.4 80.9 %all-to-all-start.1 = ((bf16[128,48,512]{2,1,0:T(8,128)(2,1)}), bf16[128,48,512]{2,1,0:T(8,128)(2,1)}, u32[]{:S(2)}, u32[]{:S(2)}) async-start(bf16[128,48,512]{2,1,0:T(8,128)(2,1)} %copy.436), calls=%async_computation.2 | async-start | bytes 12582912 | tf_op jit(solution)/shard_map/all_to_all | solution.py:309
  419.8 82.8 %copy-start.19 = (bf16[128,2048]{1,0:T(8,128)(2,1)S(1)}, bf16[128,2048]{1,0:T(8,128)(2,1)}, u32[]{:S(2)}) copy-start(bf16[128,2048]{1,0:T(8,128)(2,1)} %reduce-scatter.2.cloned.1.call-done) | copy-start | bytes 1572868
  (20 other events, 54.8 us)
Sparse Core Ops, SparseCore 0:
  10.1 35.0 all-gather.1
  244.2 47.1 reduce-scatter.1

commit v7 on v5

--- a/solution.py
+++ b/solution.py
@@ -282,8 +282,6 @@
     slots = pair_ids * capacity + places
     slot_count = local_experts * capacity
     slot_table = slots.reshape(local_rows, top_count)
-    slot_grid = jnp.arange(experts_all * capacity, dtype=jnp.int32).reshape(devices, slot_count)
-    hits = slot_table[None, None, :, :] == slot_grid[:, :, None, None]
     piece = row_piece(model_width)
     split = model_width // piece
     out_rows = lax.broadcasted_iota(jnp.int32, (devices * slot_count * split, 1), 0)
@@ -307,16 +305,26 @@
     answers = run_experts(
         arrived, local_experts, capacity, w_expert_gate, w_expert_up, w_expert_down
     )
-    returned = lax.all_to_all(
-        answers, ("seq", "exp"), split_axis=0, concat_axis=0, tiled=True
-    ).reshape(devices, slot_count, model_width)
+    returned = lax.all_to_all(answers, ("seq", "exp"), split_axis=0, concat_axis=0, tiled=True)
     gates = route_gates.reshape(local_rows, top_count)
-    weight = jnp.sum(
-        jnp.where(hits, gates[None, None, :, :], 0.0), axis=-1
-    )
-    moe_sum = jnp.einsum(
-        "dst,dsx->tx", weight, returned.astype(jnp.float32), precision=HIGHEST
-    )
+    sum_rows = lax.broadcasted_iota(jnp.int32, (local_rows * split, 1), 0)
+    sum_cols = lax.broadcasted_iota(jnp.int32, (1, devices * slot_count * split), 1)
+    row_slots = jnp.repeat(slot_table, split, axis=0)
+    row_gates = jnp.repeat(gates, split, axis=0)
+    spread_weight = jnp.sum(
+        jnp.where(row_slots[:, None, :] == (sum_cols // split)[:, :, None], row_gates[:, None, :], 0.0),
+        axis=-1,
+    )
+    spread_weight = jnp.where(sum_rows % split == sum_cols % split, spread_weight, 0.0)
+    weight_hi = spread_weight.astype(jnp.bfloat16)
+    rest = spread_weight - weight_hi.astype(jnp.float32)
+    weight_mid = rest.astype(jnp.bfloat16)
+    weight_lo = (rest - weight_mid.astype(jnp.float32)).astype(jnp.bfloat16)
+    back_rows = returned.reshape(devices * slot_count * split, piece)
+    moe_sum = sum(
+        jnp.dot(part, back_rows, preferred_element_type=jnp.float32)
+        for part in (weight_hi, weight_mid, weight_lo)
+    ).reshape(local_rows, model_width)
     mixed = (residual.astype(jnp.float32) + moe_sum).astype(jnp.bfloat16)
     return mixed.reshape(1, local_rows, model_width)
 

time: 522 us -> 531 us (1.017)
  other arithmetic: 41.8 us -> 62.6 us
  waiting for transfers between devices: 210 us -> 191 us
  matrix products: 146 us -> 157 us
    all_to_all x1, waiting for transfers between devices: 73.6 us -> 54.5 us  [local(): lax.all_to_all(answers, ('seq', 'exp'), split_axis=0, concat_axis=0, tile...]
    reduce_sum x1, other arithmetic: 1.89 us -> 20.5 us  [local(): jnp.sum(jnp.where(row_slots[:, None, :] == (sum_cols // split)[:, :, None...]
    dot_general x1 -> x3, matrix products: 10.4 us -> 22.1 us  [local(): jnp.dot(part, back_rows, preferred_element_type=jnp.float32)]
    all_to_all x1 -> x0, local copies, waits for them, and re-layouts: 9.28 us -> none  [local(): lax.all_to_all(answers, ('seq', 'exp'), split_axis=0, concat_axis=0, tile...]
  transfers between devices with their start and end apart: 11 -> 11, of which waited for: 7 -> 7; matrix products, arithmetic and copies ran while one was open for 10% -> 13% of each run, Pallas kernels for 0% -> 0%
where the time goes in v7:
time: 531 us; the launch traced here: 522 us
  waiting for transfers between devices  191 us (36%)
  matrix products  157 us (30%)
  other arithmetic  62.6 us (12%)
  local copies, waits for them, and re-layouts  45.5 us (9%)
  starting transfers between devices  37.8 us (7%)
  between operations  14.8 us (3%)
  blocking collectives  13.3 us (3%)
    dot_general x48, matrix products, mm(): return jnp.matmul(a, b, precision=HIGHEST)  93 us
    all_to_all x1, waiting for transfers between devices, local(): lax.all_to_all(outgoing.reshape(devices, slot_count * split, piece), ('se...  67.4 us
    all_to_all x1, waiting for transfers between devices, local(): lax.all_to_all(answers, ('seq', 'exp'), split_axis=0, concat_axis=0, tile...  54.5 us
    reduce_scatter x1, waiting for transfers between devices, local(): lax.psum_scatter(jnp.dot(picked, w_out, preferred_element_type=jnp.float3...  29.9 us
    dot_general x3, matrix products, local(): jnp.dot(part, back_rows, preferred_element_type=jnp.float32)  22.1 us
    reduce_sum x1, other arithmetic, local(): jnp.sum(jnp.where(row_slots[:, None, :] == (sum_cols // split)[:, :, None...  20.5 us
    all_gather x1, waiting for transfers between devices, local(): lax.all_gather(normed, 'seq', axis=0, tiled=True)  18.8 us
    ppermute x5, starting transfers between devices, segment_entry(): lax.ppermute(jnp.concatenate([inc_map, inc_shift], axis=-1), axis, pairs)  16.7 us
  transfers between devices with their start and end apart: 11, of which 7 were waited for; matrix products, arithmetic and copies ran while one was open for 13% of the time, Pallas kernels for 0%

profile of v7, /device:TPU:5, one launch (start us, length us, event | category | flops | bytes accessed | tf_op | source)
XLA Modules:
  0.0 522.0 jit_solution(10907645283543139195)
XLA Ops:
  11.5 13.3 %all_gather.7 = bf16[1024,64]{0,1:T(8,128)(2,1)S(1)} all-gather(bf16[128,64]{0,1:T(8,128)(2,1)S(1)} %convolution_convert_fusion.1), channel_id=1, replica_groups=mesh['seq'=8,'exp'=16] {'seq'}, dimensions={0}, use_global_device_ids=true | all-gather | bytes 147456 | tf_op jit(solution)/shard_map/all_gather | solution.py:210
  26.5 18.8 %all-gather.2.cloned.1.call-done = bf16[1024,2048]{1,0:T(8,128)(2,1)} async-done(((bf16[128,2048]{1,0:T(8,128)(2,1)}), bf16[1024,2048]{1,0:T(8,128)(2,1)}) %all-gather.2.cloned.1.call-update) | async-done | bytes 4194320 | tf_op jit(solution)/shard_map/all_gather | solution.py:209
  45.3 5.3 %fusion.169 = f32[1024,512]{1,0:T(8,128)S(1)} fusion(bf16[1024,2048]{1,0:T(8,128)(2,1)} %all-gather.2.cloned.1.call-done, bf16[2048,512]{1,0:T(8,128)(2,1)} %param.25), kind=kOutput, calls=%fused_computation.294 | convolution fusion | flops 2147483648 | bytes 8388608 | tf_op jit(solution)/shard_map/dot_general | solution.py:215
  56.7 3.8 fusion.179
  88.5 3.6 fusion.176
  92.2 3.7 fusion.175
  104.0 4.0 convolution_add_fusion
  112.5 7.8 %fusion.57 = f32[4,16,128,128]{2,3,1,0:T(8,128)S(1)} fusion(f32[4,16,64,128]{3,2,1,0:T(8,128)S(1)} %fusion.54, f32[4,16,64,128]{3,2,1,0:T(8,128)S(1)} %bitcast.404, f32[4,16,64]{2,1,0:T(8,128)S(1)} %get-tuple-element.13), kind=kOutput, calls=%fused_computation.70 | convolution fusion | flops 805830656 | bytes 8404992 | tf_op jit(solution)/shard_map/dot_general | solution.py:37
  122.8 7.9 %multiply_subtract_fusion = f32[4,16,128,128]{3,2,1,0:T(8,128)S(1)} fusion(f32[4,16,64,128]{3,2,1,0:T(8,128)S(1)} %fusion.51, f32[128,128]{1,0:T(8,128)S(1)} %fusion.141, f32[4,16]{1,0:T(4,128)S(1)} %exp.61, f32[4,16,64,128]{3,2,1,0:T(8,128)S(1)} %bitcast.405, f32[4,16,64]{2,1,0:T(8,128)S(1)} %get-tuple-element.13), kind=kOutput, calls=%fused_computation.23 | convolution fusion | flops 807927808 | bytes 8470784 | tf_op jit(solution)/shard_map/dot_general | solution.py:37
  134.3 4.5 copy_add_fusion
  148.5 4.5 collective-permute-start.3
  165.8 7.4 %collective-permute-done.3 = f32[4,128,256]{1,2,0:T(8,128)} collective-permute-done((f32[4,128,256]{1,2,0:T(8,128)}, f32[4,128,256]{1,2,0:T(8,128)}, u32[]{:S(2)}, u32[]{:S(2)}) %collective-permute-start.3) | collective-permute-done | bytes 524320 | tf_op jit(solution)/shard_map/ppermute | solution.py:108
  179.7 5.0 collective-permute-start.5
  192.7 9.2 %collective-permute-done.6 = f32[4,128,128]{1,2,0:T(8,128)S(1)} collective-permute-done((f32[4,128,128]{1,2,0:T(8,128)S(1)}, f32[4,128,128]{1,2,0:T(8,128)S(1)}, u32[]{:S(2)}, u32[]{:S(2)}) %collective-permute-start.6) | collective-permute-done | bytes 262176 | tf_op jit(solution)/shard_map/ppermute | solution.py:106
  216.6 9.8 %fusion.66 = f32[4,16,64,128]{3,2,1,0:T(8,128)} fusion(f32[4,16,64,128]{3,2,1,0:T(8,128)S(1)} %fusion.177, f32[4,16,128,128]{2,3,0,1:T(8,128)S(1)} %fusion.83, f32[4,16,64,128]{3,2,1,0:T(8,128)S(1)} %fusion.178, f32[4,16,64,128]{3,2,1,0:T(8,128)S(1)} %bitcast.408, f32[4,16,64]{2,1,0:T(8,128)S(1)} %get-tuple-element.11), kind=kOutput, calls=%fused_computation.80 | convolution fusion | flops 806879232 | bytes 12599296 | tf_op jit(solution)/shard_map/dot_general | solution.py:37
  233.8 4.4 convolution_convert_fusion
  241.6 13.9 %compare_reduce_fusion = pred[6144,512]{1,0:T(8,128)(4,1)} fusion(s32[512,10]{0,1:T(8,128)S(1)} %copy.337, s32[6144]{0:T(1024)S(1)} %add_select_fusion), kind=kLoop, calls=%fused_computation.1 | loop fusion | flops 59768832 | bytes 3190784 | tf_op jit(solution)/shard_map/reduce_or | solution.py:290
  255.5 29.9 %reduce-scatter.2.cloned.1.call-done = bf16[128,2048]{1,0:T(8,128)(2,1)} async-done(((bf16[1024,2048]{1,0:T(8,128)(2,1)}), bf16[128,2048]{1,0:T(8,128)(2,1)}) %reduce-scatter.2.cloned.1.call-update) | async-done | bytes 524304 | tf_op jit(solution)/shard_map/reduce_scatter | solution.py:264
  288.3 6.8 %fusion.4 = bf16[6144,512]{1,0:T(8,128)(2,1)} fusion(bf16[512,512]{1,0:T(8,128)(2,1)S(1)} %reshape.328, pred[6144,512]{1,0:T(8,128)(4,1)} %compare_reduce_fusion, s32[512]{0:T(512)S(1)} %add_select_fusion.2, s32[6144]{0:T(1024)S(1)} %add_select_fusion.1), kind=kOutput, calls=%fused_computation.9 | convolution fusion | flops 3230662656 | bytes 9988096 | tf_op jit(solution)/shard_map/dot_general | solution.py:293
  295.2 11.1 %all-to-all-start = ((bf16[128,48,512]{2,1,0:T(8,128)(2,1)}), bf16[128,48,512]{2,1,0:T(8,128)(2,1)}, u32[]{:S(2)}, u32[]{:S(2)}) async-start(bf16[128,48,512]{2,1,0:T(8,128)(2,1)} %bitcast.412), calls=%async_computation.1 | async-start | bytes 12582912 | tf_op jit(solution)/shard_map/all_to_all | solution.py:298
  306.3 7.9 %reshape.333 = bf16[2,512,4,512]{3,2,1,0:T(4,128)(2,1)} reshape(bf16[2,512,2048]{2,1,0:T(8,128)(2,1)} %param.39) | data formatting | bytes 8388608 | tf_op jit(solution)/shard_map/reshape | solution.py:173
  314.2 67.4 %all-to-all-done = bf16[128,48,512]{2,1,0:T(8,128)(2,1)} async-done(((bf16[128,48,512]{2,1,0:T(8,128)(2,1)}), bf16[128,48,512]{2,1,0:T(8,128)(2,1)}, u32[]{:S(2)}, u32[]{:S(2)}) %all-to-all-start) | async-done | bytes 6291488 | tf_op jit(solution)/shard_map/all_to_all | solution.py:298
  381.6 6.5 %copy.341 = bf16[128,48,512]{2,0,1:T(8,128)(2,1)S(1)} copy(bf16[128,48,512]{2,1,0:T(8,128)(2,1)} %all-to-all-done) | data formatting | bytes 12582912 | tf_op jit(solution)/shard_map/all_to_all | solution.py:298
  391.6 3.8 fusion.24
  395.4 3.7 fusion.21
  399.1 6.3 %copy.343 = bf16[128,48,512]{2,1,0:T(8,128)(2,1)} copy(bf16[128,48,512]{2,0,1:T(8,128)(2,1)S(1)} %bitcast.415) | data formatting | bytes 12582912 | tf_op jit(solution)/shard_map/reshape | solution.py:176
  405.4 5.7 %all-to-all-start.1 = ((bf16[128,48,512]{2,1,0:T(8,128)(2,1)}), bf16[128,48,512]{2,1,0:T(8,128)(2,1)}, u32[]{:S(2)}, u32[]{:S(2)}) async-start(bf16[128,48,512]{2,1,0:T(8,128)(2,1)} %copy.343), calls=%async_computation.2 | async-start | bytes 12582912 | tf_op jit(solution)/shard_map/all_to_all | solution.py:308
  411.4 20.5 %select_reduce_fusion = f32[512,6144]{1,0:T(8,128)} fusion(f32[512,10]{0,1:T(8,128)S(1)} %copy.339, s32[6144]{0:T(1024)S(1)} %add_select_fusion, s32[512,10]{0,1:T(8,128)S(1)} %copy.337), kind=kLoop, calls=%fused_computation | loop fusion | flops 91226112 | bytes 12648448 | tf_op jit(solution)/shard_map/reduce_sum | solution.py:314
  431.9 54.5 %all-to-all-done.1 = bf16[128,48,512]{2,1,0:T(8,128)(2,1)} async-done(((bf16[128,48,512]{2,1,0:T(8,128)(2,1)}), bf16[128,48,512]{2,1,0:T(8,128)(2,1)}, u32[]{:S(2)}, u32[]{:S(2)}) %all-to-all-start.1) | async-done | bytes 6291488 | tf_op jit(solution)/shard_map/all_to_all | solution.py:308
  486.4 8.5 %fusion.7 = f32[512,512]{1,0:T(8,128)S(1)} fusion(bf16[6144,512]{1,0:T(8,128)(2,1)} %bitcast.110, f32[512,6144]{1,0:T(8,128)} %select_reduce_fusion, s32[6144]{0:T(1024)S(1)} %add_select_fusion.1, s32[512]{0:T(512)S(1)} %add_select_fusion.2), kind=kOutput, calls=%fused_computation.10 | convolution fusion | flops 3227516928 | bytes 19949568 | tf_op jit(solution)/shard_map/dot_general | solution.py:325
  496.4 6.2 %fusion.79 = f32[512,512]{1,0:T(8,128)S(1)} fusion(f32[512,512]{1,0:T(8,128)S(1)} %fusion.7, bf16[6144,512]{1,0:T(8,128)(2,1)} %bitcast.110, f32[512,6144]{1,0:T(8,128)S(1)} %copy-done.17, s32[6144]{0:T(1024)S(1)} %add_select_fusion.1, s32[512]{0:T(512)S(1)} %add_select_fusion.2), kind=kOutput, calls=%fused_computation.98 | convolution fusion | flops 3240361984 | bytes 20998144 | tf_op jit(solution)/shard_map/dot_general | solution.py:325
  502.7 7.4 %fusion.78 = f32[512,512]{1,0:T(8,128)} fusion(f32[512,512]{1,0:T(8,128)S(1)} %fusion.79, bf16[6144,512]{1,0:T(8,128)(2,1)} %bitcast.110, f32[512,6144]{1,0:T(8,128)S(1)} %copy-done.17, s32[6144]{0:T(1024)S(1)} %add_select_fusion.1, s32[512]{0:T(512)S(1)} %add_select_fusion.2), kind=kOutput, calls=%fused_computation.97 | convolution fusion | flops 3249799168 | bytes 20998144 | tf_op jit(solution)/shard_map/dot_general | solution.py:325
  (218 shorter events, 134.0 us)
Async XLA Ops:
  6.5 227.3 %copy-start = (bf16[512,2048]{1,0:T(8,128)(2,1)S(1)}, bf16[512,2048]{1,0:T(8,128)(2,1)}, u32[]{:S(2)}) copy-start(bf16[512,2048]{1,0:T(8,128)(2,1)} %param.34) | copy-start | bytes 6291460
  6.5 18.3 %copy-start.40 = (f32[4]{0:T(128)S(1)}, f32[4]{0:T(128)}, u32[]{:S(2)}) copy-start(f32[4]{0:T(128)} %param.31) | copy-start | bytes 52
  6.5 18.3 %copy-start.32 = (f32[4]{0:T(128)S(1)}, f32[4]{0:T(128)}, u32[]{:S(2)}) copy-start(f32[4]{0:T(128)} %param.32) | copy-start | bytes 52
  6.5 19.7 %copy-start.30 = (f32[4,256]{1,0:T(4,128)S(1)}, f32[4,256]{1,0:T(4,128)}, u32[]{:S(2)}) copy-start(f32[4,256]{1,0:T(4,128)} %param.28) | copy-start | bytes 12292
  6.5 19.7 %copy-start.31 = (f32[4,256]{1,0:T(4,128)S(1)}, f32[4,256]{1,0:T(4,128)}, u32[]{:S(2)}) copy-start(f32[4,256]{1,0:T(4,128)} %param.29) | copy-start | bytes 12292
  6.6 19.7 %copy-start.27 = (f32[4,512]{1,0:T(4,128)S(1)}, f32[4,512]{1,0:T(4,128)}, u32[]{:S(2)}) copy-start(f32[4,512]{1,0:T(4,128)} %param.30) | copy-start | bytes 24580
  6.6 38.7 %all-gather.2.cloned.1.call-start = ((), (), s32[]{:S(2)}) async-start(), calls=%async_computation.3 | async-start | bytes 4718592 | tf_op jit(solution)/shard_map/all_gather | solution.py:209
  10.1 275.4 %reduce-scatter.2.cloned.1.call-start = ((), (), s32[]{:S(2)}) async-start(), calls=%async_computation.4 | async-start | bytes 4718592 | tf_op jit(solution)/shard_map/reduce_scatter | solution.py:264
  45.3 5.4 %copy-start.38 = (bf16[2048,256]{1,0:T(8,128)(2,1)S(1)}, bf16[2048,256]{1,0:T(8,128)(2,1)}, u32[]{:S(2)}) copy-start(bf16[2048,256]{1,0:T(8,128)(2,1)} %param.23) | copy-start | bytes 3145732
  53.9 6.6 %collective-permute-start = (f32[3,1024]{1,0:T(4,128)S(1)}, f32[3,1024]{1,0:T(4,128)S(1)}, u32[]{:S(2)}, u32[]{:S(2)}) collective-permute-start(f32[3,1024]{1,0:T(4,128)S(1)} %pad_maximum_fusion.5), channel_id=1, source_target_pairs={{0,1},{1,2},{2,3},{3,4},{4,5},{5,6},{6,7},{7,8},{8,9},{9,10},{10,1... | collective-permute-start | bytes 36872 | tf_op jit(solution)/shard_map/ppermute | solution.py:226
  110.3 12.5 %copy-start.9 = (f32[4,16,64,128]{3,2,1,0:T(8,128)}, f32[4,16,64,128]{3,2,1,0:T(8,128)S(1)}, u32[]{:S(2)}) copy-start(f32[4,16,64,128]{3,2,1,0:T(8,128)S(1)} %fusion.51) | copy-start | bytes 6291460
  112.5 7.8 %copy-start.11 = (f32[4,16,64,128]{3,2,1,0:T(8,128)}, f32[4,16,64,128]{3,2,1,0:T(8,128)S(1)}, u32[]{:S(2)}) copy-start(f32[4,16,64,128]{3,2,1,0:T(8,128)S(1)} %fusion.54) | copy-start | bytes 6291460
  143.6 11.3 %copy-start.21 = (f32[4,128,128]{1,2,0:T(8,128)}, f32[4,128,128]{1,2,0:T(8,128)S(1)}, u32[]{:S(2)}) copy-start(f32[4,128,128]{1,2,0:T(8,128)S(1)} %fusion.135) | copy-start | bytes 786436
  145.1 20.7 %collective-permute-start.2 = (f32[4,128,256]{1,2,0:T(8,128)}, f32[4,128,256]{1,2,0:T(8,128)}, u32[]{:S(2)}, u32[]{:S(2)}) collective-permute-start(f32[4,128,256]{1,2,0:T(8,128)} %pad_maximum_fusion.3), channel_id=1, source_target_pairs={{0,2},{1,3},{2,4},{3,5},{4,6},{5,7},{6,8},{7,9},{8,10},{9,11},{10,... | collective-permute-start | bytes 1572872 | tf_op jit(solution)/shard_map/ppermute | solution.py:108
  148.5 24.7 %collective-permute-start.3 = (f32[4,128,256]{1,2,0:T(8,128)}, f32[4,128,256]{1,2,0:T(8,128)}, u32[]{:S(2)}, u32[]{:S(2)}) collective-permute-start(f32[4,128,256]{1,2,0:T(8,128)} %pad_maximum_fusion.3), channel_id=1, source_target_pairs={{0,3},{1,4},{2,5},{3,6},{4,7},{5,8},{6,9},{7,10},{8,11},{9,12},{10... | collective-permute-start | bytes 1572872 | tf_op jit(solution)/shard_map/ppermute | solution.py:108
  153.0 23.1 %collective-permute-start.1 = (f32[4,128,256]{1,2,0:T(8,128)}, f32[4,128,256]{1,2,0:T(8,128)}, u32[]{:S(2)}, u32[]{:S(2)}) collective-permute-start(f32[4,128,256]{1,2,0:T(8,128)} %pad_maximum_fusion.3), channel_id=1, source_target_pairs={{0,1},{1,2},{2,3},{3,4},{4,5},{5,6},{6,7},{7,8},{8,9},{9,10},{10,1... | collective-permute-start | bytes 1572872 | tf_op jit(solution)/shard_map/ppermute | solution.py:108
  165.8 13.2 %copy-start.22 = (f32[4,128,128]{1,2,0:T(8,128)S(1)}, f32[4,128,128]{1,2,0:T(8,128)}, u32[]{:S(2)}) copy-start(f32[4,128,128]{1,2,0:T(8,128)} %copy-done.21) | copy-start | bytes 786436
  177.5 7.3 %copy-start.10 = (f32[4,16,64,128]{3,2,1,0:T(8,128)S(1)}, f32[4,16,64,128]{3,2,1,0:T(8,128)}, u32[]{:S(2)}) copy-start(f32[4,16,64,128]{3,2,1,0:T(8,128)} %copy-done.9) | copy-start | bytes 6291460
  179.7 10.6 %copy-start.12 = (f32[4,16,64,128]{3,2,1,0:T(8,128)S(1)}, f32[4,16,64,128]{3,2,1,0:T(8,128)}, u32[]{:S(2)}) copy-start(f32[4,16,64,128]{3,2,1,0:T(8,128)} %copy-done.11) | copy-start | bytes 6291460
  179.7 22.2 %collective-permute-start.5 = (f32[4,128,256]{1,2,0:T(8,128)S(1)}, f32[4,128,256]{1,2,0:T(8,128)S(1)}, u32[]{:S(2)}, u32[]{:S(2)}) collective-permute-start(f32[4,128,256]{1,2,0:T(8,128)S(1)} %pad_maximum_fusion.4), channel_id=1, source_target_pairs={{0,8},{1,9},{2,10},{3,11},{4,12},{5,13},{6,14},{7,15},{16,24},{17,... | collective-permute-start | bytes 1572872 | tf_op jit(solution)/shard_map/ppermute | solution.py:108
  187.1 14.8 %collective-permute-start.6 = (f32[4,128,128]{1,2,0:T(8,128)S(1)}, f32[4,128,128]{1,2,0:T(8,128)S(1)}, u32[]{:S(2)}, u32[]{:S(2)}) collective-permute-start(f32[4,128,128]{1,2,0:T(8,128)S(1)} %get-tuple-element.8), channel_id=1, source_target_pairs={{0,12},{1,13},{2,14},{3,15},{16,28},{17,29},{18,30},{19,31},{32,44... | collective-permute-start | bytes 786440 | tf_op jit(solution)/shard_map/ppermute | solution.py:106
  188.4 17.4 %collective-permute-start.4 = (f32[4,128,256]{1,2,0:T(8,128)S(1)}, f32[4,128,256]{1,2,0:T(8,128)S(1)}, u32[]{:S(2)}, u32[]{:S(2)}) collective-permute-start(f32[4,128,256]{1,2,0:T(8,128)S(1)} %pad_maximum_fusion.4), channel_id=1, source_target_pairs={{0,4},{1,5},{2,6},{3,7},{4,8},{5,9},{6,10},{7,11},{8,12},{9,13},{1... | collective-permute-start | bytes 1572872 | tf_op jit(solution)/shard_map/ppermute | solution.py:108
  190.4 16.2 %copy-start.6 = (f32[4,16,128,128]{3,2,1,0:T(8,128)S(1)}, f32[4,16,128,128]{3,2,1,0:T(8,128)}, u32[]{:S(2)}) copy-start(f32[4,16,128,128]{3,2,1,0:T(8,128)} %copy-done.5) | copy-start | bytes 12582916
  190.4 16.2 %copy-start.8 = (f32[4,16,128,128]{2,3,1,0:T(8,128)S(1)}, f32[4,16,128,128]{2,3,1,0:T(8,128)}, u32[]{:S(2)}) copy-start(f32[4,16,128,128]{2,3,1,0:T(8,128)} %copy-done.7) | copy-start | bytes 12582916
  241.2 44.2 %copy-start.16 = (bf16[1,128,2048]{2,1,0:T(8,128)(2,1)S(1)}, bf16[1,128,2048]{2,1,0:T(8,128)(2,1)}, u32[]{:S(2)}) copy-start(bf16[1,128,2048]{2,1,0:T(8,128)(2,1)} %param.20) | copy-start | bytes 1572868
  241.6 45.2 %copy-start.26 = (f32[2048]{0:T(1024)S(1)}, f32[2048]{0:T(1024)}, u32[]{:S(2)}) copy-start(f32[2048]{0:T(1024)} %param.22) | copy-start | bytes 24580
  295.2 86.4 %all-to-all-start = ((bf16[128,48,512]{2,1,0:T(8,128)(2,1)}), bf16[128,48,512]{2,1,0:T(8,128)(2,1)}, u32[]{:S(2)}, u32[]{:S(2)}) async-start(bf16[128,48,512]{2,1,0:T(8,128)(2,1)} %bitcast.412), calls=%async_computation.1 | async-start | bytes 12582912 | tf_op jit(solution)/shard_map/all_to_all | solution.py:298
  381.6 6.5 %copy-start.34 = (bf16[2,2048,512]{2,1,0:T(8,128)(2,1)S(1)}, bf16[2,2048,512]{2,1,0:T(8,128)(2,1)}, u32[]{:S(2)}) copy-start(bf16[2,2048,512]{2,1,0:T(8,128)(2,1)} %param.38) | copy-start | bytes 12582916
  405.4 5.7 %copy-start.29 = (f32[1,128,10]{1,0,2:T(1,128)S(1)}, f32[1,128,10]{1,0,2:T(1,128)}, u32[]{:S(2)}) copy-start(f32[1,128,10]{1,0,2:T(1,128)} %param.36) | copy-start | bytes 15364
  405.4 81.0 %all-to-all-start.1 = ((bf16[128,48,512]{2,1,0:T(8,128)(2,1)}), bf16[128,48,512]{2,1,0:T(8,128)(2,1)}, u32[]{:S(2)}, u32[]{:S(2)}) async-start(bf16[128,48,512]{2,1,0:T(8,128)(2,1)} %copy.343), calls=%async_computation.2 | async-start | bytes 12582912 | tf_op jit(solution)/shard_map/all_to_all | solution.py:308
  486.4 10.0 %copy-start.17 = (f32[512,6144]{1,0:T(8,128)S(1)}, f32[512,6144]{1,0:T(8,128)}, u32[]{:S(2)}) copy-start(f32[512,6144]{1,0:T(8,128)} %select_reduce_fusion) | copy-start | bytes 37748740
  502.6 12.3 %copy-start.1 = (bf16[512,2048]{1,0:T(8,128)(2,1)S(1)}, bf16[512,2048]{1,0:T(8,128)(2,1)}, u32[]{:S(2)}) copy-start(bf16[512,2048]{1,0:T(8,128)(2,1)} %param.34) | copy-start | bytes 6291460
  (20 other events, 58.8 us)
Sparse Core Ops, SparseCore 0:
  10.2 35.0 all-gather.1
  238.3 47.0 reduce-scatter.1

commit v8 on v5

--- a/solution.py
+++ b/solution.py
@@ -315,7 +315,7 @@
         jnp.where(hits, gates[None, None, :, :], 0.0), axis=-1
     )
     moe_sum = jnp.einsum(
-        "dst,dsx->tx", weight, returned.astype(jnp.float32), precision=HIGHEST
+        "dst,dsx->tx", weight, returned.astype(jnp.float32), precision=lax.Precision.HIGH
     )
     mixed = (residual.astype(jnp.float32) + moe_sum).astype(jnp.bfloat16)
     return mixed.reshape(1, local_rows, model_width)

time: 522 us -> 520 us (level)
  no operation moved by 1% of the time
where the time goes in v8:
time: 520 us; the launch traced here: 511 us
  waiting for transfers between devices  210 us (40%)
  matrix products  144 us (28%)
  local copies, waits for them, and re-layouts  50.3 us (10%)
  other arithmetic  41.8 us (8%)
  starting transfers between devices  37.2 us (7%)
  between operations  15 us (3%)
  blocking collectives  13.3 us (3%)
    dot_general x48, matrix products, mm(): return jnp.matmul(a, b, precision=HIGHEST)  93.1 us
    all_to_all x1, waiting for transfers between devices, local(): lax.all_to_all(answers, ('seq', 'exp'), split_axis=0, concat_axis=0, tile...  73.6 us
    all_to_all x1, waiting for transfers between devices, local(): lax.all_to_all(outgoing.reshape(devices, slot_count * split, piece), ('se...  67.5 us
    reduce_scatter x1, waiting for transfers between devices, local(): lax.psum_scatter(jnp.dot(picked, w_out, preferred_element_type=jnp.float3...  30 us
    all_gather x1, waiting for transfers between devices, local(): lax.all_gather(normed, 'seq', axis=0, tiled=True)  18.8 us
    ppermute x5, starting transfers between devices, segment_entry(): lax.ppermute(jnp.concatenate([inc_map, inc_shift], axis=-1), axis, pairs)  16.8 us
    reduce_or x1, other arithmetic, local(): jnp.any(spread_slots[None, :, :] == (out_rows // split)[:, :, None], axis...  13.9 us
    all_gather x1, blocking collectives, local(): lax.all_gather(rate_logits, 'seq', axis=0, tiled=True)  13.3 us
  transfers between devices with their start and end apart: 11, of which 7 were waited for; matrix products, arithmetic and copies ran while one was open for 10% of the time, Pallas kernels for 0%

profile of v8, /device:TPU:5, one launch (start us, length us, event | category | flops | bytes accessed | tf_op | source)
XLA Modules:
  0.0 511.4 jit_solution(12908975455510165210)
XLA Ops:
  11.5 13.3 %all_gather.7 = bf16[1024,64]{0,1:T(8,128)(2,1)S(1)} all-gather(bf16[128,64]{0,1:T(8,128)(2,1)S(1)} %convolution_convert_fusion.1), channel_id=1, replica_groups=mesh['seq'=8,'exp'=16] {'seq'}, dimensions={0}, use_global_device_ids=true | all-gather | bytes 147456 | tf_op jit(solution)/shard_map/all_gather | solution.py:210
  26.5 18.8 %all-gather.2.cloned.1.call-done = bf16[1024,2048]{1,0:T(8,128)(2,1)} async-done(((bf16[128,2048]{1,0:T(8,128)(2,1)}), bf16[1024,2048]{1,0:T(8,128)(2,1)}) %all-gather.2.cloned.1.call-update) | async-done | bytes 4194320 | tf_op jit(solution)/shard_map/all_gather | solution.py:209
  45.3 5.3 %fusion.153 = f32[1024,512]{1,0:T(8,128)S(1)} fusion(bf16[1024,2048]{1,0:T(8,128)(2,1)} %all-gather.2.cloned.1.call-done, bf16[2048,512]{1,0:T(8,128)(2,1)} %param.25), kind=kOutput, calls=%fused_computation.281 | convolution fusion | flops 2147483648 | bytes 8388608 | tf_op jit(solution)/shard_map/dot_general | solution.py:215
  56.7 3.8 fusion.163
  68.7 3.6 select_negate_fusion
  88.6 3.6 fusion.160
  92.3 3.7 fusion.159
  104.1 4.0 convolution_add_fusion
  112.6 7.8 %fusion.48 = f32[4,16,128,128]{2,3,1,0:T(8,128)S(1)} fusion(f32[4,16,64,128]{3,2,1,0:T(8,128)S(1)} %fusion.45, f32[4,16,64,128]{3,2,1,0:T(8,128)S(1)} %bitcast.412, f32[4,16,64]{2,1,0:T(8,128)S(1)} %get-tuple-element.13), kind=kOutput, calls=%fused_computation.62 | convolution fusion | flops 805830656 | bytes 8404992 | tf_op jit(solution)/shard_map/dot_general | solution.py:37
  123.0 7.8 %multiply_subtract_fusion = f32[4,16,128,128]{3,2,1,0:T(8,128)S(1)} fusion(f32[4,16,64,128]{3,2,1,0:T(8,128)S(1)} %fusion.42, f32[128,128]{1,0:T(8,128)S(1)} %fusion.126, f32[4,16]{1,0:T(4,128)S(1)} %exp.61, f32[4,16,64,128]{3,2,1,0:T(8,128)S(1)} %bitcast.413, f32[4,16,64]{2,1,0:T(8,128)S(1)} %get-tuple-element.13), kind=kOutput, calls=%fused_computation.12 | convolution fusion | flops 807927808 | bytes 8470784 | tf_op jit(solution)/shard_map/dot_general | solution.py:37
  134.4 4.5 copy_add_fusion
  148.6 4.5 collective-permute-start.3
  162.4 3.5 fusion.47
  165.9 7.4 %collective-permute-done.3 = f32[4,128,256]{1,2,0:T(8,128)} collective-permute-done((f32[4,128,256]{1,2,0:T(8,128)}, f32[4,128,256]{1,2,0:T(8,128)}, u32[]{:S(2)}, u32[]{:S(2)}) %collective-permute-start.3) | collective-permute-done | bytes 524320 | tf_op jit(solution)/shard_map/ppermute | solution.py:108
  179.9 4.9 collective-permute-start.5
  192.8 9.2 %collective-permute-done.6 = f32[4,128,128]{1,2,0:T(8,128)S(1)} collective-permute-done((f32[4,128,128]{1,2,0:T(8,128)S(1)}, f32[4,128,128]{1,2,0:T(8,128)S(1)}, u32[]{:S(2)}, u32[]{:S(2)}) %collective-permute-start.6) | collective-permute-done | bytes 262176 | tf_op jit(solution)/shard_map/ppermute | solution.py:106
  216.6 9.8 %fusion.57 = f32[4,16,64,128]{3,2,1,0:T(8,128)} fusion(f32[4,16,64,128]{3,2,1,0:T(8,128)S(1)} %fusion.161, f32[4,16,128,128]{2,3,0,1:T(8,128)S(1)} %fusion.70, f32[4,16,64,128]{3,2,1,0:T(8,128)S(1)} %fusion.162, f32[4,16,64,128]{3,2,1,0:T(8,128)S(1)} %bitcast.417, f32[4,16,64]{2,1,0:T(8,128)S(1)} %get-tuple-element.11), kind=kOutput, calls=%fused_computation.72 | convolution fusion | flops 806879232 | bytes 12599296 | tf_op jit(solution)/shard_map/dot_general | solution.py:37
  233.9 4.4 convolution_convert_fusion
  241.7 13.9 %compare_reduce_fusion = pred[6144,512]{1,0:T(8,128)(4,1)} fusion(s32[512,10]{0,1:T(8,128)S(1)} %copy.433, s32[6144]{0:T(1024)S(1)} %add_select_fusion), kind=kLoop, calls=%fused_computation | loop fusion | flops 59768832 | bytes 3190784 | tf_op jit(solution)/shard_map/reduce_or | solution.py:292
  255.6 30.0 %reduce-scatter.2.cloned.1.call-done = bf16[128,2048]{1,0:T(8,128)(2,1)} async-done(((bf16[1024,2048]{1,0:T(8,128)(2,1)}), bf16[128,2048]{1,0:T(8,128)(2,1)}) %reduce-scatter.2.cloned.1.call-update) | async-done | bytes 524304 | tf_op jit(solution)/shard_map/reduce_scatter | solution.py:264
  288.5 6.8 %fusion.3 = bf16[6144,512]{1,0:T(8,128)(2,1)} fusion(bf16[512,512]{1,0:T(8,128)(2,1)S(1)} %reshape.272, pred[6144,512]{1,0:T(8,128)(4,1)} %compare_reduce_fusion, s32[512]{0:T(512)S(1)} %add_select_fusion.1, s32[6144]{0:T(1024)S(1)} %fusion.127), kind=kOutput, calls=%fused_computation.4 | convolution fusion | flops 3230662656 | bytes 9988096 | tf_op jit(solution)/shard_map/dot_general | solution.py:295
  295.4 11.0 %all-to-all-start = ((bf16[128,48,512]{2,1,0:T(8,128)(2,1)}), bf16[128,48,512]{2,1,0:T(8,128)(2,1)}, u32[]{:S(2)}, u32[]{:S(2)}) async-start(bf16[128,48,512]{2,1,0:T(8,128)(2,1)} %bitcast.421), calls=%async_computation.1 | async-start | bytes 12582912 | tf_op jit(solution)/shard_map/all_to_all | solution.py:300
  306.4 7.8 %reshape.277 = bf16[2,512,4,512]{3,2,1,0:T(4,128)(2,1)} reshape(bf16[2,512,2048]{2,1,0:T(8,128)(2,1)} %param.39) | data formatting | bytes 8388608 | tf_op jit(solution)/shard_map/reshape | solution.py:173
  314.2 67.5 %all-to-all-done = bf16[128,48,512]{2,1,0:T(8,128)(2,1)} async-done(((bf16[128,48,512]{2,1,0:T(8,128)(2,1)}), bf16[128,48,512]{2,1,0:T(8,128)(2,1)}, u32[]{:S(2)}, u32[]{:S(2)}) %all-to-all-start) | async-done | bytes 6291488 | tf_op jit(solution)/shard_map/all_to_all | solution.py:300
  381.7 6.5 %copy.434 = bf16[128,48,512]{2,0,1:T(8,128)(2,1)S(1)} copy(bf16[128,48,512]{2,1,0:T(8,128)(2,1)} %all-to-all-done) | data formatting | bytes 12582912 | tf_op jit(solution)/shard_map/all_to_all | solution.py:300
  391.6 3.8 fusion.15
  395.4 4.0 fusion.12
  399.4 6.3 %copy.436 = bf16[128,48,512]{2,1,0:T(8,128)(2,1)} copy(bf16[128,48,512]{2,0,1:T(8,128)(2,1)S(1)} %bitcast.424) | data formatting | bytes 12582912 | tf_op jit(solution)/shard_map/reshape | solution.py:176
  405.7 5.3 %all-to-all-start.1 = ((bf16[128,48,512]{2,1,0:T(8,128)(2,1)}), bf16[128,48,512]{2,1,0:T(8,128)(2,1)}, u32[]{:S(2)}, u32[]{:S(2)}) async-start(bf16[128,48,512]{2,1,0:T(8,128)(2,1)} %copy.436), calls=%async_computation.2 | async-start | bytes 12582912 | tf_op jit(solution)/shard_map/all_to_all | solution.py:310
  413.0 73.6 %all-to-all-done.1 = bf16[128,48,512]{2,1,0:T(8,128)(2,1)} async-done(((bf16[128,48,512]{2,1,0:T(8,128)(2,1)}), bf16[128,48,512]{2,1,0:T(8,128)(2,1)}, u32[]{:S(2)}, u32[]{:S(2)}) %all-to-all-start.1) | async-done | bytes 6291488 | tf_op jit(solution)/shard_map/all_to_all | solution.py:310
  486.6 9.3 %copy.437 = bf16[128,48,512]{0,2,1:T(8,128)(2,1)} copy(bf16[128,48,512]{2,1,0:T(8,128)(2,1)} %all-to-all-done.1) | data formatting | bytes 12582912 | tf_op jit(solution)/shard_map/all_to_all | solution.py:310
  495.9 8.3 %fusion.21 = bf16[1,128,2048]{2,1,0:T(8,128)(2,1)} fusion(f32[128,12,128]{2,0,1:T(8,128)} %select_reduce_fusion, bf16[128,12,2048]{0,2,1:T(8,128)(2,1)} %bitcast.415, bf16[128,2048]{1,0:T(8,128)(2,1)S(1)} %copy-done.18, bf16[1,128,2048]{2,1,0:T(8,128)(2,1)S(1)} %copy-done.16), kind=kOutput, calls=%fused_computation.27 | convolution fusion | flops 2417754112 | bytes 8650752 | tf_op jit(solution)/shard_map/dst,dsx->tx/dot_general | solution.py:317
  (213 shorter events, 122.2 us)
Async XLA Ops:
  6.5 227.3 %copy-start = (bf16[512,2048]{1,0:T(8,128)(2,1)S(1)}, bf16[512,2048]{1,0:T(8,128)(2,1)}, u32[]{:S(2)}) copy-start(bf16[512,2048]{1,0:T(8,128)(2,1)} %param.34) | copy-start | bytes 6291460
  6.5 18.3 %copy-start.39 = (f32[4]{0:T(128)S(1)}, f32[4]{0:T(128)}, u32[]{:S(2)}) copy-start(f32[4]{0:T(128)} %param.31) | copy-start | bytes 52
  6.5 18.3 %copy-start.31 = (f32[4]{0:T(128)S(1)}, f32[4]{0:T(128)}, u32[]{:S(2)}) copy-start(f32[4]{0:T(128)} %param.32) | copy-start | bytes 52
  6.5 19.7 %copy-start.29 = (f32[4,256]{1,0:T(4,128)S(1)}, f32[4,256]{1,0:T(4,128)}, u32[]{:S(2)}) copy-start(f32[4,256]{1,0:T(4,128)} %param.28) | copy-start | bytes 12292
  6.5 19.7 %copy-start.30 = (f32[4,256]{1,0:T(4,128)S(1)}, f32[4,256]{1,0:T(4,128)}, u32[]{:S(2)}) copy-start(f32[4,256]{1,0:T(4,128)} %param.29) | copy-start | bytes 12292
  6.6 19.7 %copy-start.26 = (f32[4,512]{1,0:T(4,128)S(1)}, f32[4,512]{1,0:T(4,128)}, u32[]{:S(2)}) copy-start(f32[4,512]{1,0:T(4,128)} %param.30) | copy-start | bytes 24580
  6.6 38.7 %all-gather.2.cloned.1.call-start = ((), (), s32[]{:S(2)}) async-start(), calls=%async_computation.3 | async-start | bytes 4718592 | tf_op jit(solution)/shard_map/all_gather | solution.py:209
  10.1 275.6 %reduce-scatter.2.cloned.1.call-start = ((), (), s32[]{:S(2)}) async-start(), calls=%async_computation.4 | async-start | bytes 4718592 | tf_op jit(solution)/shard_map/reduce_scatter | solution.py:264
  45.3 5.4 %copy-start.37 = (bf16[2048,256]{1,0:T(8,128)(2,1)S(1)}, bf16[2048,256]{1,0:T(8,128)(2,1)}, u32[]{:S(2)}) copy-start(bf16[2048,256]{1,0:T(8,128)(2,1)} %param.23) | copy-start | bytes 3145732
  53.9 6.6 %collective-permute-start = (f32[3,1024]{1,0:T(4,128)S(1)}, f32[3,1024]{1,0:T(4,128)S(1)}, u32[]{:S(2)}, u32[]{:S(2)}) collective-permute-start(f32[3,1024]{1,0:T(4,128)S(1)} %pad_maximum_fusion.5), channel_id=1, source_target_pairs={{0,1},{1,2},{2,3},{3,4},{4,5},{5,6},{6,7},{7,8},{8,9},{9,10},{10,1... | collective-permute-start | bytes 36872 | tf_op jit(solution)/shard_map/ppermute | solution.py:226
  110.4 12.6 %copy-start.9 = (f32[4,16,64,128]{3,2,1,0:T(8,128)}, f32[4,16,64,128]{3,2,1,0:T(8,128)S(1)}, u32[]{:S(2)}) copy-start(f32[4,16,64,128]{3,2,1,0:T(8,128)S(1)} %fusion.42) | copy-start | bytes 6291460
  112.6 7.8 %copy-start.11 = (f32[4,16,64,128]{3,2,1,0:T(8,128)}, f32[4,16,64,128]{3,2,1,0:T(8,128)S(1)}, u32[]{:S(2)}) copy-start(f32[4,16,64,128]{3,2,1,0:T(8,128)S(1)} %fusion.45) | copy-start | bytes 6291460
  143.7 11.3 %copy-start.20 = (f32[4,128,128]{1,2,0:T(8,128)}, f32[4,128,128]{1,2,0:T(8,128)S(1)}, u32[]{:S(2)}) copy-start(f32[4,128,128]{1,2,0:T(8,128)S(1)} %fusion.120) | copy-start | bytes 786436
  145.2 20.7 %collective-permute-start.2 = (f32[4,128,256]{1,2,0:T(8,128)}, f32[4,128,256]{1,2,0:T(8,128)}, u32[]{:S(2)}, u32[]{:S(2)}) collective-permute-start(f32[4,128,256]{1,2,0:T(8,128)} %pad_maximum_fusion.3), channel_id=1, source_target_pairs={{0,2},{1,3},{2,4},{3,5},{4,6},{5,7},{6,8},{7,9},{8,10},{9,11},{10,... | collective-permute-start | bytes 1572872 | tf_op jit(solution)/shard_map/ppermute | solution.py:108
  148.6 24.7 %collective-permute-start.3 = (f32[4,128,256]{1,2,0:T(8,128)}, f32[4,128,256]{1,2,0:T(8,128)}, u32[]{:S(2)}, u32[]{:S(2)}) collective-permute-start(f32[4,128,256]{1,2,0:T(8,128)} %pad_maximum_fusion.3), channel_id=1, source_target_pairs={{0,3},{1,4},{2,5},{3,6},{4,7},{5,8},{6,9},{7,10},{8,11},{9,12},{10... | collective-permute-start | bytes 1572872 | tf_op jit(solution)/shard_map/ppermute | solution.py:108
  153.1 23.1 %collective-permute-start.1 = (f32[4,128,256]{1,2,0:T(8,128)}, f32[4,128,256]{1,2,0:T(8,128)}, u32[]{:S(2)}, u32[]{:S(2)}) collective-permute-start(f32[4,128,256]{1,2,0:T(8,128)} %pad_maximum_fusion.3), channel_id=1, source_target_pairs={{0,1},{1,2},{2,3},{3,4},{4,5},{5,6},{6,7},{7,8},{8,9},{9,10},{10,1... | collective-permute-start | bytes 1572872 | tf_op jit(solution)/shard_map/ppermute | solution.py:108
  165.9 13.2 %copy-start.21 = (f32[4,128,128]{1,2,0:T(8,128)S(1)}, f32[4,128,128]{1,2,0:T(8,128)}, u32[]{:S(2)}) copy-start(f32[4,128,128]{1,2,0:T(8,128)} %copy-done.20) | copy-start | bytes 786436
  177.6 7.2 %copy-start.10 = (f32[4,16,64,128]{3,2,1,0:T(8,128)S(1)}, f32[4,16,64,128]{3,2,1,0:T(8,128)}, u32[]{:S(2)}) copy-start(f32[4,16,64,128]{3,2,1,0:T(8,128)} %copy-done.9) | copy-start | bytes 6291460
  179.9 10.6 %copy-start.12 = (f32[4,16,64,128]{3,2,1,0:T(8,128)S(1)}, f32[4,16,64,128]{3,2,1,0:T(8,128)}, u32[]{:S(2)}) copy-start(f32[4,16,64,128]{3,2,1,0:T(8,128)} %copy-done.11) | copy-start | bytes 6291460
  179.9 22.2 %collective-permute-start.5 = (f32[4,128,256]{1,2,0:T(8,128)S(1)}, f32[4,128,256]{1,2,0:T(8,128)S(1)}, u32[]{:S(2)}, u32[]{:S(2)}) collective-permute-start(f32[4,128,256]{1,2,0:T(8,128)S(1)} %pad_maximum_fusion.4), channel_id=1, source_target_pairs={{0,8},{1,9},{2,10},{3,11},{4,12},{5,13},{6,14},{7,15},{16,24},{17,... | collective-permute-start | bytes 1572872 | tf_op jit(solution)/shard_map/ppermute | solution.py:108
  187.2 14.9 %collective-permute-start.6 = (f32[4,128,128]{1,2,0:T(8,128)S(1)}, f32[4,128,128]{1,2,0:T(8,128)S(1)}, u32[]{:S(2)}, u32[]{:S(2)}) collective-permute-start(f32[4,128,128]{1,2,0:T(8,128)S(1)} %get-tuple-element.8), channel_id=1, source_target_pairs={{0,12},{1,13},{2,14},{3,15},{16,28},{17,29},{18,30},{19,31},{32,44... | collective-permute-start | bytes 786440 | tf_op jit(solution)/shard_map/ppermute | solution.py:106
  188.5 17.4 %collective-permute-start.4 = (f32[4,128,256]{1,2,0:T(8,128)S(1)}, f32[4,128,256]{1,2,0:T(8,128)S(1)}, u32[]{:S(2)}, u32[]{:S(2)}) collective-permute-start(f32[4,128,256]{1,2,0:T(8,128)S(1)} %pad_maximum_fusion.4), channel_id=1, source_target_pairs={{0,4},{1,5},{2,6},{3,7},{4,8},{5,9},{6,10},{7,11},{8,12},{9,13},{1... | collective-permute-start | bytes 1572872 | tf_op jit(solution)/shard_map/ppermute | solution.py:108
  190.5 16.1 %copy-start.6 = (f32[4,16,128,128]{3,2,1,0:T(8,128)S(1)}, f32[4,16,128,128]{3,2,1,0:T(8,128)}, u32[]{:S(2)}) copy-start(f32[4,16,128,128]{3,2,1,0:T(8,128)} %copy-done.5) | copy-start | bytes 12582916
  190.5 16.1 %copy-start.8 = (f32[4,16,128,128]{2,3,1,0:T(8,128)S(1)}, f32[4,16,128,128]{2,3,1,0:T(8,128)}, u32[]{:S(2)}) copy-start(f32[4,16,128,128]{2,3,1,0:T(8,128)} %copy-done.7) | copy-start | bytes 12582916
  241.3 44.3 %copy-start.16 = (bf16[1,128,2048]{2,1,0:T(8,128)(2,1)S(1)}, bf16[1,128,2048]{2,1,0:T(8,128)(2,1)}, u32[]{:S(2)}) copy-start(bf16[1,128,2048]{2,1,0:T(8,128)(2,1)} %param.20) | copy-start | bytes 1572868
  241.6 45.3 %copy-start.25 = (f32[2048]{0:T(1024)S(1)}, f32[2048]{0:T(1024)}, u32[]{:S(2)}) copy-start(f32[2048]{0:T(1024)} %param.22) | copy-start | bytes 24580
  295.4 86.3 %all-to-all-start = ((bf16[128,48,512]{2,1,0:T(8,128)(2,1)}), bf16[128,48,512]{2,1,0:T(8,128)(2,1)}, u32[]{:S(2)}, u32[]{:S(2)}) async-start(bf16[128,48,512]{2,1,0:T(8,128)(2,1)} %bitcast.421), calls=%async_computation.1 | async-start | bytes 12582912 | tf_op jit(solution)/shard_map/all_to_all | solution.py:300
  381.7 6.5 %copy-start.33 = (bf16[2,2048,512]{2,1,0:T(8,128)(2,1)S(1)}, bf16[2,2048,512]{2,1,0:T(8,128)(2,1)}, u32[]{:S(2)}) copy-start(bf16[2,2048,512]{2,1,0:T(8,128)(2,1)} %param.38) | copy-start | bytes 12582916
  405.7 5.4 %copy-start.28 = (f32[1,128,10]{1,0,2:T(1,128)S(1)}, f32[1,128,10]{1,0,2:T(1,128)}, u32[]{:S(2)}) copy-start(f32[1,128,10]{1,0,2:T(1,128)} %param.36) | copy-start | bytes 15364
  405.7 80.9 %all-to-all-start.1 = ((bf16[128,48,512]{2,1,0:T(8,128)(2,1)}), bf16[128,48,512]{2,1,0:T(8,128)(2,1)}, u32[]{:S(2)}, u32[]{:S(2)}) async-start(bf16[128,48,512]{2,1,0:T(8,128)(2,1)} %copy.436), calls=%async_computation.2 | async-start | bytes 12582912 | tf_op jit(solution)/shard_map/all_to_all | solution.py:310
  413.0 82.9 %copy-start.18 = (bf16[128,2048]{1,0:T(8,128)(2,1)S(1)}, bf16[128,2048]{1,0:T(8,128)(2,1)}, u32[]{:S(2)}) copy-start(bf16[128,2048]{1,0:T(8,128)(2,1)} %reduce-scatter.2.cloned.1.call-done) | copy-start | bytes 1572868
  495.9 8.3 %copy-start.1 = (bf16[512,2048]{1,0:T(8,128)(2,1)S(1)}, bf16[512,2048]{1,0:T(8,128)(2,1)}, u32[]{:S(2)}) copy-start(bf16[512,2048]{1,0:T(8,128)(2,1)} %param.34) | copy-start | bytes 6291460
  (19 other events, 56.0 us)
Sparse Core Ops, SparseCore 0:
  10.2 35.0 all-gather.1
  238.4 47.1 reduce-scatter.1
